TPU v7x, 256 devices: a whole 4x4x8 slice. The times are simulated.
256 devices in a mesh: seq: 32 (over z, y), head: 8 (over x, core).
Axes of the slice: x: 4, y: 4, z: 8, core: 2. Of those that a mesh axis runs over, the one named last changes fastest.
Arguments:
- queries: bfloat16 [8192, 4096], P('seq', 'head'), may hold values from -32 to 32
- key_rows: bfloat16 [8192, 4096], P('seq', 'head'), may hold values from -6 to 6
- value_rows: bfloat16 [8192, 4096], P('seq', 'head'), may hold values from -6 to 6
- out_weight: bfloat16 [4096, 4096], P('head', 'seq'), may hold values from -0.1875 to 0.1875
- grad_output: bfloat16 [8192, 4096], P('seq', 'head'), may hold values from -6 to 6
- cluster_ids: int32 [8192], P('seq'), may hold values from 0 to 31, as said below
- block_pattern: int32 [32, 2, 2], replicated, may hold values from 0 to 1, as said below
Outputs:
- layer_out: bfloat16 [8192, 4096], P('seq', 'head')
- grad_queries: bfloat16 [8192, 4096], P('seq', 'head')
- grad_keys: bfloat16 [8192, 4096], P('seq', 'head')
- grad_values: bfloat16 [8192, 4096], P('seq', 'head')
Inputs may be any that keep to these rules, and one draw needn't show every extreme that they name: `cluster_ids`: every cluster holds exactly 256 tokens. The 256 tokens of one index of seq name one cluster at most 16 times, and each such index names some cluster exactly 16 times. block_pattern[c, b, b] = 1 and block_pattern[c, b, b2] = 0 for b2 > b.
All inputs are finite; a program needn't handle non-finite values.
Results may differ from a plain program's by a relative error of at most 0.03.
Values may be sent and summed in bfloat16 or wider, within the bound.
No kernel may reach another device: no remote copies, remote signals or barrier semaphores. Data moves between devices by JAX's collectives and lax.ppermute only.
A program may use at most 64 MiB of HBM per device.

v0:
```python
import math

import jax
import jax.numpy as jnp
from jax import lax
from jax.sharding import PartitionSpec as P

HD = 128
BLK = 128


def probabilities(query_part, key_part, allowed, score_scale):
    scores = (
        jnp.einsum("qd,kd->qk", query_part, key_part, preferred_element_type=jnp.float32)
        * score_scale
    )
    scores = jnp.where(allowed, scores, -jnp.inf)
    shifted = jnp.exp(scores - jnp.max(scores, axis=1, keepdims=True))
    return shifted / jnp.sum(shifted, axis=1, keepdims=True)


def attend(query_side, key_side, value_side, allowed, head_count, score_scale):
    results = []
    for which_head in range(head_count):
        lower = which_head * HD
        probs = probabilities(
            query_side[:, lower : lower + HD], key_side[:, lower : lower + HD], allowed, score_scale
        )
        mixed = jnp.dot(
            probs.astype(jnp.bfloat16),
            value_side[:, lower : lower + HD],
            preferred_element_type=jnp.float32,
        )
        results.append(mixed.astype(jnp.bfloat16))
    return jnp.concatenate(results, axis=1)


def attend_back(
    query_side, key_side, value_side, allowed, attn_side, grad_side, head_count, score_scale
):
    grad_q, grad_k, grad_v = ([], [], [])
    for which_head in range(head_count):
        lower = which_head * HD
        query_head = query_side[:, lower : lower + HD]
        key_head = key_side[:, lower : lower + HD]
        value_head = value_side[:, lower : lower + HD]
        grad_head = grad_side[:, lower : lower + HD]
        attn_head = attn_side[:, lower : lower + HD]
        probs = probabilities(query_head, key_head, allowed, score_scale)
        probs_low = probs.astype(jnp.bfloat16)
        delta = jnp.sum(
            grad_head.astype(jnp.float32) * attn_head.astype(jnp.float32), axis=1, keepdims=True
        )
        dprobs = jnp.einsum("qd,kd->qk", grad_head, value_head, preferred_element_type=jnp.float32)
        dscores = (probs * (dprobs - delta)).astype(jnp.bfloat16)
        grad_q.append(
            (jnp.dot(dscores, key_head, preferred_element_type=jnp.float32) * score_scale).astype(
                jnp.bfloat16
            )
        )
        grad_k.append(
            (
                jnp.einsum("qk,qd->kd", dscores, query_head, preferred_element_type=jnp.float32)
                * score_scale
            ).astype(jnp.bfloat16)
        )
        grad_v.append(
            jnp.einsum(
                "qk,qd->kd", probs_low, grad_head, preferred_element_type=jnp.float32
            ).astype(jnp.bfloat16)
        )
    return (
        jnp.concatenate(grad_q, axis=1),
        jnp.concatenate(grad_k, axis=1),
        jnp.concatenate(grad_v, axis=1),
    )


def on_device(queries, key_rows, value_rows, out_weight, grad_output, cluster_ids, block_pattern):
    tokens = queries.shape[0]
    width = queries.shape[1]
    head_count = width // HD
    groups = lax.axis_size("seq")
    slot_rows = 2 * tokens // groups
    slot_total = groups * slot_rows
    blocks = block_pattern.shape[1]
    owner_index = lax.axis_index("seq")
    score_scale = 1.0 / math.sqrt(HD)
    members = (cluster_ids[:, None] == jnp.arange(groups, dtype=jnp.int32)[None, :]).astype(
        jnp.int32
    )
    earlier = jnp.cumsum(members, axis=0) - members
    local_rank = jnp.sum(earlier * members, axis=1)
    send_counts = jnp.sum(members, axis=0)
    slot_index = cluster_ids * slot_rows + local_rank

    def to_slots(row_data):
        return (
            jnp.zeros((slot_total, row_data.shape[1]), row_data.dtype).at[slot_index].set(row_data)
        )

    def from_slots(buffer):
        return jnp.take(buffer, slot_index, axis=0)

    full_weight = lax.all_gather(out_weight, "seq", axis=1, tiled=True)
    query_in, key_in, value_in, got_counts = (
        lax.all_to_all(to_slots(queries), "seq", split_axis=0, concat_axis=0, tiled=True),
        lax.all_to_all(to_slots(key_rows), "seq", split_axis=0, concat_axis=0, tiled=True),
        lax.all_to_all(to_slots(value_rows), "seq", split_axis=0, concat_axis=0, tiled=True),
        lax.all_to_all(send_counts, "seq", split_axis=0, concat_axis=0, tiled=True),
    )
    offsets = jnp.cumsum(got_counts) - got_counts
    pattern = lax.dynamic_index_in_dim(block_pattern, owner_index, 0, keepdims=False).astype(
        jnp.float32
    )
    slot_source = jnp.arange(slot_total, dtype=jnp.int32) // slot_rows
    slot_place = jnp.arange(slot_total, dtype=jnp.int32) % slot_rows
    row_live = slot_place < jnp.take(got_counts, slot_source)
    rank_rows = jnp.take(offsets, slot_source) + slot_place
    query_side, key_side, value_side = (query_in, key_in, value_in)
    onehot = (rank_rows[:, None] // BLK == jnp.arange(blocks, dtype=jnp.int32)[None, :]).astype(
        jnp.float32
    )
    block_ok = jnp.dot(jnp.dot(onehot, pattern), onehot.T) > 0.5
    usable = (
        block_ok
        & (rank_rows[None, :] <= rank_rows[:, None])
        & row_live[None, :]
        & row_live[:, None]
    )
    diagonal = jnp.eye(rank_rows.shape[0], dtype=bool)
    allowed = usable | diagonal & ~row_live[:, None]
    attn_side = attend(query_side, key_side, value_side, allowed, head_count, score_scale)
    attn_local = from_slots(
        lax.all_to_all(attn_side, "seq", split_axis=0, concat_axis=0, tiled=True)
    )
    partial_value = jnp.dot(attn_local, full_weight, preferred_element_type=jnp.float32)
    rounded_part = lax.optimization_barrier(partial_value.astype(jnp.bfloat16)).astype(jnp.float32)
    layer_out = lax.psum_scatter(
        rounded_part.astype(jnp.bfloat16), "head", scatter_dimension=1, tiled=True
    )
    grad_sum = jnp.einsum(
        "td,wd->tw",
        lax.all_gather(grad_output, "head", axis=1, tiled=True),
        full_weight,
        preferred_element_type=jnp.float32,
    )
    grad_attention = grad_sum.astype(jnp.bfloat16)
    grad_in = lax.all_to_all(
        to_slots(grad_attention), "seq", split_axis=0, concat_axis=0, tiled=True
    )
    grad_q, grad_k, grad_v = attend_back(
        query_side, key_side, value_side, allowed, attn_side, grad_in, head_count, score_scale
    )
    back_q, back_k, back_v = (
        lax.all_to_all(grad_q, "seq", split_axis=0, concat_axis=0, tiled=True),
        lax.all_to_all(grad_k, "seq", split_axis=0, concat_axis=0, tiled=True),
        lax.all_to_all(grad_v, "seq", split_axis=0, concat_axis=0, tiled=True),
    )
    return (layer_out, from_slots(back_q), from_slots(back_k), from_slots(back_v))


def solution(mesh):
    in_specs = (
        P("seq", "head"),
        P("seq", "head"),
        P("seq", "head"),
        P("head", "seq"),
        P("seq", "head"),
        P("seq"),
        P(),
    )
    out_specs = (P("seq", "head"), P("seq", "head"), P("seq", "head"), P("seq", "head"))
    return jax.shard_map(
        on_device, mesh=mesh, in_specs=in_specs, out_specs=out_specs, check_vma=False
    )
```

profile of v0, /device:TPU:4, one launch (start us, length us, event | category | flops | bytes accessed | tf_op | source)
XLA Modules:
  0.0 280.2 jit_solution(10742743238701622217)
XLA Ops:
  10.1 0.9 fusion.77
  11.7 11.5 %all-to-all-start = ((s32[32,1,1]{2,1,0:T(1,128)}), s32[32,1,1]{2,1,0:T(1,128)S(1)}, u32[]{:S(2)}, u32[]{:S(2)}) async-start(s32[32,1,1]{2,1,0:T(1,128)} %copy.50), calls=%async_computation | async-start | bytes 32768 | tf_op jit(solution)/shard_map/all_to_all | solution.py:110
  23.2 1.2 compare_and_fusion
  24.4 2.8 scatter_custom_fusion
  27.2 5.7 %all-to-all-done = s32[32,1,1]{2,1,0:T(1,128)S(1)} async-done(((s32[32,1,1]{2,1,0:T(1,128)}), s32[32,1,1]{2,1,0:T(1,128)S(1)}, u32[]{:S(2)}, u32[]{:S(2)}) %all-to-all-start) | async-done | bytes 160 | tf_op jit(solution)/shard_map/all_to_all | solution.py:110
  32.9 4.0 %all-to-all-start.1 = ((bf16[32,16,512]{2,1,0:T(8,128)(2,1)}), bf16[32,16,512]{2,1,0:T(8,128)(2,1)S(1)}, u32[]{:S(2)}, u32[]{:S(2)}) async-start(bf16[32,16,512]{2,1,0:T(8,128)(2,1)} %bitcast.68), calls=%async_computation.1 | async-start | bytes 1048576 | tf_op jit(solution)/shard_map/all_to_all | solution.py:107
  37.0 2.7 scatter_custom_fusion.1
  39.7 2.7 scatter_custom_fusion.2
  42.4 0.8 convert_reduce_fusion.1
  43.2 10.9 %all-to-all-done.1 = bf16[32,16,512]{2,1,0:T(8,128)(2,1)S(1)} async-done(((bf16[32,16,512]{2,1,0:T(8,128)(2,1)}), bf16[32,16,512]{2,1,0:T(8,128)(2,1)S(1)}, u32[]{:S(2)}, u32[]{:S(2)}) %all-to-all-start.1) | async-done | bytes 524320 | tf_op jit(solution)/shard_map/all_to_all | solution.py:107
  54.2 4.6 %all-to-all-start.2 = ((bf16[32,16,512]{2,1,0:T(8,128)(2,1)}), bf16[32,16,512]{2,1,0:T(8,128)(2,1)S(1)}, u32[]{:S(2)}, u32[]{:S(2)}) async-start(bf16[32,16,512]{2,1,0:T(8,128)(2,1)} %bitcast.70), calls=%async_computation.2 | async-start | bytes 1048576 | tf_op jit(solution)/shard_map/all_to_all | solution.py:108
  61.7 19.9 %fusion.97 = (pred[512]{0:T(512)(128)(4,1)S(1)}, pred[512]{0:T(512)(128)(4,1)S(1)}) fusion(s32[]{:T(128)} %bitcast.67, s32[]{:T(128)} %bitcast.66, s32[]{:T(128)} %bitcast.65, s32[]{:T(128)} %bitcast.64, s32[]{:T(128)} %bitcast.63, s32[]{:T(128)} %bitcast.62, s32[]{:T(128)} %bitcast.61, s32[]{:T(128)} %bitcast.60, s32[]{:T(128)} %bitcast.59, s32[]{:T(128)} %bitcast.58, ...), kind=kLoop, calls=%fused_computation.202 | loop fusion | flops 42496 | bytes 1152 | tf_op jit(solution)/shard_map/not | solution.py:132
  83.1 19.9 %add_select_fusion = (s32[512]{0:T(512)S(1)}, s32[512]{0:T(512)S(1)}) fusion(s32[]{:T(128)} %bitcast.35, s32[]{:T(128)} %bitcast.34, s32[]{:T(128)} %bitcast.33, s32[]{:T(128)} %bitcast.32, s32[]{:T(128)} %bitcast.31, s32[]{:T(128)} %bitcast.30, s32[]{:T(128)} %bitcast.29, s32[]{:T(128)} %bitcast.28, s32[]{:T(128)} %bitcast.27, s32[]{:T(128)} %bitcast.26, ...), kind=kLoop, calls=%fused_computation.146 | loop fusion | flops 49664 | bytes 4224 | tf_op jit(solution)/shard_map/jit(floor_divide)/jit(_where)/select_n | solution.py:121
  104.8 1.7 fusion.105
  106.5 22.8 %all-gather.3.cloned.1.call-done = bf16[512,4096]{1,0:T(8,128)(2,1)} async-done(((bf16[512,128]{1,0:T(8,128)(2,1)}), bf16[512,4096]{1,0:T(8,128)(2,1)}) %all-gather.3.cloned.1.call-update) | async-done | bytes 4194320 | tf_op jit(solution)/shard_map/all_gather | solution.py:105
  129.3 4.8 %convolution_convert_fusion.1 = bf16[256,512]{1,0:T(8,128)(2,1)} fusion(bf16[256,4096]{1,0:T(8,128)(2,1)} %all-gather.5.cloned.1.call-done, bf16[512,4096]{1,0:T(8,128)(2,1)} %all-gather.3.cloned.1.call-done), kind=kOutput, calls=%fused_computation.30 | convolution fusion | flops 1073872896 | bytes 6553600 | tf_op jit(solution)/shard_map/td,wd->tw/dot_general | solution.py:142
  134.1 2.8 scatter_custom_fusion.3
  136.9 9.5 %all-to-all-start.5 = ((bf16[32,16,512]{2,1,0:T(8,128)(2,1)}), bf16[32,16,512]{2,1,0:T(8,128)(2,1)}, u32[]{:S(2)}, u32[]{:S(2)}) async-start(bf16[32,16,512]{2,1,0:T(8,128)(2,1)} %bitcast.141), calls=%async_computation.6 | async-start | bytes 1048576 | tf_op jit(solution)/shard_map/all_to_all | solution.py:149
  147.0 1.3 fusion.106
  148.5 0.9 fusion.35
  149.4 10.7 %all-to-all-done.5 = bf16[32,16,512]{2,1,0:T(8,128)(2,1)} async-done(((bf16[32,16,512]{2,1,0:T(8,128)(2,1)}), bf16[32,16,512]{2,1,0:T(8,128)(2,1)}, u32[]{:S(2)}, u32[]{:S(2)}) %all-to-all-start.5) | async-done | bytes 524320 | tf_op jit(solution)/shard_map/all_to_all | solution.py:149
  160.2 4.6 %all-to-all-start.3 = ((bf16[32,16,512]{2,1,0:T(8,128)(2,1)}), bf16[32,16,512]{2,1,0:T(8,128)(2,1)}, u32[]{:S(2)}, u32[]{:S(2)}) async-start(bf16[32,16,512]{2,1,0:T(8,128)(2,1)} %bitcast.138), calls=%async_computation.3 | async-start | bytes 1048576 | tf_op jit(solution)/shard_map/all_to_all | solution.py:109
  164.8 1.0 fusion.36
  165.8 1.0 fusion.37
  166.7 1.0 fusion.38
  167.8 1.8 fusion.98
  169.5 1.7 copy.68
  171.2 0.8 copy.70
  173.5 5.0 %all-to-all-done.3 = bf16[32,16,512]{2,1,0:T(8,128)(2,1)} async-done(((bf16[32,16,512]{2,1,0:T(8,128)(2,1)}), bf16[32,16,512]{2,1,0:T(8,128)(2,1)}, u32[]{:S(2)}, u32[]{:S(2)}) %all-to-all-start.3) | async-done | bytes 524320 | tf_op jit(solution)/shard_map/all_to_all | solution.py:109
  178.5 1.5 multiply_reduce_fusion
  180.0 2.1 fusion.8
  182.2 1.8 multiply_reduce_fusion.1
  184.0 1.8 multiply_reduce_fusion.2
  185.8 1.8 multiply_reduce_fusion.3
  187.6 1.0 copy.52
  188.6 4.8 %all-to-all-start.4 = ((bf16[32,16,512]{2,1,0:T(8,128)(2,1)}), bf16[32,16,512]{2,1,0:T(8,128)(2,1)S(1)}, u32[]{:S(2)}, u32[]{:S(2)}) async-start(bf16[32,16,512]{2,1,0:T(8,128)(2,1)} %bitcast.140), calls=%async_computation.4 | async-start | bytes 1048576 | tf_op jit(solution)/shard_map/all_to_all | solution.py:135
  193.4 1.3 fusion.23
  194.8 1.7 fusion.9
  197.4 2.1 fusion.10
  199.4 7.8 %all-to-all-done.4 = bf16[32,16,512]{2,1,0:T(8,128)(2,1)S(1)} async-done(((bf16[32,16,512]{2,1,0:T(8,128)(2,1)}), bf16[32,16,512]{2,1,0:T(8,128)(2,1)S(1)}, u32[]{:S(2)}, u32[]{:S(2)}) %all-to-all-start.4) | async-done | bytes 524320 | tf_op jit(solution)/shard_map/all_to_all | solution.py:135
  207.2 1.2 gather_fusion
  208.4 4.9 %convolution_convert_fusion = bf16[256,4096]{1,0:T(8,128)(2,1)} fusion(bf16[512,4096]{1,0:T(8,128)(2,1)} %all-gather.3.cloned.1.call-done, bf16[256,512]{1,0:T(8,128)(2,1)S(1)} %gather_fusion, pred[256]{0:T(512)(128)(4,1)S(1)} %copy-done.29), kind=kOutput, calls=%fused_computation.8 | convolution fusion | flops 1074921472 | bytes 6553856 | tf_op jit(solution)/shard_map/dot_general | solution.py:137
  213.7 1.4 fusion.11
  215.9 1.0 copy.62
  216.9 4.3 %all-to-all-start.7 = ((bf16[32,16,512]{2,1,0:T(8,128)(2,1)}), bf16[32,16,512]{2,1,0:T(8,128)(2,1)S(1)}, u32[]{:S(2)}, u32[]{:S(2)}) async-start(bf16[32,16,512]{2,1,0:T(8,128)(2,1)} %bitcast.80), calls=%async_computation.8 | async-start | bytes 1048576 | tf_op jit(solution)/shard_map/all_to_all | solution.py:157
  221.3 1.4 fusion.19
  222.7 1.3 fusion.18
  224.0 1.3 fusion.17
  225.3 1.3 fusion.16
  226.7 1.0 copy.61
  227.7 7.4 %all-to-all-done.7 = bf16[32,16,512]{2,1,0:T(8,128)(2,1)S(1)} async-done(((bf16[32,16,512]{2,1,0:T(8,128)(2,1)}), bf16[32,16,512]{2,1,0:T(8,128)(2,1)S(1)}, u32[]{:S(2)}, u32[]{:S(2)}) %all-to-all-start.7) | async-done | bytes 524320 | tf_op jit(solution)/shard_map/all_to_all | solution.py:157
  235.1 4.4 %all-to-all-start.6 = ((bf16[32,16,512]{2,1,0:T(8,128)(2,1)}), bf16[32,16,512]{2,1,0:T(8,128)(2,1)S(1)}, u32[]{:S(2)}, u32[]{:S(2)}) async-start(bf16[32,16,512]{2,1,0:T(8,128)(2,1)} %bitcast.139), calls=%async_computation.7 | async-start | bytes 1048576 | tf_op jit(solution)/shard_map/all_to_all | solution.py:156
  239.5 1.2 convolution_convert_fusion.2
  240.7 1.2 convolution_convert_fusion.3
  241.9 1.2 convolution_convert_fusion.4
  243.2 1.2 convolution_convert_fusion.5
  244.4 1.1 copy.63
  245.5 8.0 %all-to-all-done.6 = bf16[32,16,512]{2,1,0:T(8,128)(2,1)S(1)} async-done(((bf16[32,16,512]{2,1,0:T(8,128)(2,1)}), bf16[32,16,512]{2,1,0:T(8,128)(2,1)S(1)}, u32[]{:S(2)}, u32[]{:S(2)}) %all-to-all-start.6) | async-done | bytes 524320 | tf_op jit(solution)/shard_map/all_to_all | solution.py:156
  253.4 4.2 %all-to-all-start.8 = ((bf16[32,16,512]{2,1,0:T(8,128)(2,1)}), bf16[32,16,512]{2,1,0:T(8,128)(2,1)S(1)}, u32[]{:S(2)}, u32[]{:S(2)}) async-start(bf16[32,16,512]{2,1,0:T(8,128)(2,1)} %bitcast.82), calls=%async_computation.9 | async-start | bytes 1048576 | tf_op jit(solution)/shard_map/all_to_all | solution.py:158
  257.7 1.2 gather_fusion.2
  258.8 1.2 gather_fusion.1
  260.0 11.5 %all-to-all-done.8 = bf16[32,16,512]{2,1,0:T(8,128)(2,1)S(1)} async-done(((bf16[32,16,512]{2,1,0:T(8,128)(2,1)}), bf16[32,16,512]{2,1,0:T(8,128)(2,1)S(1)}, u32[]{:S(2)}, u32[]{:S(2)}) %all-to-all-start.8) | async-done | bytes 524320 | tf_op jit(solution)/shard_map/all_to_all | solution.py:158
  271.5 1.2 gather_fusion.3
  272.6 1.0 broadcast_select_fusion
  (104 shorter events, 14.3 us)
Async XLA Ops:
  7.2 99.4 %all-gather.5.cloned.1.call-start = ((), (), s32[]{:S(2)}) async-start(), calls=%async_computation.12 | async-start | bytes 2359296 | tf_op jit(solution)/shard_map/all_gather | solution.py:144
  7.9 121.4 %all-gather.3.cloned.1.call-start = ((), (), s32[]{:S(2)}) async-start(), calls=%async_computation.10 | async-start | bytes 4325376 | tf_op jit(solution)/shard_map/all_gather | solution.py:105
  11.7 21.2 %all-to-all-start = ((s32[32,1,1]{2,1,0:T(1,128)}), s32[32,1,1]{2,1,0:T(1,128)S(1)}, u32[]{:S(2)}, u32[]{:S(2)}) async-start(s32[32,1,1]{2,1,0:T(1,128)} %copy.50), calls=%async_computation | async-start | bytes 32768 | tf_op jit(solution)/shard_map/all_to_all | solution.py:110
  32.9 21.3 %all-to-all-start.1 = ((bf16[32,16,512]{2,1,0:T(8,128)(2,1)}), bf16[32,16,512]{2,1,0:T(8,128)(2,1)S(1)}, u32[]{:S(2)}, u32[]{:S(2)}) async-start(bf16[32,16,512]{2,1,0:T(8,128)(2,1)} %bitcast.68), calls=%async_computation.1 | async-start | bytes 1048576 | tf_op jit(solution)/shard_map/all_to_all | solution.py:107
  54.2 49.9 %copy-start.4 = (bf16[32,16,512]{2,1,0:T(8,128)(2,1)}, bf16[32,16,512]{2,1,0:T(8,128)(2,1)S(1)}, u32[]{:S(2)}) copy-start(bf16[32,16,512]{2,1,0:T(8,128)(2,1)S(1)} %all-to-all-done.1) | copy-start | bytes 1572868
  54.2 49.5 %all-to-all-start.2 = ((bf16[32,16,512]{2,1,0:T(8,128)(2,1)}), bf16[32,16,512]{2,1,0:T(8,128)(2,1)S(1)}, u32[]{:S(2)}, u32[]{:S(2)}) async-start(bf16[32,16,512]{2,1,0:T(8,128)(2,1)} %bitcast.70), calls=%async_computation.2 | async-start | bytes 1048576 | tf_op jit(solution)/shard_map/all_to_all | solution.py:108
  103.7 0.8 copy-start.6
  104.5 41.9 %copy-start.1 = (f32[512,512]{0,1:T(8,128)}, f32[512,512]{0,1:T(8,128)S(1)}, u32[]{:S(2)}) copy-start(f32[512,512]{0,1:T(8,128)S(1)} %get-tuple-element.86) | copy-start | bytes 3145732
  104.8 60.0 %copy-start = (f32[512,512]{0,1:T(8,128)}, f32[512,512]{0,1:T(8,128)S(1)}, u32[]{:S(2)}) copy-start(f32[512,512]{0,1:T(8,128)S(1)} %get-tuple-element.88) | copy-start | bytes 3145732
  136.9 23.3 %all-to-all-start.5 = ((bf16[32,16,512]{2,1,0:T(8,128)(2,1)}), bf16[32,16,512]{2,1,0:T(8,128)(2,1)}, u32[]{:S(2)}, u32[]{:S(2)}) async-start(bf16[32,16,512]{2,1,0:T(8,128)(2,1)} %bitcast.141), calls=%async_computation.6 | async-start | bytes 1048576 | tf_op jit(solution)/shard_map/all_to_all | solution.py:149
  146.6 19.2 %copy-start.28 = (f32[512]{0:T(512)}, f32[512]{0:T(512)S(1)}, u32[]{:S(2)}) copy-start(f32[512]{0:T(512)S(1)} %fusion.34) | copy-start | bytes 6148
  146.6 1.9 copy-start.2
  146.8 20.0 %copy-start.26 = (f32[512]{0:T(512)}, f32[512]{0:T(512)S(1)}, u32[]{:S(2)}) copy-start(f32[512]{0:T(512)S(1)} %fusion.32) | copy-start | bytes 6148
  147.0 19.8 %copy-start.24 = (f32[512]{0:T(512)}, f32[512]{0:T(512)S(1)}, u32[]{:S(2)}) copy-start(f32[512]{0:T(512)S(1)} %fusion.30) | copy-start | bytes 6148
  148.5 19.3 %copy-start.22 = (f32[512]{0:T(512)}, f32[512]{0:T(512)S(1)}, u32[]{:S(2)}) copy-start(f32[512]{0:T(512)S(1)} %fusion.28) | copy-start | bytes 6148
  160.2 18.3 %all-to-all-start.3 = ((bf16[32,16,512]{2,1,0:T(8,128)(2,1)}), bf16[32,16,512]{2,1,0:T(8,128)(2,1)}, u32[]{:S(2)}, u32[]{:S(2)}) async-start(bf16[32,16,512]{2,1,0:T(8,128)(2,1)} %bitcast.138), calls=%async_computation.3 | async-start | bytes 1048576 | tf_op jit(solution)/shard_map/all_to_all | solution.py:109
  165.8 14.3 %copy-start.3 = (f32[512,512]{0,1:T(8,128)S(1)}, f32[512,512]{0,1:T(8,128)}, u32[]{:S(2)}) copy-start(f32[512,512]{0,1:T(8,128)} %copy-done.1) | copy-start | bytes 3145732
  172.0 13.8 %copy-start.18 = (bf16[512,128]{0,1:T(8,128)(2,1)S(1)}, bf16[512,128]{0,1:T(8,128)(2,1)}, u32[]{:S(2)}) copy-start(bf16[512,128]{0,1:T(8,128)(2,1)} %copy.68) | copy-start | bytes 393220
  172.8 11.2 %copy-start.19 = (bf16[512,128]{0,1:T(8,128)(2,1)S(1)}, bf16[512,128]{0,1:T(8,128)(2,1)}, u32[]{:S(2)}) copy-start(bf16[512,128]{0,1:T(8,128)(2,1)} %copy.69) | copy-start | bytes 393220
  173.5 8.6 %copy-start.20 = (bf16[512,128]{0,1:T(8,128)(2,1)S(1)}, bf16[512,128]{0,1:T(8,128)(2,1)}, u32[]{:S(2)}) copy-start(bf16[512,128]{0,1:T(8,128)(2,1)} %copy.70) | copy-start | bytes 393220
  178.5 3.7 %copy-start.13 = (bf16[512,512]{0,1:T(8,128)(2,1)S(1)}, bf16[512,512]{0,1:T(8,128)(2,1)}, u32[]{:S(2)}) copy-start(bf16[512,512]{0,1:T(8,128)(2,1)} %fusion.36) | copy-start | bytes 1572868
  178.5 5.5 %copy-start.11 = (bf16[512,512]{0,1:T(8,128)(2,1)S(1)}, bf16[512,512]{0,1:T(8,128)(2,1)}, u32[]{:S(2)}) copy-start(bf16[512,512]{0,1:T(8,128)(2,1)} %fusion.37) | copy-start | bytes 1572868
  178.5 7.3 %copy-start.9 = (bf16[512,512]{0,1:T(8,128)(2,1)S(1)}, bf16[512,512]{0,1:T(8,128)(2,1)}, u32[]{:S(2)}) copy-start(bf16[512,512]{0,1:T(8,128)(2,1)} %fusion.38) | copy-start | bytes 1572868
  182.2 11.3 %copy-start.5 = (bf16[32,16,512]{2,1,0:T(8,128)(2,1)S(1)}, bf16[32,16,512]{2,1,0:T(8,128)(2,1)}, u32[]{:S(2)}) copy-start(bf16[32,16,512]{2,1,0:T(8,128)(2,1)} %copy-done.4) | copy-start | bytes 1572868
  182.2 12.6 %copy-start.27 = (f32[512]{0:T(512)S(1)}, f32[512]{0:T(512)}, u32[]{:S(2)}) copy-start(f32[512]{0:T(512)} %copy-done.26) | copy-start | bytes 6148
  187.6 9.8 %copy-start.25 = (f32[512]{0:T(512)S(1)}, f32[512]{0:T(512)}, u32[]{:S(2)}) copy-start(f32[512]{0:T(512)} %copy-done.24) | copy-start | bytes 6148
  187.6 9.8 %copy-start.31 = (f32[512]{0:T(512)S(1)}, f32[512]{0:T(512)}, u32[]{:S(2)}) copy-start(f32[512]{0:T(512)} %get-tuple-element.97) | copy-start | bytes 6148
  188.6 18.6 %all-to-all-start.4 = ((bf16[32,16,512]{2,1,0:T(8,128)(2,1)}), bf16[32,16,512]{2,1,0:T(8,128)(2,1)S(1)}, u32[]{:S(2)}, u32[]{:S(2)}) async-start(bf16[32,16,512]{2,1,0:T(8,128)(2,1)} %bitcast.140), calls=%async_computation.4 | async-start | bytes 1048576 | tf_op jit(solution)/shard_map/all_to_all | solution.py:135
  193.4 80.3 %reduce-scatter.2.cloned.1.call-start = ((), (), s32[]{:S(2)}) async-start(), calls=%async_computation.11 | async-start | bytes 2359296 | tf_op jit(solution)/shard_map/reduce_scatter | solution.py:139
  194.8 12.4 %copy-start.21 = (s32[1024]{0:T(1024)S(1)}, s32[1024]{0:T(1024)}, u32[]{:S(2)}) copy-start(s32[1024]{0:T(1024)} %pad_clamp_fusion) | copy-start | bytes 12292
  196.5 0.8 copy-start.15
  196.5 11.8 %copy-start.29 = (pred[256]{0:T(512)(128)(4,1)S(1)}, pred[256]{0:T(512)(128)(4,1)}, u32[]{:S(2)}) copy-start(pred[256]{0:T(512)(128)(4,1)} %get-tuple-element.8) | copy-start | bytes 772
  208.4 5.0 %copy-start.16 = (bf16[512,512]{0,1:T(8,128)(2,1)S(1)}, bf16[512,512]{0,1:T(8,128)(2,1)}, u32[]{:S(2)}) copy-start(bf16[512,512]{0,1:T(8,128)(2,1)} %fusion.10) | copy-start | bytes 1572868
  208.4 5.3 %copy-start.23 = (f32[512]{0:T(512)S(1)}, f32[512]{0:T(512)}, u32[]{:S(2)}) copy-start(f32[512]{0:T(512)} %copy-done.22) | copy-start | bytes 6148
  208.4 5.3 %copy-start.30 = (f32[512]{0:T(512)S(1)}, f32[512]{0:T(512)}, u32[]{:S(2)}) copy-start(f32[512]{0:T(512)} %get-tuple-element.99) | copy-start | bytes 6148
  213.7 7.6 %copy-start.7 = (bf16[32,16,512]{2,1,0:T(8,128)(2,1)S(1)}, bf16[32,16,512]{2,1,0:T(8,128)(2,1)}, u32[]{:S(2)}) copy-start(bf16[32,16,512]{2,1,0:T(8,128)(2,1)} %copy-done.6) | copy-start | bytes 1572868
  215.1 0.8 copy-start.17
  215.9 23.6 %copy-start.8 = (bf16[512,512]{0,1:T(8,128)(2,1)S(1)}, bf16[512,512]{0,1:T(8,128)(2,1)}, u32[]{:S(2)}) copy-start(bf16[512,512]{0,1:T(8,128)(2,1)} %fusion.35) | copy-start | bytes 1572868
  216.9 23.8 %copy-start.14 = (bf16[512,512]{0,1:T(8,128)(2,1)S(1)}, bf16[512,512]{0,1:T(8,128)(2,1)}, u32[]{:S(2)}) copy-start(bf16[512,512]{0,1:T(8,128)(2,1)} %fusion.36) | copy-start | bytes 1572868
  216.9 18.1 %all-to-all-start.7 = ((bf16[32,16,512]{2,1,0:T(8,128)(2,1)}), bf16[32,16,512]{2,1,0:T(8,128)(2,1)S(1)}, u32[]{:S(2)}, u32[]{:S(2)}) async-start(bf16[32,16,512]{2,1,0:T(8,128)(2,1)} %bitcast.80), calls=%async_computation.8 | async-start | bytes 1048576 | tf_op jit(solution)/shard_map/all_to_all | solution.py:157
  221.3 20.7 %copy-start.12 = (bf16[512,512]{0,1:T(8,128)(2,1)S(1)}, bf16[512,512]{0,1:T(8,128)(2,1)}, u32[]{:S(2)}) copy-start(bf16[512,512]{0,1:T(8,128)(2,1)} %fusion.37) | copy-start | bytes 1572868
  221.3 21.9 %copy-start.10 = (bf16[512,512]{0,1:T(8,128)(2,1)S(1)}, bf16[512,512]{0,1:T(8,128)(2,1)}, u32[]{:S(2)}) copy-start(bf16[512,512]{0,1:T(8,128)(2,1)} %fusion.38) | copy-start | bytes 1572868
  235.1 18.4 %all-to-all-start.6 = ((bf16[32,16,512]{2,1,0:T(8,128)(2,1)}), bf16[32,16,512]{2,1,0:T(8,128)(2,1)S(1)}, u32[]{:S(2)}, u32[]{:S(2)}) async-start(bf16[32,16,512]{2,1,0:T(8,128)(2,1)} %bitcast.139), calls=%async_computation.7 | async-start | bytes 1048576 | tf_op jit(solution)/shard_map/all_to_all | solution.py:156
  253.4 18.1 %all-to-all-start.8 = ((bf16[32,16,512]{2,1,0:T(8,128)(2,1)}), bf16[32,16,512]{2,1,0:T(8,128)(2,1)S(1)}, u32[]{:S(2)}, u32[]{:S(2)}) async-start(bf16[32,16,512]{2,1,0:T(8,128)(2,1)} %bitcast.82), calls=%async_computation.9 | async-start | bytes 1048576 | tf_op jit(solution)/shard_map/all_to_all | solution.py:158
Sparse Core Ops, SparseCore 0:
  9.8 29.8 all-gather.4
  42.1 87.1 all-gather.2
  213.5 27.1 reduce-scatter.1
where the time goes:
time: 282 us; the launch traced here: 280 us
  waiting for transfers between devices  91.2 us (32%)
  starting transfers between devices  52 us (18%)
  other arithmetic  51.3 us (18%)
  matrix products  40.7 us (14%)
  local copies, waits for them, and re-layouts  30.7 us (11%)
  between operations  14.3 us (5%)
    all_gather x1, waiting for transfers between devices, on_device(): full_weight = lax.all_gather(out_weight, 'seq', axis=1, tiled=True)  22.8 us
    select_n x1, other arithmetic, on_device(): rank_rows[:, None] // BLK == jnp.arange(blocks, dtype=jnp.int32)[None, :]  19.9 us
    not x1, other arithmetic, on_device(): allowed = usable | diagonal & ~row_live[:, None]  19.9 us
    all_to_all x1, waiting for transfers between devices, on_device(): lax.all_to_all(grad_v, 'seq', split_axis=0, concat_axis=0, tiled=True)  11.5 us
    all_to_all x1, starting transfers between devices, on_device(): lax.all_to_all(send_counts, 'seq', split_axis=0, concat_axis=0, tiled=True)  11.5 us
    scatter x4, local copies, waits for them, and re-layouts, to_slots(): jnp.zeros((slot_total, row_data.shape[1]), row_data.dtype).at[slot_index]  11 us
    all_to_all x1, waiting for transfers between devices, on_device(): lax.all_to_all(to_slots(queries), 'seq', split_axis=0, concat_axis=0, til...  10.9 us
    all_to_all x1, waiting for transfers between devices, on_device(): lax.all_to_all(to_slots(grad_attention), 'seq', split_axis=0, concat_axis...  10.7 us
  transfers between devices with their start and end apart: 12, of which 9 were waited for; matrix products, arithmetic and copies ran while one was open for 35% of the time, Pallas kernels for 0%

commit v1 on v0

v1 whole, which is shorter than its diff:
```python
import math

import jax
import jax.numpy as jnp
from jax import lax
from jax.sharding import PartitionSpec as P

HD = 128
BLK = 128


def select_rows(onehot, rows):
    return jnp.dot(onehot, rows, preferred_element_type=jnp.float32).astype(rows.dtype)


def select_rows_t(onehot, rows):
    return lax.dot_general(
        onehot, rows, (((0,), (0,)), ((), ())), preferred_element_type=jnp.float32
    ).astype(rows.dtype)


def on_device(queries, key_rows, value_rows, out_weight, grad_output, cluster_ids, block_pattern):
    tokens = queries.shape[0]
    width = queries.shape[1]
    head_count = width // HD
    groups = lax.axis_size("seq")
    slot_rows = 2 * tokens // groups
    slot_total = groups * slot_rows
    ranks = tokens
    owner_index = lax.axis_index("seq")
    score_scale = 1.0 / math.sqrt(HD)

    members = (cluster_ids[:, None] == jnp.arange(groups, dtype=jnp.int32)[None, :]).astype(
        jnp.int32
    )
    earlier = jnp.cumsum(members, axis=0) - members
    local_rank = jnp.sum(earlier * members, axis=1)
    send_counts = jnp.sum(members, axis=0)
    slot_index = cluster_ids * slot_rows + local_rank
    to_slot = (
        jnp.arange(slot_total, dtype=jnp.int32)[:, None] == slot_index[None, :]
    ).astype(jnp.bfloat16)

    full_weight = lax.all_gather(out_weight, "seq", axis=1, tiled=True)
    qkv = jnp.concatenate([queries, key_rows, value_rows], axis=1)
    qkv_in = lax.all_to_all(select_rows(to_slot, qkv), "seq", 0, 0, tiled=True)
    got_counts = lax.all_to_all(send_counts, "seq", 0, 0, tiled=True)

    offsets = jnp.cumsum(got_counts) - got_counts
    place = jnp.arange(slot_rows, dtype=jnp.int32)
    row_live = (place[None, :] < got_counts[:, None]).reshape(slot_total)
    rank_rows = (offsets[:, None] + place[None, :]).reshape(slot_total)
    to_rank = (
        (rank_rows[None, :] == jnp.arange(ranks, dtype=jnp.int32)[:, None]) & row_live[None, :]
    ).astype(jnp.bfloat16)
    qkv_c = select_rows(to_rank, qkv_in)
    q_c = qkv_c[:, :width].reshape(ranks, head_count, HD)
    k_c = qkv_c[:, width : 2 * width].reshape(ranks, head_count, HD)
    v_c = qkv_c[:, 2 * width :].reshape(ranks, head_count, HD)

    pattern = lax.dynamic_index_in_dim(block_pattern, owner_index, 0, keepdims=False)
    rank = jnp.arange(ranks, dtype=jnp.int32)
    blk = rank // BLK
    blk_q = blk[:, None]
    blk_k = blk[None, :]
    pat = jnp.where(
        blk_q == 0,
        jnp.where(blk_k == 0, pattern[0, 0], pattern[0, 1]),
        jnp.where(blk_k == 0, pattern[1, 0], pattern[1, 1]),
    )
    allowed = (rank[None, :] <= rank[:, None]) & (pat == 1)

    scores = (
        jnp.einsum("qhd,khd->hqk", q_c, k_c, preferred_element_type=jnp.float32) * score_scale
    )
    scores = jnp.where(allowed[None], scores, -jnp.inf)
    shifted = jnp.exp(scores - jnp.max(scores, axis=2, keepdims=True))
    probs = shifted / jnp.sum(shifted, axis=2, keepdims=True)
    probs_b = probs.astype(jnp.bfloat16)
    attn_c = jnp.einsum("hqk,khd->qhd", probs_b, v_c, preferred_element_type=jnp.float32).astype(
        jnp.bfloat16
    )

    attn_back = lax.all_to_all(
        select_rows_t(to_rank, attn_c.reshape(ranks, width)), "seq", 0, 0, tiled=True
    )
    attn_local = select_rows_t(to_slot, attn_back)
    partial_value = jnp.dot(attn_local, full_weight, preferred_element_type=jnp.float32)
    rounded_part = lax.optimization_barrier(partial_value.astype(jnp.bfloat16)).astype(jnp.float32)
    layer_out = lax.psum_scatter(
        rounded_part.astype(jnp.bfloat16), "head", scatter_dimension=1, tiled=True
    )

    grad_sum = jnp.einsum(
        "td,wd->tw",
        lax.all_gather(grad_output, "head", axis=1, tiled=True),
        full_weight,
        preferred_element_type=jnp.float32,
    )
    grad_attention = grad_sum.astype(jnp.bfloat16)
    grad_in = lax.all_to_all(select_rows(to_slot, grad_attention), "seq", 0, 0, tiled=True)
    g_c = select_rows(to_rank, grad_in).reshape(ranks, head_count, HD)

    delta = jnp.sum(g_c.astype(jnp.float32) * attn_c.astype(jnp.float32), axis=2).T[:, :, None]
    dprobs = jnp.einsum("qhd,khd->hqk", g_c, v_c, preferred_element_type=jnp.float32)
    dscores = (probs * (dprobs - delta)).astype(jnp.bfloat16)
    grad_q = (
        jnp.einsum("hqk,khd->qhd", dscores, k_c, preferred_element_type=jnp.float32) * score_scale
    ).astype(jnp.bfloat16)
    grad_k = (
        jnp.einsum("hqk,qhd->khd", dscores, q_c, preferred_element_type=jnp.float32) * score_scale
    ).astype(jnp.bfloat16)
    grad_v = jnp.einsum("hqk,qhd->khd", probs_b, g_c, preferred_element_type=jnp.float32).astype(
        jnp.bfloat16
    )
    grads_c = jnp.concatenate(
        [
            grad_q.reshape(ranks, width),
            grad_k.reshape(ranks, width),
            grad_v.reshape(ranks, width),
        ],
        axis=1,
    )
    grads_back = lax.all_to_all(select_rows_t(to_rank, grads_c), "seq", 0, 0, tiled=True)
    grads_local = select_rows_t(to_slot, grads_back)
    return (
        layer_out,
        grads_local[:, :width],
        grads_local[:, width : 2 * width],
        grads_local[:, 2 * width :],
    )


def solution(mesh):
    in_specs = (
        P("seq", "head"),
        P("seq", "head"),
        P("seq", "head"),
        P("head", "seq"),
        P("seq", "head"),
        P("seq"),
        P(),
    )
    out_specs = (P("seq", "head"), P("seq", "head"), P("seq", "head"), P("seq", "head"))
    return jax.shard_map(
        on_device, mesh=mesh, in_specs=in_specs, out_specs=out_specs, check_vma=False
    )
```

time: 282 us -> 234 us (0.83)
  other arithmetic: 51.3 us -> 6.58 us
  blocking collectives: 0 us -> 36.8 us
  waiting for transfers between devices: 91.2 us -> 124 us
  local copies, waits for them, and re-layouts: 30.7 us -> 3.22 us
  starting transfers between devices: 52 us -> 29.1 us
  matrix products: 40.7 us -> 19.3 us
    all_gather x1, waiting for transfers between devices: 22.8 us -> 91.1 us  [on_device(): full_weight = lax.all_gather(out_weight, 'seq', axis=1, tiled=True)]
    all_to_all x0 -> x1, blocking collectives: none -> 36.8 us  [on_device(): lax.all_to_all(select_rows_t(to_rank, grads_c), 'seq', 0, 0, tiled=True)]
    all_to_all x9 -> x4, waiting for transfers between devices: 67 us -> 31.5 us  [the longest x1 13.2 us: on_device(): lax.all_to_all(select_rows_t(to_rank, attn_c.reshape(ranks, width)), 'seq...]
    all_to_all x9 -> x4, starting transfers between devices: 51.9 us -> 29 us  [the longest x1 11.5 us: on_device(): got_counts = lax.all_to_all(send_counts, 'seq', 0, 0, tiled=True)]
    dot_general x26 -> x12, matrix products: 35.8 us -> 13.7 us  [the longest x4 8.94 us: select_rows(): jnp.dot(onehot, rows, preferred_element_type=jnp.float32).astype(rows.dtype)]
    not x1 -> x0, other arithmetic: 19.9 us -> none  [on_device(): allowed = usable | diagonal & ~row_live[:, None]]
    select_n x2 -> x1, other arithmetic: 20.9 us -> 2.59 us  [on_device(): jnp.where(blk_k == 0, pattern[1, 0], pattern[1, 1])]
    scatter x4 -> x0, local copies, waits for them, and re-layouts: 11 us -> none  [to_slots(): jnp.zeros((slot_total, row_data.shape[1]), row_data.dtype).at[slot_index]]
  transfers between devices with their start and end apart: 12 -> 7, of which waited for: 9 -> 4; matrix products, arithmetic and copies ran while one was open for 35% -> 9% of each run, Pallas kernels for 0% -> 0%
where the time goes in v1:
time: 234 us; the launch traced here: 233 us
  waiting for transfers between devices  124 us (53%)
  blocking collectives  36.8 us (16%)
  starting transfers between devices  29.1 us (12%)
  matrix products  19.3 us (8%)
  between operations  13.9 us (6%)
  other arithmetic  6.58 us (3%)
  local copies, waits for them, and re-layouts  3.22 us (1%)
    all_gather x1, waiting for transfers between devices, on_device(): full_weight = lax.all_gather(out_weight, 'seq', axis=1, tiled=True)  91.1 us
    all_to_all x1, blocking collectives, on_device(): lax.all_to_all(select_rows_t(to_rank, grads_c), 'seq', 0, 0, tiled=True)  36.8 us
    all_to_all x1, waiting for transfers between devices, on_device(): lax.all_to_all(select_rows_t(to_rank, attn_c.reshape(ranks, width)), 'seq...  13.2 us
    all_to_all x1, waiting for transfers between devices, on_device(): lax.all_to_all(select_rows(to_slot, grad_attention), 'seq', 0, 0, tiled=T...  12.2 us
    all_to_all x1, starting transfers between devices, on_device(): got_counts = lax.all_to_all(send_counts, 'seq', 0, 0, tiled=True)  11.5 us
    all_to_all x1, starting transfers between devices, on_device(): lax.all_to_all(select_rows(to_slot, grad_attention), 'seq', 0, 0, tiled=T...  9.14 us
    dot_general x4, matrix products, select_rows(): jnp.dot(onehot, rows, preferred_element_type=jnp.float32).astype(rows.dtype)  8.94 us
    all_to_all x1, waiting for transfers between devices, on_device(): got_counts = lax.all_to_all(send_counts, 'seq', 0, 0, tiled=True)  6.13 us
  transfers between devices with their start and end apart: 7, of which 4 were waited for; matrix products, arithmetic and copies ran while one was open for 9% of the time, Pallas kernels for 0%

profile of v1, /device:TPU:4, one launch (start us, length us, event | category | flops | bytes accessed | tf_op | source)
XLA Modules:
  0.0 232.9 jit_solution(15324087626395265288)
XLA Ops:
  7.2 0.0 copy-start
  7.2 0.0 all-gather.5.cloned.1.call-start
  7.2 0.7 all-gather.5.cloned.1.call-update
  7.9 0.0 all-gather.3.cloned.1.call-start
  8.0 0.7 all-gather.3.cloned.1.call-update
  8.7 0.7 fusion.45
  9.4 0.6 reduce-window.18
  9.9 0.2 slice_reduce_fusion
  10.2 0.9 convert_reduce_fusion
  11.0 0.7 copy.57
  11.7 11.5 %all-to-all-start = ((s32[32,1,1]{2,1,0:T(1,128)}), s32[32,1,1]{2,1,0:T(1,128)S(1)}, u32[]{:S(2)}, u32[]{:S(2)}) async-start(s32[32,1,1]{2,1,0:T(1,128)} %copy.57), calls=%async_computation | async-start | bytes 32768 | tf_op jit(solution)/shard_map/all_to_all | solution.py:47
  23.2 0.7 multiply_add_fusion
  23.9 2.9 %convolution_convert_fusion.2 = bf16[512,1536]{1,0:T(8,128)(2,1)} fusion(bf16[256,512]{1,0:T(8,128)(2,1)} %param.9, bf16[256,512]{1,0:T(8,128)(2,1)} %param.8, bf16[256,512]{1,0:T(8,128)(2,1)} %param.7, s32[256]{0:T(256)S(1)} %multiply_add_fusion), kind=kOutput, calls=%fused_computation.3 | convolution fusion | flops 405929984 | bytes 2360320 | tf_op jit(solution)/shard_map/dot_general | solution.py:13
  26.8 6.1 %all-to-all-done = s32[32,1,1]{2,1,0:T(1,128)S(1)} async-done(((s32[32,1,1]{2,1,0:T(1,128)}), s32[32,1,1]{2,1,0:T(1,128)S(1)}, u32[]{:S(2)}, u32[]{:S(2)}) %all-to-all-start) | async-done | bytes 160 | tf_op jit(solution)/shard_map/all_to_all | solution.py:47
  32.9 4.0 %all-to-all-start.1 = ((bf16[32,16,1536]{2,1,0:T(8,128)(2,1)}), bf16[32,16,1536]{2,1,0:T(8,128)(2,1)S(1)}, u32[]{:S(2)}, u32[]{:S(2)}) async-start(bf16[32,16,1536]{2,1,0:T(8,128)(2,1)} %bitcast.4), calls=%async_computation.1 | async-start | bytes 3145728 | tf_op jit(solution)/shard_map/all_to_all | solution.py:46
  36.9 0.0 copy-done
  36.9 0.2 dynamic-slice_reduce_fusion
  37.1 0.6 fusion.56
  37.7 2.6 %broadcast_select_fusion = (s32[256]{0:T(256)S(1)}, s32[256]{0:T(256)S(1)}) fusion(s32[]{:T(128)} %bitcast.9, s32[]{:T(128)} %bitcast.8, s32[]{:T(128)} %bitcast.7, s32[]{:T(128)} %bitcast.6), kind=kLoop, calls=%fused_computation.80 | loop fusion | flops 2816 | bytes 2064 | tf_op jit(solution)/shard_map/jit(_where)/select_n | solution.py:69
  40.3 0.1 fusion.36
  40.5 0.1 reduce-window.20
  40.5 0.1 reduce.1
  40.6 0.7 reduce.2
  41.3 0.1 iota_compare_fusion.10
  41.4 0.1 lt.24
  41.5 0.0 all-gather.5.cloned.1.call-done
  41.5 91.1 %all-gather.3.cloned.1.call-done = bf16[512,4096]{1,0:T(8,128)(2,1)} async-done(((bf16[512,128]{1,0:T(8,128)(2,1)}), bf16[512,4096]{1,0:T(8,128)(2,1)}) %all-gather.3.cloned.1.call-update) | async-done | bytes 4194320 | tf_op jit(solution)/shard_map/all_gather | solution.py:44
  132.6 5.2 %convolution_convert_fusion.6 = bf16[512,512]{1,0:T(8,128)(2,1)} fusion(bf16[256,4096]{1,0:T(8,128)(2,1)} %all-gather.5.cloned.1.call-done, bf16[512,4096]{1,0:T(8,128)(2,1)} %all-gather.3.cloned.1.call-done, s32[256]{0:T(256)S(1)} %multiply_add_fusion), kind=kOutput, calls=%fused_computation.14 | convolution fusion | flops 1208483840 | bytes 6816768 | tf_op jit(solution)/shard_map/dot_general | solution.py:13
  137.8 0.0 all-to-all-done.1
  137.8 9.1 %all-to-all-start.3 = ((bf16[32,16,512]{2,1,0:T(8,128)(2,1)}), bf16[32,16,512]{2,1,0:T(8,128)(2,1)S(1)}, u32[]{:S(2)}, u32[]{:S(2)}) async-start(bf16[32,16,512]{2,1,0:T(8,128)(2,1)} %bitcast.14), calls=%async_computation.4 | async-start | bytes 1048576 | tf_op jit(solution)/shard_map/all_to_all | solution.py:101
  146.9 0.1 iota_add_fusion
  147.0 0.1 add.47
  147.1 0.6 convolution_convert_fusion.4
  147.6 0.1 fusion.55
  147.7 0.1 copy.79
  147.8 0.1 copy.78
  148.0 0.5 fusion.57
  148.5 12.2 %all-to-all-done.3 = bf16[32,16,512]{2,1,0:T(8,128)(2,1)S(1)} async-done(((bf16[32,16,512]{2,1,0:T(8,128)(2,1)}), bf16[32,16,512]{2,1,0:T(8,128)(2,1)S(1)}, u32[]{:S(2)}, u32[]{:S(2)}) %all-to-all-start.3) | async-done | bytes 524320 | tf_op jit(solution)/shard_map/all_to_all | solution.py:101
  160.7 0.3 convolution_convert_fusion.8
  161.0 0.1 copy.63
  161.2 0.8 multiply_reduce_fusion
  162.0 1.2 convolution_convert_fusion.5
  163.1 4.4 %all-to-all-start.2 = ((bf16[32,16,512]{2,1,0:T(8,128)(2,1)}), bf16[32,16,512]{2,1,0:T(8,128)(2,1)S(1)}, u32[]{:S(2)}, u32[]{:S(2)}) async-start(bf16[32,16,512]{2,1,0:T(8,128)(2,1)} %bitcast.12), calls=%async_computation.2 | async-start | bytes 1048576 | tf_op jit(solution)/shard_map/all_to_all | solution.py:84
  167.5 0.0 reduce-scatter.2.cloned.1.call-start
  167.5 0.3 fusion.5
  167.8 0.3 fusion.7
  168.2 13.2 %all-to-all-done.2 = bf16[32,16,512]{2,1,0:T(8,128)(2,1)S(1)} async-done(((bf16[32,16,512]{2,1,0:T(8,128)(2,1)}), bf16[32,16,512]{2,1,0:T(8,128)(2,1)S(1)}, u32[]{:S(2)}, u32[]{:S(2)}) %all-to-all-start.2) | async-done | bytes 524320 | tf_op jit(solution)/shard_map/all_to_all | solution.py:84
  181.3 5.0 %convolution_convert_fusion = bf16[256,4096]{1,0:T(8,128)(2,1)} fusion(bf16[512,4096]{1,0:T(8,128)(2,1)} %all-gather.3.cloned.1.call-done, bf16[512,512]{1,0:T(8,128)(2,1)S(1)} %bitcast.75, s32[256]{0:T(256)S(1)} %multiply_add_fusion), kind=kOutput, calls=%fused_computation.1 | convolution fusion | flops 1209270272 | bytes 6816768 | tf_op jit(solution)/shard_map/dot_general | solution.py:88
  186.4 0.0 reduce-scatter.2.cloned.1.call-update
  186.4 0.8 convolution_convert_fusion.7
  187.2 0.2 fusion.6
  187.4 0.6 convolution_convert_fusion.1
  188.1 36.8 %all_to_all.57 = bf16[32,16,1536]{2,1,0:T(8,128)(2,1)S(1)} all-to-all(bf16[32,16,1536]{2,1,0:T(8,128)(2,1)S(1)} %bitcast.76), channel_id=1, replica_groups=mesh['seq'=32,'head'=8] {'seq'}, dimensions={0} | all-to-all | bytes 3145728 | tf_op jit(solution)/shard_map/all_to_all | solution.py:124
  224.9 0.6 convolution_convert_fusion.3
  225.5 0.9 fusion.54
  226.4 0.0 reduce-scatter.2.cloned.1.call-done
  (4 shorter events, 0.1 us)
Async XLA Ops:
  7.2 29.7 %copy-start = (s32[32,2,2]{0,2,1:T(2,128)S(1)}, s32[32,2,2]{0,2,1:T(2,128)}, u32[]{:S(2)}) copy-start(s32[32,2,2]{0,2,1:T(2,128)} %param.13) | copy-start | bytes 1540
  7.2 34.3 %all-gather.5.cloned.1.call-start = ((), (), s32[]{:S(2)}) async-start(), calls=%async_computation.8 | async-start | bytes 2359296 | tf_op jit(solution)/shard_map/all_gather | solution.py:96
  7.9 124.6 %all-gather.3.cloned.1.call-start = ((), (), s32[]{:S(2)}) async-start(), calls=%async_computation.6 | async-start | bytes 4325376 | tf_op jit(solution)/shard_map/all_gather | solution.py:44
  11.7 21.2 %all-to-all-start = ((s32[32,1,1]{2,1,0:T(1,128)}), s32[32,1,1]{2,1,0:T(1,128)S(1)}, u32[]{:S(2)}, u32[]{:S(2)}) async-start(s32[32,1,1]{2,1,0:T(1,128)} %copy.57), calls=%async_computation | async-start | bytes 32768 | tf_op jit(solution)/shard_map/all_to_all | solution.py:47
  32.9 104.8 %all-to-all-start.1 = ((bf16[32,16,1536]{2,1,0:T(8,128)(2,1)}), bf16[32,16,1536]{2,1,0:T(8,128)(2,1)S(1)}, u32[]{:S(2)}, u32[]{:S(2)}) async-start(bf16[32,16,1536]{2,1,0:T(8,128)(2,1)} %bitcast.4), calls=%async_computation.1 | async-start | bytes 3145728 | tf_op jit(solution)/shard_map/all_to_all | solution.py:46
  137.8 23.0 %all-to-all-start.3 = ((bf16[32,16,512]{2,1,0:T(8,128)(2,1)}), bf16[32,16,512]{2,1,0:T(8,128)(2,1)S(1)}, u32[]{:S(2)}, u32[]{:S(2)}) async-start(bf16[32,16,512]{2,1,0:T(8,128)(2,1)} %bitcast.14), calls=%async_computation.4 | async-start | bytes 1048576 | tf_op jit(solution)/shard_map/all_to_all | solution.py:101
  163.1 18.2 %all-to-all-start.2 = ((bf16[32,16,512]{2,1,0:T(8,128)(2,1)}), bf16[32,16,512]{2,1,0:T(8,128)(2,1)S(1)}, u32[]{:S(2)}, u32[]{:S(2)}) async-start(bf16[32,16,512]{2,1,0:T(8,128)(2,1)} %bitcast.12), calls=%async_computation.2 | async-start | bytes 1048576 | tf_op jit(solution)/shard_map/all_to_all | solution.py:84
  167.5 58.9 %reduce-scatter.2.cloned.1.call-start = ((), (), s32[]{:S(2)}) async-start(), calls=%async_computation.7 | async-start | bytes 2359296 | tf_op jit(solution)/shard_map/reduce_scatter | solution.py:90
Sparse Core Ops, SparseCore 0:
  9.8 29.8 all-gather.4
  42.1 90.3 all-gather.2
  186.5 27.1 reduce-scatter.1

commit v2 on v1

--- a/solution.py
+++ b/solution.py
@@ -41,7 +41,10 @@
         jnp.arange(slot_total, dtype=jnp.int32)[:, None] == slot_index[None, :]
     ).astype(jnp.bfloat16)
 
-    full_weight = lax.all_gather(out_weight, "seq", axis=1, tiled=True)
+    cols = out_weight.shape[1]
+    heads_n = lax.axis_size("head")
+    w_blocks = lax.all_gather(out_weight, "seq", axis=0, tiled=False)
+    w_grouped = w_blocks.reshape(heads_n, groups // heads_n, out_weight.shape[0], cols)
     qkv = jnp.concatenate([queries, key_rows, value_rows], axis=1)
     qkv_in = lax.all_to_all(select_rows(to_slot, qkv), "seq", 0, 0, tiled=True)
     got_counts = lax.all_to_all(send_counts, "seq", 0, 0, tiled=True)
@@ -85,17 +88,19 @@
         select_rows_t(to_rank, attn_c.reshape(ranks, width)), "seq", 0, 0, tiled=True
     )
     attn_local = select_rows_t(to_slot, attn_back)
-    partial_value = jnp.dot(attn_local, full_weight, preferred_element_type=jnp.float32)
+    partial_value = jnp.einsum(
+        "tr,kjrc->ktjc", attn_local, w_grouped, preferred_element_type=jnp.float32
+    ).reshape(heads_n, tokens, -1)
     rounded_part = lax.optimization_barrier(partial_value.astype(jnp.bfloat16)).astype(jnp.float32)
     layer_out = lax.psum_scatter(
-        rounded_part.astype(jnp.bfloat16), "head", scatter_dimension=1, tiled=True
+        rounded_part.astype(jnp.bfloat16), "head", scatter_dimension=0, tiled=False
     )
 
+    grad_blocks = lax.all_gather(grad_output, "head", axis=0, tiled=False).reshape(
+        heads_n, tokens, groups // heads_n, cols
+    )
     grad_sum = jnp.einsum(
-        "td,wd->tw",
-        lax.all_gather(grad_output, "head", axis=1, tiled=True),
-        full_weight,
-        preferred_element_type=jnp.float32,
+        "ktjc,kjwc->tw", grad_blocks, w_grouped, preferred_element_type=jnp.float32
     )
     grad_attention = grad_sum.astype(jnp.bfloat16)
     grad_in = lax.all_to_all(select_rows(to_slot, grad_attention), "seq", 0, 0, tiled=True)

time: 234 us -> 243 us (1.038)
  local copies, waits for them, and re-layouts: 3.22 us -> 21.4 us
  waiting for transfers between devices: 124 us -> 108 us
  blocking collectives: 36.8 us -> 41.2 us
  matrix products: 19.3 us -> 22.2 us
    reshape x0 -> x3, local copies, waits for them, and re-layouts: none -> 14.8 us  [the longest x1 8.09 us: on_device(): w_blocks.reshape(heads_n, groups // heads_n, out_weight.shape[0], cols)]
    all_gather x2, waiting for transfers between devices: 91.1 us -> 80.7 us  [the longest x1 80.7 us: on_device(): w_blocks = lax.all_gather(out_weight, 'seq', axis=0, tiled=False)]
    all_to_all x1, blocking collectives: 36.8 us -> 41.2 us  [on_device(): lax.all_to_all(select_rows_t(to_rank, grads_c), 'seq', 0, 0, tiled=True)]
    all_to_all x1, starting transfers between devices: 9.14 us -> 5.36 us  [on_device(): lax.all_to_all(select_rows(to_slot, grad_attention), 'seq', 0, 0, tiled=T...]
    all_to_all x1, waiting for transfers between devices: 6.13 us -> 2.57 us  [on_device(): got_counts = lax.all_to_all(send_counts, 'seq', 0, 0, tiled=True)]
    all_to_all x1, starting transfers between devices: 3.97 us -> 7.34 us  [on_device(): qkv_in = lax.all_to_all(select_rows(to_slot, qkv), 'seq', 0, 0, tiled=True)]
  transfers between devices with their start and end apart: 7 -> 7, of which waited for: 4 -> 4; matrix products, arithmetic and copies ran while one was open for 9% -> 17% of each run, Pallas kernels for 0% -> 0%
where the time goes in v2:
time: 243 us
  waiting for transfers between devices  108 us (44%)
  blocking collectives  41.2 us (17%)
  starting transfers between devices  28.8 us (12%)
  matrix products  22.2 us (9%)
  local copies, waits for them, and re-layouts  21.4 us (9%)
  between operations  14 us (6%)
  other arithmetic  6.51 us (3%)
    all_gather x1, waiting for transfers between devices, on_device(): w_blocks = lax.all_gather(out_weight, 'seq', axis=0, tiled=False)  80.7 us
    all_to_all x1, blocking collectives, on_device(): lax.all_to_all(select_rows_t(to_rank, grads_c), 'seq', 0, 0, tiled=True)  41.2 us
    all_to_all x1, waiting for transfers between devices, on_device(): lax.all_to_all(select_rows_t(to_rank, attn_c.reshape(ranks, width)), 'seq...  12.3 us
    all_to_all x1, starting transfers between devices, on_device(): got_counts = lax.all_to_all(send_counts, 'seq', 0, 0, tiled=True)  11.5 us
    all_to_all x1, waiting for transfers between devices, on_device(): lax.all_to_all(select_rows(to_slot, grad_attention), 'seq', 0, 0, tiled=T...  11.4 us
    dot_general x4, matrix products, select_rows(): jnp.dot(onehot, rows, preferred_element_type=jnp.float32).astype(rows.dtype)  9.83 us
    reshape x1, local copies, waits for them, and re-layouts, on_device(): w_blocks.reshape(heads_n, groups // heads_n, out_weight.shape[0], cols)  8.09 us
    all_to_all x1, starting transfers between devices, on_device(): qkv_in = lax.all_to_all(select_rows(to_slot, qkv), 'seq', 0, 0, tiled=True)  7.34 us
  transfers between devices with their start and end apart: 7, of which 4 were waited for; matrix products, arithmetic and copies ran while one was open for 17% of the time, Pallas kernels for 0%

profile of v2, /device:TPU:4, one launch (start us, length us, event | category | flops | bytes accessed | tf_op | source)
XLA Modules:
  0.0 242.5 jit_solution(91056458434291576)
XLA Ops:
  7.2 0.0 copy-start
  7.2 0.0 all-gather.7.cloned.1.call-start
  7.2 0.7 all-gather.7.cloned.1.call-update
  7.9 0.0 all-gather.5.cloned.1.call-start
  8.0 0.7 all-gather.5.cloned.1.call-update
  8.7 0.7 fusion.47
  9.4 0.6 reduce-window.18
  9.9 0.2 slice_reduce_fusion
  10.2 0.9 convert_reduce_fusion
  11.0 0.7 copy.63
  11.7 11.5 %all-to-all-start = ((s32[32,1,1]{2,1,0:T(1,128)}), s32[32,1,1]{2,1,0:T(1,128)S(1)}, u32[]{:S(2)}, u32[]{:S(2)}) async-start(s32[32,1,1]{2,1,0:T(1,128)} %copy.63), calls=%async_computation | async-start | bytes 32768 | tf_op jit(solution)/shard_map/all_to_all | solution.py:50
  23.2 0.0 copy-done
  23.2 0.2 dynamic-slice_reduce_fusion
  23.5 0.6 fusion.58
  24.1 2.5 %broadcast_select_fusion = (s32[256]{0:T(256)S(1)}, s32[256]{0:T(256)S(1)}) fusion(s32[]{:T(128)} %bitcast.9, s32[]{:T(128)} %bitcast.8, s32[]{:T(128)} %bitcast.7, s32[]{:T(128)} %bitcast.6), kind=kLoop, calls=%fused_computation.82 | loop fusion | flops 2816 | bytes 2064 | tf_op jit(solution)/shard_map/jit(_where)/select_n | solution.py:72
  26.6 0.7 multiply_add_fusion
  27.3 2.9 %convolution_convert_fusion.1 = bf16[512,1536]{1,0:T(8,128)(2,1)} fusion(bf16[256,512]{1,0:T(8,128)(2,1)} %param.9, bf16[256,512]{1,0:T(8,128)(2,1)} %param.8, bf16[256,512]{1,0:T(8,128)(2,1)} %param.7, s32[256]{0:T(256)S(1)} %multiply_add_fusion), kind=kOutput, calls=%fused_computation.2 | convolution fusion | flops 405929984 | bytes 2360320 | tf_op jit(solution)/shard_map/dot_general | solution.py:13
  30.2 0.1 fusion.38
  30.3 2.6 %all-to-all-done = s32[32,1,1]{2,1,0:T(1,128)S(1)} async-done(((s32[32,1,1]{2,1,0:T(1,128)}), s32[32,1,1]{2,1,0:T(1,128)S(1)}, u32[]{:S(2)}, u32[]{:S(2)}) %all-to-all-start) | async-done | bytes 160 | tf_op jit(solution)/shard_map/all_to_all | solution.py:50
  32.9 7.3 %all-to-all-start.1 = ((bf16[32,16,1536]{2,1,0:T(8,128)(2,1)}), bf16[32,16,1536]{2,1,0:T(8,128)(2,1)}, u32[]{:S(2)}, u32[]{:S(2)}) async-start(bf16[32,16,1536]{2,1,0:T(8,128)(2,1)} %bitcast.4), calls=%async_computation.1 | async-start | bytes 3145728 | tf_op jit(solution)/shard_map/all_to_all | solution.py:49
  40.3 0.1 reduce-window.20
  40.3 0.1 reduce.1
  40.4 0.7 reduce.2
  41.1 0.1 iota_add_fusion
  41.2 0.1 add.47
  41.3 2.6 %reshape.242 = bf16[8,256,4,128]{3,2,1,0:T(4,128)(2,1)S(1)} reshape(bf16[2048,512]{1,0:T(8,128)(2,1)} %all-gather.7.cloned.1.call-done) | data formatting | bytes 4194304 | tf_op jit(solution)/shard_map/reshape | solution.py:99
  43.8 4.1 %copy.86 = bf16[8,256,4,128]{1,0,2,3:T(8,128)(2,1)} copy(bf16[8,256,4,128]{3,2,1,0:T(4,128)(2,1)S(1)} %reshape.242) | data formatting | bytes 4194304 | tf_op jit(solution)/shard_map/reshape | solution.py:99
  47.9 80.7 %all-gather.5.cloned.1.call-done = bf16[16384,128]{1,0:T(8,128)(2,1)} async-done(((bf16[512,128]{1,0:T(8,128)(2,1)}), bf16[16384,128]{1,0:T(8,128)(2,1)}) %all-gather.5.cloned.1.call-update) | async-done | bytes 4194320 | tf_op jit(solution)/shard_map/all_gather | solution.py:46
  128.6 8.1 %copy.87 = bf16[8,4,512,128]{2,0,1,3:T(8,128)(2,1)} copy(bf16[8,4,512,128]{3,2,1,0:T(8,128)(2,1)} %bitcast.92) | data formatting | bytes 8388608 | tf_op jit(solution)/shard_map/reshape | solution.py:47
  136.7 4.6 %convolution_convert_fusion.6 = bf16[512,512]{1,0:T(8,128)(2,1)} fusion(bf16[8,256,4,128]{1,0,2,3:T(8,128)(2,1)S(1)} %copy-done.1, bf16[8,4,512,128]{2,0,1,3:T(8,128)(2,1)} %copy.87, s32[256]{0:T(256)S(1)} %multiply_add_fusion), kind=kOutput, calls=%fused_computation.14 | convolution fusion | flops 1208483840 | bytes 6816768 | tf_op jit(solution)/shard_map/dot_general | solution.py:13
  141.3 0.0 all-to-all-done.1
  141.4 5.4 %all-to-all-start.3 = ((bf16[32,16,512]{2,1,0:T(8,128)(2,1)}), bf16[32,16,512]{2,1,0:T(8,128)(2,1)S(1)}, u32[]{:S(2)}, u32[]{:S(2)}) async-start(bf16[32,16,512]{2,1,0:T(8,128)(2,1)} %bitcast.22), calls=%async_computation.4 | async-start | bytes 1048576 | tf_op jit(solution)/shard_map/all_to_all | solution.py:106
  146.7 0.1 iota_compare_fusion.10
  146.8 0.1 lt.24
  146.9 2.0 convolution_convert_fusion.3
  148.9 0.1 fusion.57
  148.9 0.1 copy.98
  149.1 0.0 copy-start.2
  149.1 0.1 copy.99
  149.2 1.5 fusion.59
  150.7 11.4 %all-to-all-done.3 = bf16[32,16,512]{2,1,0:T(8,128)(2,1)S(1)} async-done(((bf16[32,16,512]{2,1,0:T(8,128)(2,1)}), bf16[32,16,512]{2,1,0:T(8,128)(2,1)S(1)}, u32[]{:S(2)}, u32[]{:S(2)}) %all-to-all-start.3) | async-done | bytes 524320 | tf_op jit(solution)/shard_map/all_to_all | solution.py:106
  162.1 0.3 convolution_convert_fusion.8
  162.5 0.1 copy.74
  162.6 0.0 copy-start.4
  162.6 0.8 multiply_reduce_fusion
  163.4 1.2 convolution_convert_fusion.5
  164.6 4.4 %all-to-all-start.2 = ((bf16[32,16,512]{2,1,0:T(8,128)(2,1)}), bf16[32,16,512]{2,1,0:T(8,128)(2,1)S(1)}, u32[]{:S(2)}, u32[]{:S(2)}) async-start(bf16[32,16,512]{2,1,0:T(8,128)(2,1)} %bitcast.12), calls=%async_computation.2 | async-start | bytes 1048576 | tf_op jit(solution)/shard_map/all_to_all | solution.py:87
  168.9 0.2 reduce-scatter.2.cloned.1.call-start
  169.2 1.5 fusion.5
  170.7 0.0 copy-done.2
  170.7 1.0 fusion.7
  171.7 12.3 %all-to-all-done.2 = bf16[32,16,512]{2,1,0:T(8,128)(2,1)S(1)} async-done(((bf16[32,16,512]{2,1,0:T(8,128)(2,1)}), bf16[32,16,512]{2,1,0:T(8,128)(2,1)S(1)}, u32[]{:S(2)}, u32[]{:S(2)}) %all-to-all-start.2) | async-done | bytes 524320 | tf_op jit(solution)/shard_map/all_to_all | solution.py:87
  184.0 4.1 %convolution_convert_fusion.4 = bf16[256,8,4,128]{0,3,2,1:T(8,128)(2,1)S(1)} fusion(bf16[8,4,512,128]{3,2,1,0:T(8,128)(2,1)} %bitcast.93, bf16[512,512]{1,0:T(8,128)(2,1)S(1)} %bitcast.96, s32[256]{0:T(256)S(1)} %multiply_add_fusion), kind=kOutput, calls=%fused_computation.5 | convolution fusion | flops 1209270272 | bytes 6816768 | tf_op jit(solution)/shard_map/tr,kjrc->ktjc/dot_general | solution.py:91
  188.1 2.4 copy.70
  190.5 0.0 reduce-scatter.2.cloned.1.call-update
  190.5 0.9 copy-done.3
  191.4 0.1 copy-done.5
  191.5 0.8 convolution_convert_fusion.7
  192.3 0.2 fusion.6
  192.6 0.0 copy-done.6
  192.6 0.6 convolution_convert_fusion
  193.2 41.2 %all_to_all.57 = bf16[32,16,1536]{2,1,0:T(8,128)(2,1)S(1)} all-to-all(bf16[32,16,1536]{2,1,0:T(8,128)(2,1)S(1)} %bitcast.97), channel_id=1, replica_groups=mesh['seq'=32,'head'=8] {'seq'}, dimensions={0} | all-to-all | bytes 3145728 | tf_op jit(solution)/shard_map/all_to_all | solution.py:129
  234.5 0.6 convolution_convert_fusion.2
  235.1 0.9 fusion.56
  (12 shorter events, 0.1 us)
Async XLA Ops:
  7.2 16.1 %copy-start = (s32[32,2,2]{0,2,1:T(2,128)S(1)}, s32[32,2,2]{0,2,1:T(2,128)}, u32[]{:S(2)}) copy-start(s32[32,2,2]{0,2,1:T(2,128)} %param.13) | copy-start | bytes 1540
  7.2 34.1 %all-gather.7.cloned.1.call-start = ((), (), s32[]{:S(2)}) async-start(), calls=%async_computation.8 | async-start | bytes 2359296 | tf_op jit(solution)/shard_map/all_gather | solution.py:99
  7.9 120.7 %all-gather.5.cloned.1.call-start = ((), (), s32[]{:S(2)}) async-start(), calls=%async_computation.7 | async-start | bytes 4325376 | tf_op jit(solution)/shard_map/all_gather | solution.py:46
  11.7 21.2 %all-to-all-start = ((s32[32,1,1]{2,1,0:T(1,128)}), s32[32,1,1]{2,1,0:T(1,128)S(1)}, u32[]{:S(2)}, u32[]{:S(2)}) async-start(s32[32,1,1]{2,1,0:T(1,128)} %copy.63), calls=%async_computation | async-start | bytes 32768 | tf_op jit(solution)/shard_map/all_to_all | solution.py:50
  32.9 108.4 %all-to-all-start.1 = ((bf16[32,16,1536]{2,1,0:T(8,128)(2,1)}), bf16[32,16,1536]{2,1,0:T(8,128)(2,1)}, u32[]{:S(2)}, u32[]{:S(2)}) async-start(bf16[32,16,1536]{2,1,0:T(8,128)(2,1)} %bitcast.4), calls=%async_computation.1 | async-start | bytes 3145728 | tf_op jit(solution)/shard_map/all_to_all | solution.py:49
  128.6 8.1 %copy-start.1 = (bf16[8,256,4,128]{1,0,2,3:T(8,128)(2,1)S(1)}, bf16[8,256,4,128]{1,0,2,3:T(8,128)(2,1)}, u32[]{:S(2)}) copy-start(bf16[8,256,4,128]{1,0,2,3:T(8,128)(2,1)} %copy.86) | copy-start | bytes 6291460
  141.4 20.8 %all-to-all-start.3 = ((bf16[32,16,512]{2,1,0:T(8,128)(2,1)}), bf16[32,16,512]{2,1,0:T(8,128)(2,1)S(1)}, u32[]{:S(2)}, u32[]{:S(2)}) async-start(bf16[32,16,512]{2,1,0:T(8,128)(2,1)} %bitcast.22), calls=%async_computation.4 | async-start | bytes 1048576 | tf_op jit(solution)/shard_map/all_to_all | solution.py:106
  149.1 21.6 %copy-start.2 = (bf16[256,512]{0,1:T(8,128)(2,1)}, bf16[256,512]{0,1:T(8,128)(2,1)S(1)}, u32[]{:S(2)}) copy-start(bf16[256,512]{0,1:T(8,128)(2,1)S(1)} %copy.98) | copy-start | bytes 786436
  162.6 6.6 %copy-start.4 = (bf16[256,512]{0,1:T(8,128)(2,1)}, bf16[256,512]{0,1:T(8,128)(2,1)S(1)}, u32[]{:S(2)}) copy-start(bf16[256,512]{0,1:T(8,128)(2,1)S(1)} %copy.74) | copy-start | bytes 786436
  164.6 19.4 %all-to-all-start.2 = ((bf16[32,16,512]{2,1,0:T(8,128)(2,1)}), bf16[32,16,512]{2,1,0:T(8,128)(2,1)S(1)}, u32[]{:S(2)}, u32[]{:S(2)}) async-start(bf16[32,16,512]{2,1,0:T(8,128)(2,1)} %bitcast.12), calls=%async_computation.2 | async-start | bytes 1048576 | tf_op jit(solution)/shard_map/all_to_all | solution.py:87
  168.9 67.1 %reduce-scatter.2.cloned.1.call-start = ((), (), s32[]{:S(2)}) async-start(), calls=%async_computation.6 | async-start | bytes 2359296 | tf_op jit(solution)/shard_map/reduce_scatter | solution.py:95
  190.5 0.9 copy-start.3
  190.5 1.0 copy-start.5
  191.5 1.0 copy-start.6
Sparse Core Ops, SparseCore 0:
  9.8 29.8 all-gather.6
  42.3 86.2 all-gather.4
  190.6 27.3 reduce-scatter.1

commit v3 on v1

--- a/solution.py
+++ b/solution.py
@@ -17,6 +17,33 @@
     return lax.dot_general(
         onehot, rows, (((0,), (0,)), ((), ())), preferred_element_type=jnp.float32
     ).astype(rows.dtype)
+
+
+def ring_gather_cols(block, axis_name, ny, nz):
+    index = lax.axis_index(axis_name)
+    y = index % ny
+    z = index // ny
+    n = ny * nz
+    cols = block.shape[1]
+
+    def perm(dy, dz):
+        return [(i, ((i // ny + dz) % nz) * ny + (i % ny + dy) % ny) for i in range(n)]
+
+    def ring(piece, pos, count, step_perm, width, total):
+        out = jnp.zeros((piece.shape[0], total), piece.dtype)
+        out = lax.dynamic_update_slice(out, piece, (0, pos * width))
+        fwd = piece
+        bwd = piece
+        for step in range(1, count // 2 + 1):
+            fwd = lax.ppermute(fwd, axis_name, step_perm(1))
+            out = lax.dynamic_update_slice(out, fwd, (0, ((pos - step) % count) * width))
+            if count - step != step:
+                bwd = lax.ppermute(bwd, axis_name, step_perm(-1))
+                out = lax.dynamic_update_slice(out, bwd, (0, ((pos + step) % count) * width))
+        return out
+
+    row = ring(block, y, ny, lambda d: perm(d, 0), cols, ny * cols)
+    return ring(row, z, nz, lambda d: perm(0, d), ny * cols, n * cols)
 
 
 def on_device(queries, key_rows, value_rows, out_weight, grad_output, cluster_ids, block_pattern):
@@ -41,7 +68,8 @@
         jnp.arange(slot_total, dtype=jnp.int32)[:, None] == slot_index[None, :]
     ).astype(jnp.bfloat16)
 
-    full_weight = lax.all_gather(out_weight, "seq", axis=1, tiled=True)
+    ring_y = 4 if groups % 4 == 0 else 1
+    full_weight = ring_gather_cols(out_weight, "seq", ring_y, groups // ring_y)
     qkv = jnp.concatenate([queries, key_rows, value_rows], axis=1)
     qkv_in = lax.all_to_all(select_rows(to_slot, qkv), "seq", 0, 0, tiled=True)
     got_counts = lax.all_to_all(send_counts, "seq", 0, 0, tiled=True)
@@ -84,6 +112,7 @@
     attn_back = lax.all_to_all(
         select_rows_t(to_rank, attn_c.reshape(ranks, width)), "seq", 0, 0, tiled=True
     )
+    attn_back, full_weight = lax.optimization_barrier((attn_back, full_weight))
     attn_local = select_rows_t(to_slot, attn_back)
     partial_value = jnp.dot(attn_local, full_weight, preferred_element_type=jnp.float32)
     rounded_part = lax.optimization_barrier(partial_value.astype(jnp.bfloat16)).astype(jnp.float32)

time: 234 us -> 221 us (0.944)
  waiting for transfers between devices: 124 us -> 71.1 us
  starting transfers between devices: 29.1 us -> 47.8 us
  local copies, waits for them, and re-layouts: 3.22 us -> 16.1 us
  blocking collectives: 36.8 us -> 43.6 us
    all_gather x1 -> x0, waiting for transfers between devices: 91.1 us -> none  [on_device(): full_weight = lax.all_gather(out_weight, 'seq', axis=1, tiled=True)]
    ppermute x0 -> x10, waiting for transfers between devices: none -> 53.1 us  [the longest x6 42.3 us: ring(): fwd = lax.ppermute(fwd, axis_name, step_perm(1))]
    ppermute x0 -> x10, starting transfers between devices: none -> 14.9 us  [the longest x4 10.1 us: ring(): bwd = lax.ppermute(bwd, axis_name, step_perm(-1))]
    all_to_all x1, waiting for transfers between devices: 13.2 us -> 0.01 us  [on_device(): lax.all_to_all(select_rows_t(to_rank, attn_c.reshape(ranks, width)), 'seq...]
    dynamic_update_slice x0 -> x12, local copies, waits for them, and re-layouts: none -> 10.3 us  [the longest x6 5.69 us: ring(): out = lax.dynamic_update_slice(out, fwd, (0, (pos - step) % count * width))]
    all_to_all x1, blocking collectives: 36.8 us -> 43.6 us  [on_device(): lax.all_to_all(select_rows_t(to_rank, grads_c), 'seq', 0, 0, tiled=True)]
    all_to_all x1, starting transfers between devices: 4.37 us -> 9.27 us  [on_device(): lax.all_to_all(select_rows_t(to_rank, attn_c.reshape(ranks, width)), 'seq...]
    broadcast_in_dim x0 -> x2, local copies, waits for them, and re-layouts: none -> 2.47 us  [ring(): out = jnp.zeros((piece.shape[0], total), piece.dtype)]
  transfers between devices with their start and end apart: 7 -> 16, of which waited for: 4 -> 9; matrix products, arithmetic and copies ran while one was open for 9% -> 16% of each run, Pallas kernels for 0% -> 0%
where the time goes in v3:
time: 221 us
  waiting for transfers between devices  71.1 us (32%)
  starting transfers between devices  47.8 us (22%)
  blocking collectives  43.6 us (20%)
  matrix products  20.6 us (9%)
  local copies, waits for them, and re-layouts  16.1 us (7%)
  between operations  14.6 us (7%)
  other arithmetic  6.71 us (3%)
    all_to_all x1, blocking collectives, on_device(): lax.all_to_all(select_rows_t(to_rank, grads_c), 'seq', 0, 0, tiled=True)  43.6 us
    ppermute x6, waiting for transfers between devices, ring(): fwd = lax.ppermute(fwd, axis_name, step_perm(1))  42.3 us
    all_to_all x1, waiting for transfers between devices, on_device(): lax.all_to_all(select_rows(to_slot, grad_attention), 'seq', 0, 0, tiled=T...  11.8 us
    all_to_all x1, starting transfers between devices, on_device(): got_counts = lax.all_to_all(send_counts, 'seq', 0, 0, tiled=True)  11.5 us
    ppermute x4, waiting for transfers between devices, ring(): bwd = lax.ppermute(bwd, axis_name, step_perm(-1))  10.9 us
    ppermute x4, starting transfers between devices, ring(): bwd = lax.ppermute(bwd, axis_name, step_perm(-1))  10.1 us
    all_to_all x1, starting transfers between devices, on_device(): lax.all_to_all(select_rows_t(to_rank, attn_c.reshape(ranks, width)), 'seq...  9.27 us
    dot_general x4, matrix products, select_rows(): jnp.dot(onehot, rows, preferred_element_type=jnp.float32).astype(rows.dtype)  9.13 us
  transfers between devices with their start and end apart: 16, of which 9 were waited for; matrix products, arithmetic and copies ran while one was open for 16% of the time, Pallas kernels for 0%

profile of v3, /device:TPU:4, one launch (start us, length us, event | category | flops | bytes accessed | tf_op | source)
XLA Modules:
  0.0 220.5 jit_solution(10499551500836500329)
XLA Ops:
  7.2 0.7 fusion.45
  7.9 0.6 reduce-window.18
  8.5 0.2 slice_reduce_fusion
  8.7 0.9 convert_reduce_fusion
  9.6 0.7 copy.57
  10.3 11.5 %all-to-all-start = ((s32[32,1,1]{2,1,0:T(1,128)}), s32[32,1,1]{2,1,0:T(1,128)S(1)}, u32[]{:S(2)}, u32[]{:S(2)}) async-start(s32[32,1,1]{2,1,0:T(1,128)} %copy.57), calls=%async_computation | async-start | bytes 32768 | tf_op jit(solution)/shard_map/all_to_all | solution.py:75
  21.8 0.7 multiply_add_fusion
  22.5 2.8 %convolution_convert_fusion.2 = bf16[512,1536]{1,0:T(8,128)(2,1)} fusion(bf16[256,512]{1,0:T(8,128)(2,1)} %param.9, bf16[256,512]{1,0:T(8,128)(2,1)} %param.8, bf16[256,512]{1,0:T(8,128)(2,1)} %param.7, s32[256]{0:T(256)S(1)} %multiply_add_fusion), kind=kOutput, calls=%fused_computation.3 | convolution fusion | flops 405929984 | bytes 2360320 | tf_op jit(solution)/shard_map/dot_general | solution.py:13
  25.3 6.2 %all-to-all-done = s32[32,1,1]{2,1,0:T(1,128)S(1)} async-done(((s32[32,1,1]{2,1,0:T(1,128)}), s32[32,1,1]{2,1,0:T(1,128)S(1)}, u32[]{:S(2)}, u32[]{:S(2)}) %all-to-all-start) | async-done | bytes 160 | tf_op jit(solution)/shard_map/all_to_all | solution.py:75
  31.5 4.0 %all-to-all-start.1 = ((bf16[32,16,1536]{2,1,0:T(8,128)(2,1)}), bf16[32,16,1536]{2,1,0:T(8,128)(2,1)S(1)}, u32[]{:S(2)}, u32[]{:S(2)}) async-start(bf16[32,16,1536]{2,1,0:T(8,128)(2,1)} %bitcast.4), calls=%async_computation.1 | async-start | bytes 3145728 | tf_op jit(solution)/shard_map/all_to_all | solution.py:74
  35.5 1.8 collective-permute-start
  37.3 1.6 collective-permute-start.1
  39.0 4.6 %collective-permute-done = bf16[512,128]{1,0:T(8,128)(2,1)S(1)} collective-permute-done((bf16[512,128]{1,0:T(8,128)(2,1)S(1)}, bf16[512,128]{1,0:T(8,128)(2,1)S(1)}, u32[]{:S(2)}, u32[]{:S(2)}) %collective-permute-start) | collective-permute-done | bytes 131104 | tf_op jit(solution)/shard_map/ppermute | solution.py:38
  43.6 1.0 collective-permute-start.2
  44.6 1.8 collective-permute-done.1
  46.4 4.1 %collective-permute-done.2 = bf16[512,128]{1,0:T(8,128)(2,1)S(1)} collective-permute-done((bf16[512,128]{1,0:T(8,128)(2,1)S(1)}, bf16[512,128]{1,0:T(8,128)(2,1)S(1)}, u32[]{:S(2)}, u32[]{:S(2)}) %collective-permute-start.2) | collective-permute-done | bytes 131104 | tf_op jit(solution)/shard_map/ppermute | solution.py:38
  50.5 2.0 collective-permute-start.3
  52.5 0.2 fusion.46
  52.8 0.6 fusion.57
  53.4 2.6 %broadcast_select_fusion = (s32[256]{0:T(256)S(1)}, s32[256]{0:T(256)S(1)}) fusion(s32[]{:T(128)} %bitcast.9, s32[]{:T(128)} %bitcast.8, s32[]{:T(128)} %bitcast.7, s32[]{:T(128)} %bitcast.6), kind=kLoop, calls=%fused_computation.93 | loop fusion | flops 2816 | bytes 2064 | tf_op jit(solution)/shard_map/jit(_where)/select_n | solution.py:97
  56.0 2.4 %collective-permute-start.4 = (bf16[512,512]{1,0:T(8,128)(2,1)S(1)}, bf16[512,512]{1,0:T(8,128)(2,1)S(1)}, u32[]{:S(2)}, u32[]{:S(2)}) collective-permute-start(bf16[512,512]{1,0:T(8,128)(2,1)S(1)} %constant_dynamic-update-slice_fusion.8), channel_id=1, source_target_pairs={{0,224},{8,232},{16,240},{24,248},{32,0},{40,8},{48,16},{56,24},{6... | collective-permute-start | bytes 1572872 | tf_op jit(solution)/shard_map/ppermute | solution.py:41
  58.3 24.5 %collective-permute-done.3 = bf16[512,512]{1,0:T(8,128)(2,1)S(1)} collective-permute-done((bf16[512,512]{1,0:T(8,128)(2,1)S(1)}, bf16[512,512]{1,0:T(8,128)(2,1)S(1)}, u32[]{:S(2)}, u32[]{:S(2)}) %collective-permute-start.3) | collective-permute-done | bytes 524320 | tf_op jit(solution)/shard_map/ppermute | solution.py:38
  82.8 0.1 fusion.36
  83.0 0.1 reduce.1
  83.1 0.7 reduce.2
  83.9 0.1 add.136
  83.9 0.1 iota_compare_fusion.10
  84.0 0.1 lt.106
  84.1 3.3 %collective-permute-start.6 = (bf16[512,512]{1,0:T(8,128)(2,1)S(1)}, bf16[512,512]{1,0:T(8,128)(2,1)}, u32[]{:S(2)}, u32[]{:S(2)}) collective-permute-start(bf16[512,512]{1,0:T(8,128)(2,1)S(1)} %collective-permute-done.4), channel_id=1, source_target_pairs={{0,224},{8,232},{16,240},{24,248},{32,0},{40,8},{48,16},{56,24},{6... | collective-permute-start | bytes 1572872 | tf_op jit(solution)/shard_map/ppermute | solution.py:41
  87.4 8.8 %collective-permute-done.5 = bf16[512,512]{1,0:T(8,128)(2,1)} collective-permute-done((bf16[512,512]{1,0:T(8,128)(2,1)S(1)}, bf16[512,512]{1,0:T(8,128)(2,1)}, u32[]{:S(2)}, u32[]{:S(2)}) %collective-permute-start.5) | collective-permute-done | bytes 524320 | tf_op jit(solution)/shard_map/ppermute | solution.py:38
  96.3 0.6 convolution_convert_fusion.4
  96.9 0.1 copy.78
  97.1 0.1 copy.79
  97.2 1.5 fusion.58
  98.7 0.8 convolution_convert_fusion.11
  99.5 1.2 convolution_convert_fusion.5
  100.7 9.3 %all-to-all-start.2 = ((bf16[32,16,512]{2,1,0:T(8,128)(2,1)}), bf16[32,16,512]{2,1,0:T(8,128)(2,1)S(1)}, u32[]{:S(2)}, u32[]{:S(2)}) async-start(bf16[32,16,512]{2,1,0:T(8,128)(2,1)} %bitcast.12), calls=%async_computation.2 | async-start | bytes 1048576 | tf_op jit(solution)/shard_map/all_to_all | solution.py:112
  110.1 2.4 %broadcast_in_dim.82 = bf16[512,4096]{1,0:T(8,128)(2,1)} broadcast(bf16[]{:T(256)} %constant.130.clone.1), dimensions={} | broadcast | bytes 4194306 | tf_op jit(solution)/shard_map/broadcast_in_dim | solution.py:33
  112.6 0.9 constant_dynamic-update-slice_fusion.7
  113.4 2.9 %collective-permute-start.8 = (bf16[512,512]{1,0:T(8,128)(2,1)}, bf16[512,512]{1,0:T(8,128)(2,1)S(1)}, u32[]{:S(2)}, u32[]{:S(2)}) collective-permute-start(bf16[512,512]{1,0:T(8,128)(2,1)} %collective-permute-done.6), channel_id=1, source_target_pairs={{0,224},{8,232},{16,240},{24,248},{32,0},{40,8},{48,16},{56,24},{6... | collective-permute-start | bytes 1572872 | tf_op jit(solution)/shard_map/ppermute | solution.py:41
  116.4 0.9 constant_dynamic-update-slice_fusion.6
  117.2 0.9 constant_dynamic-update-slice_fusion.5
  118.1 1.9 constant_dynamic-update-slice_fusion.4
  120.0 1.9 constant_dynamic-update-slice_fusion.3
  121.9 1.9 constant_dynamic-update-slice_fusion.2
  123.8 9.1 %collective-permute-done.8 = bf16[512,512]{1,0:T(8,128)(2,1)S(1)} collective-permute-done((bf16[512,512]{1,0:T(8,128)(2,1)}, bf16[512,512]{1,0:T(8,128)(2,1)S(1)}, u32[]{:S(2)}, u32[]{:S(2)}) %collective-permute-start.8) | collective-permute-done | bytes 524320 | tf_op jit(solution)/shard_map/ppermute | solution.py:41
  132.9 0.9 constant_dynamic-update-slice_fusion.1
  133.8 0.4 collective-permute-done.9
  134.2 0.9 constant_dynamic-update-slice_fusion
  135.1 5.4 %convolution_convert_fusion.6 = bf16[512,512]{1,0:T(8,128)(2,1)} fusion(bf16[512,4096]{1,0:T(8,128)(2,1)} %constant_dynamic-update-slice_fusion, bf16[256,4096]{1,0:T(8,128)(2,1)} %all-gather.2.cloned.1.call-done, s32[256]{0:T(256)S(1)} %multiply_add_fusion), kind=kOutput, calls=%fused_computation.14 | convolution fusion | flops 1208483840 | bytes 6816768 | tf_op jit(solution)/shard_map/dot_general | solution.py:13
  140.5 8.1 %all-to-all-start.3 = ((bf16[32,16,512]{2,1,0:T(8,128)(2,1)}), bf16[32,16,512]{2,1,0:T(8,128)(2,1)S(1)}, u32[]{:S(2)}, u32[]{:S(2)}) async-start(bf16[32,16,512]{2,1,0:T(8,128)(2,1)} %bitcast.14), calls=%async_computation.4 | async-start | bytes 1048576 | tf_op jit(solution)/shard_map/all_to_all | solution.py:130
  148.7 5.1 %convolution_convert_fusion = bf16[256,4096]{1,0:T(8,128)(2,1)} fusion(bf16[512,4096]{1,0:T(8,128)(2,1)} %constant_dynamic-update-slice_fusion, bf16[512,512]{1,0:T(8,128)(2,1)S(1)} %bitcast.73, s32[256]{0:T(256)S(1)} %multiply_add_fusion), kind=kOutput, calls=%fused_computation.1 | convolution fusion | flops 1209270272 | bytes 6816768 | tf_op jit(solution)/shard_map/dot_general | solution.py:117
  153.9 11.8 %all-to-all-done.3 = bf16[32,16,512]{2,1,0:T(8,128)(2,1)S(1)} async-done(((bf16[32,16,512]{2,1,0:T(8,128)(2,1)}), bf16[32,16,512]{2,1,0:T(8,128)(2,1)S(1)}, u32[]{:S(2)}, u32[]{:S(2)}) %all-to-all-start.3) | async-done | bytes 524320 | tf_op jit(solution)/shard_map/all_to_all | solution.py:130
  165.7 0.3 convolution_convert_fusion.8
  166.0 0.1 copy.63
  166.1 0.1 multiply_reduce_fusion
  166.2 0.3 fusion.5
  166.5 0.2 fusion.6
  166.8 0.8 convolution_convert_fusion.7
  167.6 0.3 fusion.7
  167.9 0.6 convolution_convert_fusion.1
  168.5 43.6 %all_to_all.57 = bf16[32,16,1536]{2,1,0:T(8,128)(2,1)S(1)} all-to-all(bf16[32,16,1536]{2,1,0:T(8,128)(2,1)S(1)} %bitcast.74), channel_id=1, replica_groups=mesh['seq'=32,'head'=8] {'seq'}, dimensions={0} | all-to-all | bytes 3145728 | tf_op jit(solution)/shard_map/all_to_all | solution.py:153
  212.2 0.6 convolution_convert_fusion.3
  212.8 0.9 fusion.55
  (36 shorter events, 0.6 us)
Async XLA Ops:
  7.2 45.4 %copy-start = (s32[32,2,2]{0,2,1:T(2,128)S(1)}, s32[32,2,2]{0,2,1:T(2,128)}, u32[]{:S(2)}) copy-start(s32[32,2,2]{0,2,1:T(2,128)} %param.13) | copy-start | bytes 1540
  7.2 28.3 %copy-start.3 = (bf16[512,128]{1,0:T(8,128)(2,1)S(1)}, bf16[512,128]{1,0:T(8,128)(2,1)}, u32[]{:S(2)}) copy-start(bf16[512,128]{1,0:T(8,128)(2,1)} %param.10) | copy-start | bytes 393220
  10.3 21.2 %all-to-all-start = ((s32[32,1,1]{2,1,0:T(1,128)}), s32[32,1,1]{2,1,0:T(1,128)S(1)}, u32[]{:S(2)}, u32[]{:S(2)}) async-start(s32[32,1,1]{2,1,0:T(1,128)} %copy.57), calls=%async_computation | async-start | bytes 32768 | tf_op jit(solution)/shard_map/all_to_all | solution.py:75
  31.5 64.8 %all-to-all-start.1 = ((bf16[32,16,1536]{2,1,0:T(8,128)(2,1)}), bf16[32,16,1536]{2,1,0:T(8,128)(2,1)S(1)}, u32[]{:S(2)}, u32[]{:S(2)}) async-start(bf16[32,16,1536]{2,1,0:T(8,128)(2,1)} %bitcast.4), calls=%async_computation.1 | async-start | bytes 3145728 | tf_op jit(solution)/shard_map/all_to_all | solution.py:74
  35.5 99.7 %all-gather.2.cloned.1.call-start = ((), (), s32[]{:S(2)}) async-start(), calls=%async_computation.7 | async-start | bytes 2359296 | tf_op jit(solution)/shard_map/all_gather | solution.py:125
  35.5 8.1 %collective-permute-start = (bf16[512,128]{1,0:T(8,128)(2,1)S(1)}, bf16[512,128]{1,0:T(8,128)(2,1)S(1)}, u32[]{:S(2)}, u32[]{:S(2)}) collective-permute-start(bf16[512,128]{1,0:T(8,128)(2,1)S(1)} %copy-done.3), channel_id=1, source_target_pairs={{0,8},{8,16},{16,24},{24,0},{32,40},{40,48},{48,56},{56,32},{64,72... | collective-permute-start | bytes 393224 | tf_op jit(solution)/shard_map/ppermute | solution.py:38
  37.3 9.1 %collective-permute-start.1 = (bf16[512,128]{1,0:T(8,128)(2,1)S(1)}, bf16[512,128]{1,0:T(8,128)(2,1)S(1)}, u32[]{:S(2)}, u32[]{:S(2)}) collective-permute-start(bf16[512,128]{1,0:T(8,128)(2,1)S(1)} %copy-done.3), channel_id=1, source_target_pairs={{0,24},{8,0},{16,8},{24,16},{32,56},{40,32},{48,40},{56,48},{64,88... | collective-permute-start | bytes 393224 | tf_op jit(solution)/shard_map/ppermute | solution.py:41
  43.6 6.9 %collective-permute-start.2 = (bf16[512,128]{1,0:T(8,128)(2,1)S(1)}, bf16[512,128]{1,0:T(8,128)(2,1)S(1)}, u32[]{:S(2)}, u32[]{:S(2)}) collective-permute-start(bf16[512,128]{1,0:T(8,128)(2,1)S(1)} %collective-permute-done), channel_id=1, source_target_pairs={{0,8},{8,16},{16,24},{24,0},{32,40},{40,48},{48,56},{56,32},{64,72... | collective-permute-start | bytes 393224 | tf_op jit(solution)/shard_map/ppermute | solution.py:38
  50.5 32.3 %collective-permute-start.3 = (bf16[512,512]{1,0:T(8,128)(2,1)S(1)}, bf16[512,512]{1,0:T(8,128)(2,1)S(1)}, u32[]{:S(2)}, u32[]{:S(2)}) collective-permute-start(bf16[512,512]{1,0:T(8,128)(2,1)S(1)} %constant_dynamic-update-slice_fusion.8), channel_id=1, source_target_pairs={{0,32},{8,40},{16,48},{24,56},{32,64},{40,72},{48,80},{56,88},{64,... | collective-permute-start | bytes 1572872 | tf_op jit(solution)/shard_map/ppermute | solution.py:38
  56.0 28.1 %collective-permute-start.4 = (bf16[512,512]{1,0:T(8,128)(2,1)S(1)}, bf16[512,512]{1,0:T(8,128)(2,1)S(1)}, u32[]{:S(2)}, u32[]{:S(2)}) collective-permute-start(bf16[512,512]{1,0:T(8,128)(2,1)S(1)} %constant_dynamic-update-slice_fusion.8), channel_id=1, source_target_pairs={{0,224},{8,232},{16,240},{24,248},{32,0},{40,8},{48,16},{56,24},{6... | collective-permute-start | bytes 1572872 | tf_op jit(solution)/shard_map/ppermute | solution.py:41
  82.8 13.5 %collective-permute-start.5 = (bf16[512,512]{1,0:T(8,128)(2,1)S(1)}, bf16[512,512]{1,0:T(8,128)(2,1)}, u32[]{:S(2)}, u32[]{:S(2)}) collective-permute-start(bf16[512,512]{1,0:T(8,128)(2,1)S(1)} %collective-permute-done.3), channel_id=1, source_target_pairs={{0,32},{8,40},{16,48},{24,56},{32,64},{40,72},{48,80},{56,88},{64,... | collective-permute-start | bytes 1572872 | tf_op jit(solution)/shard_map/ppermute | solution.py:38
  84.1 29.3 %collective-permute-start.6 = (bf16[512,512]{1,0:T(8,128)(2,1)S(1)}, bf16[512,512]{1,0:T(8,128)(2,1)}, u32[]{:S(2)}, u32[]{:S(2)}) collective-permute-start(bf16[512,512]{1,0:T(8,128)(2,1)S(1)} %collective-permute-done.4), channel_id=1, source_target_pairs={{0,224},{8,232},{16,240},{24,248},{32,0},{40,8},{48,16},{56,24},{6... | collective-permute-start | bytes 1572872 | tf_op jit(solution)/shard_map/ppermute | solution.py:41
  96.3 21.0 %collective-permute-start.7 = (bf16[512,512]{1,0:T(8,128)(2,1)}, bf16[512,512]{1,0:T(8,128)(2,1)}, u32[]{:S(2)}, u32[]{:S(2)}) collective-permute-start(bf16[512,512]{1,0:T(8,128)(2,1)} %collective-permute-done.5), channel_id=1, source_target_pairs={{0,32},{8,40},{16,48},{24,56},{32,64},{40,72},{48,80},{56,88},{64,... | collective-permute-start | bytes 1572872 | tf_op jit(solution)/shard_map/ppermute | solution.py:38
  96.9 2.6 %copy-start.1 = (bf16[32,4,8,128]{3,2,1,0:T(8,128)(2,1)}, bf16[32,4,8,128]{3,2,1,0:T(8,128)(2,1)S(1)}, u32[]{:S(2)}) copy-start(bf16[32,4,8,128]{3,2,1,0:T(8,128)(2,1)S(1)} %get-tuple-element.15) | copy-start | bytes 786436
  100.7 34.4 %all-to-all-start.2 = ((bf16[32,16,512]{2,1,0:T(8,128)(2,1)}), bf16[32,16,512]{2,1,0:T(8,128)(2,1)S(1)}, u32[]{:S(2)}, u32[]{:S(2)}) async-start(bf16[32,16,512]{2,1,0:T(8,128)(2,1)} %bitcast.12), calls=%async_computation.2 | async-start | bytes 1048576 | tf_op jit(solution)/shard_map/all_to_all | solution.py:112
  113.4 19.5 %collective-permute-start.8 = (bf16[512,512]{1,0:T(8,128)(2,1)}, bf16[512,512]{1,0:T(8,128)(2,1)S(1)}, u32[]{:S(2)}, u32[]{:S(2)}) collective-permute-start(bf16[512,512]{1,0:T(8,128)(2,1)} %collective-permute-done.6), channel_id=1, source_target_pairs={{0,224},{8,232},{16,240},{24,248},{32,0},{40,8},{48,16},{56,24},{6... | collective-permute-start | bytes 1572872 | tf_op jit(solution)/shard_map/ppermute | solution.py:41
  117.2 17.0 %collective-permute-start.9 = (bf16[512,512]{1,0:T(8,128)(2,1)}, bf16[512,512]{1,0:T(8,128)(2,1)S(1)}, u32[]{:S(2)}, u32[]{:S(2)}) collective-permute-start(bf16[512,512]{1,0:T(8,128)(2,1)} %collective-permute-done.7), channel_id=1, source_target_pairs={{0,32},{8,40},{16,48},{24,56},{32,64},{40,72},{48,80},{56,88},{64,... | collective-permute-start | bytes 1572872 | tf_op jit(solution)/shard_map/ppermute | solution.py:38
  140.5 25.1 %all-to-all-start.3 = ((bf16[32,16,512]{2,1,0:T(8,128)(2,1)}), bf16[32,16,512]{2,1,0:T(8,128)(2,1)S(1)}, u32[]{:S(2)}, u32[]{:S(2)}) async-start(bf16[32,16,512]{2,1,0:T(8,128)(2,1)} %bitcast.14), calls=%async_computation.4 | async-start | bytes 1048576 | tf_op jit(solution)/shard_map/all_to_all | solution.py:130
  148.6 17.6 %copy-start.2 = (bf16[32,4,8,128]{3,2,1,0:T(8,128)(2,1)S(1)}, bf16[32,4,8,128]{3,2,1,0:T(8,128)(2,1)}, u32[]{:S(2)}) copy-start(bf16[32,4,8,128]{3,2,1,0:T(8,128)(2,1)} %copy-done.1) | copy-start | bytes 786436
  148.7 17.6 %copy-start.4 = (f32[4,256,256]{1,2,0:T(8,128)S(1)}, f32[4,256,256]{1,2,0:T(8,128)}, u32[]{:S(2)}) copy-start(f32[4,256,256]{1,2,0:T(8,128)} %get-tuple-element.21) | copy-start | bytes 3145732
  148.7 65.0 %reduce-scatter.2.cloned.1.call-start = ((), (), s32[]{:S(2)}) async-start(), calls=%async_computation.6 | async-start | bytes 2359296 | tf_op jit(solution)/shard_map/reduce_scatter | solution.py:119
Sparse Core Ops, SparseCore 0:
  39.0 27.2 all-gather.1
  154.0 32.7 reduce-scatter.1

commit v4 on v3

--- a/solution.py
+++ b/solution.py
@@ -142,21 +142,17 @@
     grad_v = jnp.einsum("hqk,qhd->khd", probs_b, g_c, preferred_element_type=jnp.float32).astype(
         jnp.bfloat16
     )
-    grads_c = jnp.concatenate(
-        [
-            grad_q.reshape(ranks, width),
-            grad_k.reshape(ranks, width),
-            grad_v.reshape(ranks, width),
-        ],
-        axis=1,
+    back_v = lax.all_to_all(
+        select_rows_t(to_rank, grad_v.reshape(ranks, width)), "seq", 0, 0, tiled=True
     )
-    grads_back = lax.all_to_all(select_rows_t(to_rank, grads_c), "seq", 0, 0, tiled=True)
-    grads_local = select_rows_t(to_slot, grads_back)
+    grads_qk = jnp.concatenate([grad_q.reshape(ranks, width), grad_k.reshape(ranks, width)], axis=1)
+    back_qk = lax.all_to_all(select_rows_t(to_rank, grads_qk), "seq", 0, 0, tiled=True)
+    local_qk = select_rows_t(to_slot, back_qk)
     return (
         layer_out,
-        grads_local[:, :width],
-        grads_local[:, width : 2 * width],
-        grads_local[:, 2 * width :],
+        local_qk[:, :width],
+        local_qk[:, width:],
+        select_rows_t(to_slot, back_v),
     )
 
 

time: 221 us -> 231 us (1.045)
  blocking collectives: 43.6 us -> 0 us
  waiting for transfers between devices: 71.1 us -> 112 us
  starting transfers between devices: 47.8 us -> 56.9 us
  matrix products: 20.6 us -> 23.5 us
    all_to_all x1 -> x0, blocking collectives: 43.6 us -> none  [on_device(): lax.all_to_all(select_rows_t(to_rank, grads_c), 'seq', 0, 0, tiled=True)]
    all_to_all x0 -> x2, waiting for transfers between devices: none -> 40.6 us  [the longest x1 26.1 us: on_device(): lax.all_to_all(select_rows_t(to_rank, grads_qk), 'seq', 0, 0, tiled=True)]
    all_to_all x0 -> x2, starting transfers between devices: none -> 9.09 us  [the longest x1 4.55 us: on_device(): lax.all_to_all(select_rows_t(to_rank, grads_qk), 'seq', 0, 0, tiled=True)]
    dot_general x3 -> x5, matrix products: 2.42 us -> 5.38 us  [select_rows_t(): lax.dot_general(onehot, rows, (((0,), (0,)), ((), ())), preferred_element...]
  transfers between devices with their start and end apart: 16 -> 18, of which waited for: 9 -> 11; matrix products, arithmetic and copies ran while one was open for 16% -> 16% of each run, Pallas kernels for 0% -> 0%
where the time goes in v4:
time: 231 us; the launch traced here: 230 us
  waiting for transfers between devices  112 us (48%)
  starting transfers between devices  56.9 us (25%)
  matrix products  23.5 us (10%)
  local copies, waits for them, and re-layouts  16 us (7%)
  between operations  14.6 us (6%)
  other arithmetic  6.71 us (3%)
    ppermute x6, waiting for transfers between devices, ring(): fwd = lax.ppermute(fwd, axis_name, step_perm(1))  42.3 us
    all_to_all x1, waiting for transfers between devices, on_device(): lax.all_to_all(select_rows_t(to_rank, grads_qk), 'seq', 0, 0, tiled=True)  26.1 us
    all_to_all x1, waiting for transfers between devices, on_device(): lax.all_to_all(select_rows_t(to_rank, grad_v.reshape(ranks, width)), 'seq...  14.5 us
    all_to_all x1, waiting for transfers between devices, on_device(): lax.all_to_all(select_rows(to_slot, grad_attention), 'seq', 0, 0, tiled=T...  11.9 us
    all_to_all x1, starting transfers between devices, on_device(): got_counts = lax.all_to_all(send_counts, 'seq', 0, 0, tiled=True)  11.5 us
    ppermute x4, waiting for transfers between devices, ring(): bwd = lax.ppermute(bwd, axis_name, step_perm(-1))  10.9 us
    ppermute x4, starting transfers between devices, ring(): bwd = lax.ppermute(bwd, axis_name, step_perm(-1))  10.1 us
    all_to_all x1, starting transfers between devices, on_device(): lax.all_to_all(select_rows_t(to_rank, attn_c.reshape(ranks, width)), 'seq...  9.27 us
  transfers between devices with their start and end apart: 18, of which 11 were waited for; matrix products, arithmetic and copies ran while one was open for 16% of the time, Pallas kernels for 0%

profile of v4, /device:TPU:4, one launch (start us, length us, event | category | flops | bytes accessed | tf_op | source)
XLA Modules:
  0.0 229.5 jit_solution(5876602745784750927)
XLA Ops:
  7.2 0.7 fusion.47
  7.9 0.6 reduce-window.18
  8.5 0.2 slice_reduce_fusion
  8.7 0.9 convert_reduce_fusion
  9.6 0.7 copy.57
  10.3 11.5 %all-to-all-start = ((s32[32,1,1]{2,1,0:T(1,128)}), s32[32,1,1]{2,1,0:T(1,128)S(1)}, u32[]{:S(2)}, u32[]{:S(2)}) async-start(s32[32,1,1]{2,1,0:T(1,128)} %copy.57), calls=%async_computation | async-start | bytes 32768 | tf_op jit(solution)/shard_map/all_to_all | solution.py:75
  21.8 0.7 multiply_add_fusion
  22.5 2.8 %convolution_convert_fusion.1 = bf16[512,1536]{1,0:T(8,128)(2,1)} fusion(bf16[256,512]{1,0:T(8,128)(2,1)} %param.9, bf16[256,512]{1,0:T(8,128)(2,1)} %param.8, bf16[256,512]{1,0:T(8,128)(2,1)} %param.7, s32[256]{0:T(256)S(1)} %multiply_add_fusion), kind=kOutput, calls=%fused_computation.2 | convolution fusion | flops 405929984 | bytes 2360320 | tf_op jit(solution)/shard_map/dot_general | solution.py:13
  25.3 6.2 %all-to-all-done = s32[32,1,1]{2,1,0:T(1,128)S(1)} async-done(((s32[32,1,1]{2,1,0:T(1,128)}), s32[32,1,1]{2,1,0:T(1,128)S(1)}, u32[]{:S(2)}, u32[]{:S(2)}) %all-to-all-start) | async-done | bytes 160 | tf_op jit(solution)/shard_map/all_to_all | solution.py:75
  31.5 4.0 %all-to-all-start.1 = ((bf16[32,16,1536]{2,1,0:T(8,128)(2,1)}), bf16[32,16,1536]{2,1,0:T(8,128)(2,1)S(1)}, u32[]{:S(2)}, u32[]{:S(2)}) async-start(bf16[32,16,1536]{2,1,0:T(8,128)(2,1)} %bitcast.4), calls=%async_computation.1 | async-start | bytes 3145728 | tf_op jit(solution)/shard_map/all_to_all | solution.py:74
  35.5 1.8 collective-permute-start
  37.3 1.6 collective-permute-start.1
  39.0 4.6 %collective-permute-done = bf16[512,128]{1,0:T(8,128)(2,1)S(1)} collective-permute-done((bf16[512,128]{1,0:T(8,128)(2,1)S(1)}, bf16[512,128]{1,0:T(8,128)(2,1)S(1)}, u32[]{:S(2)}, u32[]{:S(2)}) %collective-permute-start) | collective-permute-done | bytes 131104 | tf_op jit(solution)/shard_map/ppermute | solution.py:38
  43.6 1.0 collective-permute-start.2
  44.6 1.8 collective-permute-done.1
  46.4 4.1 %collective-permute-done.2 = bf16[512,128]{1,0:T(8,128)(2,1)S(1)} collective-permute-done((bf16[512,128]{1,0:T(8,128)(2,1)S(1)}, bf16[512,128]{1,0:T(8,128)(2,1)S(1)}, u32[]{:S(2)}, u32[]{:S(2)}) %collective-permute-start.2) | collective-permute-done | bytes 131104 | tf_op jit(solution)/shard_map/ppermute | solution.py:38
  50.5 2.0 collective-permute-start.3
  52.5 0.2 fusion.48
  52.8 0.6 fusion.59
  53.4 2.6 %broadcast_select_fusion = (s32[256]{0:T(256)S(1)}, s32[256]{0:T(256)S(1)}) fusion(s32[]{:T(128)} %bitcast.9, s32[]{:T(128)} %bitcast.8, s32[]{:T(128)} %bitcast.7, s32[]{:T(128)} %bitcast.6), kind=kLoop, calls=%fused_computation.96 | loop fusion | flops 2816 | bytes 2064 | tf_op jit(solution)/shard_map/jit(_where)/select_n | solution.py:97
  56.0 2.4 %collective-permute-start.4 = (bf16[512,512]{1,0:T(8,128)(2,1)S(1)}, bf16[512,512]{1,0:T(8,128)(2,1)S(1)}, u32[]{:S(2)}, u32[]{:S(2)}) collective-permute-start(bf16[512,512]{1,0:T(8,128)(2,1)S(1)} %constant_dynamic-update-slice_fusion.8), channel_id=1, source_target_pairs={{0,224},{8,232},{16,240},{24,248},{32,0},{40,8},{48,16},{56,24},{6... | collective-permute-start | bytes 1572872 | tf_op jit(solution)/shard_map/ppermute | solution.py:41
  58.3 24.5 %collective-permute-done.3 = bf16[512,512]{1,0:T(8,128)(2,1)S(1)} collective-permute-done((bf16[512,512]{1,0:T(8,128)(2,1)S(1)}, bf16[512,512]{1,0:T(8,128)(2,1)S(1)}, u32[]{:S(2)}, u32[]{:S(2)}) %collective-permute-start.3) | collective-permute-done | bytes 524320 | tf_op jit(solution)/shard_map/ppermute | solution.py:38
  82.8 0.1 fusion.37
  83.1 0.7 reduce.2
  84.1 3.3 %collective-permute-start.6 = (bf16[512,512]{1,0:T(8,128)(2,1)S(1)}, bf16[512,512]{1,0:T(8,128)(2,1)}, u32[]{:S(2)}, u32[]{:S(2)}) collective-permute-start(bf16[512,512]{1,0:T(8,128)(2,1)S(1)} %collective-permute-done.4), channel_id=1, source_target_pairs={{0,224},{8,232},{16,240},{24,248},{32,0},{40,8},{48,16},{56,24},{6... | collective-permute-start | bytes 1572872 | tf_op jit(solution)/shard_map/ppermute | solution.py:41
  87.4 8.8 %collective-permute-done.5 = bf16[512,512]{1,0:T(8,128)(2,1)} collective-permute-done((bf16[512,512]{1,0:T(8,128)(2,1)S(1)}, bf16[512,512]{1,0:T(8,128)(2,1)}, u32[]{:S(2)}, u32[]{:S(2)}) %collective-permute-start.5) | collective-permute-done | bytes 524320 | tf_op jit(solution)/shard_map/ppermute | solution.py:38
  96.3 0.6 convolution_convert_fusion.2
  96.9 0.1 copy.78
  97.1 0.1 copy.79
  97.2 1.5 fusion.60
  98.7 0.8 convolution_convert_fusion.13
  99.5 1.2 convolution_convert_fusion.6
  100.7 9.3 %all-to-all-start.2 = ((bf16[32,16,512]{2,1,0:T(8,128)(2,1)}), bf16[32,16,512]{2,1,0:T(8,128)(2,1)S(1)}, u32[]{:S(2)}, u32[]{:S(2)}) async-start(bf16[32,16,512]{2,1,0:T(8,128)(2,1)} %bitcast.12), calls=%async_computation.2 | async-start | bytes 1048576 | tf_op jit(solution)/shard_map/all_to_all | solution.py:112
  110.1 2.4 %broadcast_in_dim.82 = bf16[512,4096]{1,0:T(8,128)(2,1)} broadcast(bf16[]{:T(256)} %constant.130.clone.1), dimensions={} | broadcast | bytes 4194306 | tf_op jit(solution)/shard_map/broadcast_in_dim | solution.py:33
  112.6 0.9 constant_dynamic-update-slice_fusion.7
  113.4 2.9 %collective-permute-start.8 = (bf16[512,512]{1,0:T(8,128)(2,1)}, bf16[512,512]{1,0:T(8,128)(2,1)S(1)}, u32[]{:S(2)}, u32[]{:S(2)}) collective-permute-start(bf16[512,512]{1,0:T(8,128)(2,1)} %collective-permute-done.6), channel_id=1, source_target_pairs={{0,224},{8,232},{16,240},{24,248},{32,0},{40,8},{48,16},{56,24},{6... | collective-permute-start | bytes 1572872 | tf_op jit(solution)/shard_map/ppermute | solution.py:41
  116.4 0.9 constant_dynamic-update-slice_fusion.6
  117.2 0.9 constant_dynamic-update-slice_fusion.5
  118.1 1.9 constant_dynamic-update-slice_fusion.4
  120.0 1.9 constant_dynamic-update-slice_fusion.3
  121.9 1.9 constant_dynamic-update-slice_fusion.2
  123.8 9.1 %collective-permute-done.8 = bf16[512,512]{1,0:T(8,128)(2,1)S(1)} collective-permute-done((bf16[512,512]{1,0:T(8,128)(2,1)}, bf16[512,512]{1,0:T(8,128)(2,1)S(1)}, u32[]{:S(2)}, u32[]{:S(2)}) %collective-permute-start.8) | collective-permute-done | bytes 524320 | tf_op jit(solution)/shard_map/ppermute | solution.py:41
  132.9 0.9 constant_dynamic-update-slice_fusion.1
  133.8 0.4 collective-permute-done.9
  134.2 0.9 constant_dynamic-update-slice_fusion
  135.1 5.4 %convolution_convert_fusion.7 = bf16[512,512]{1,0:T(8,128)(2,1)} fusion(bf16[512,4096]{1,0:T(8,128)(2,1)} %constant_dynamic-update-slice_fusion, bf16[256,4096]{1,0:T(8,128)(2,1)} %all-gather.2.cloned.1.call-done, s32[256]{0:T(256)S(1)} %multiply_add_fusion), kind=kOutput, calls=%fused_computation.15 | convolution fusion | flops 1208483840 | bytes 6816768 | tf_op jit(solution)/shard_map/dot_general | solution.py:13
  140.5 8.1 %all-to-all-start.3 = ((bf16[32,16,512]{2,1,0:T(8,128)(2,1)}), bf16[32,16,512]{2,1,0:T(8,128)(2,1)S(1)}, u32[]{:S(2)}, u32[]{:S(2)}) async-start(bf16[32,16,512]{2,1,0:T(8,128)(2,1)} %bitcast.14), calls=%async_computation.4 | async-start | bytes 1048576 | tf_op jit(solution)/shard_map/all_to_all | solution.py:130
  148.7 5.0 %convolution_convert_fusion = bf16[256,4096]{1,0:T(8,128)(2,1)} fusion(bf16[512,4096]{1,0:T(8,128)(2,1)} %constant_dynamic-update-slice_fusion, bf16[512,512]{1,0:T(8,128)(2,1)S(1)} %bitcast.77, s32[256]{0:T(256)S(1)} %multiply_add_fusion), kind=kOutput, calls=%fused_computation.1 | convolution fusion | flops 1209270272 | bytes 6816768 | tf_op jit(solution)/shard_map/dot_general | solution.py:117
  153.8 11.9 %all-to-all-done.3 = bf16[32,16,512]{2,1,0:T(8,128)(2,1)S(1)} async-done(((bf16[32,16,512]{2,1,0:T(8,128)(2,1)}), bf16[32,16,512]{2,1,0:T(8,128)(2,1)S(1)}, u32[]{:S(2)}, u32[]{:S(2)}) %all-to-all-start.3) | async-done | bytes 524320 | tf_op jit(solution)/shard_map/all_to_all | solution.py:130
  165.7 0.3 convolution_convert_fusion.10
  166.0 0.1 copy.63
  166.1 0.8 convolution_convert_fusion.9
  166.9 1.2 convolution_convert_fusion.5
  168.1 4.5 %all-to-all-start.5 = ((bf16[32,16,512]{2,1,0:T(8,128)(2,1)}), bf16[32,16,512]{2,1,0:T(8,128)(2,1)S(1)}, u32[]{:S(2)}, u32[]{:S(2)}) async-start(bf16[32,16,512]{2,1,0:T(8,128)(2,1)} %bitcast.26), calls=%async_computation.6 | async-start | bytes 1048576 | tf_op jit(solution)/shard_map/all_to_all | solution.py:145
  172.8 0.3 fusion.5
  173.1 0.2 fusion.6
  173.3 0.3 fusion.7
  173.6 1.5 convolution_convert_fusion.3
  175.1 14.5 %all-to-all-done.5 = bf16[32,16,512]{2,1,0:T(8,128)(2,1)S(1)} async-done(((bf16[32,16,512]{2,1,0:T(8,128)(2,1)}), bf16[32,16,512]{2,1,0:T(8,128)(2,1)S(1)}, u32[]{:S(2)}, u32[]{:S(2)}) %all-to-all-start.5) | async-done | bytes 524320 | tf_op jit(solution)/shard_map/all_to_all | solution.py:145
  189.6 4.5 %all-to-all-start.4 = ((bf16[32,16,1024]{2,1,0:T(8,128)(2,1)}), bf16[32,16,1024]{2,1,0:T(8,128)(2,1)S(1)}, u32[]{:S(2)}, u32[]{:S(2)}) async-start(bf16[32,16,1024]{2,1,0:T(8,128)(2,1)} %bitcast.22), calls=%async_computation.5 | async-start | bytes 2097152 | tf_op jit(solution)/shard_map/all_to_all | solution.py:149
  194.2 1.1 convolution_convert_fusion.8
  195.3 26.1 %all-to-all-done.4 = bf16[32,16,1024]{2,1,0:T(8,128)(2,1)S(1)} async-done(((bf16[32,16,1024]{2,1,0:T(8,128)(2,1)}), bf16[32,16,1024]{2,1,0:T(8,128)(2,1)S(1)}, u32[]{:S(2)}, u32[]{:S(2)}) %all-to-all-start.4) | async-done | bytes 1048608 | tf_op jit(solution)/shard_map/all_to_all | solution.py:149
  221.4 0.5 convolution_convert_fusion.4
  221.9 0.8 fusion.58
  (41 shorter events, 1.0 us)
Async XLA Ops:
  7.2 45.4 %copy-start = (s32[32,2,2]{0,2,1:T(2,128)S(1)}, s32[32,2,2]{0,2,1:T(2,128)}, u32[]{:S(2)}) copy-start(s32[32,2,2]{0,2,1:T(2,128)} %param.13) | copy-start | bytes 1540
  7.2 28.3 %copy-start.3 = (bf16[512,128]{1,0:T(8,128)(2,1)S(1)}, bf16[512,128]{1,0:T(8,128)(2,1)}, u32[]{:S(2)}) copy-start(bf16[512,128]{1,0:T(8,128)(2,1)} %param.10) | copy-start | bytes 393220
  10.3 21.2 %all-to-all-start = ((s32[32,1,1]{2,1,0:T(1,128)}), s32[32,1,1]{2,1,0:T(1,128)S(1)}, u32[]{:S(2)}, u32[]{:S(2)}) async-start(s32[32,1,1]{2,1,0:T(1,128)} %copy.57), calls=%async_computation | async-start | bytes 32768 | tf_op jit(solution)/shard_map/all_to_all | solution.py:75
  31.5 64.8 %all-to-all-start.1 = ((bf16[32,16,1536]{2,1,0:T(8,128)(2,1)}), bf16[32,16,1536]{2,1,0:T(8,128)(2,1)S(1)}, u32[]{:S(2)}, u32[]{:S(2)}) async-start(bf16[32,16,1536]{2,1,0:T(8,128)(2,1)} %bitcast.4), calls=%async_computation.1 | async-start | bytes 3145728 | tf_op jit(solution)/shard_map/all_to_all | solution.py:74
  35.5 99.7 %all-gather.2.cloned.1.call-start = ((), (), s32[]{:S(2)}) async-start(), calls=%async_computation.8 | async-start | bytes 2359296 | tf_op jit(solution)/shard_map/all_gather | solution.py:125
  35.5 8.1 %collective-permute-start = (bf16[512,128]{1,0:T(8,128)(2,1)S(1)}, bf16[512,128]{1,0:T(8,128)(2,1)S(1)}, u32[]{:S(2)}, u32[]{:S(2)}) collective-permute-start(bf16[512,128]{1,0:T(8,128)(2,1)S(1)} %copy-done.3), channel_id=1, source_target_pairs={{0,8},{8,16},{16,24},{24,0},{32,40},{40,48},{48,56},{56,32},{64,72... | collective-permute-start | bytes 393224 | tf_op jit(solution)/shard_map/ppermute | solution.py:38
  37.3 9.1 %collective-permute-start.1 = (bf16[512,128]{1,0:T(8,128)(2,1)S(1)}, bf16[512,128]{1,0:T(8,128)(2,1)S(1)}, u32[]{:S(2)}, u32[]{:S(2)}) collective-permute-start(bf16[512,128]{1,0:T(8,128)(2,1)S(1)} %copy-done.3), channel_id=1, source_target_pairs={{0,24},{8,0},{16,8},{24,16},{32,56},{40,32},{48,40},{56,48},{64,88... | collective-permute-start | bytes 393224 | tf_op jit(solution)/shard_map/ppermute | solution.py:41
  43.6 6.9 %collective-permute-start.2 = (bf16[512,128]{1,0:T(8,128)(2,1)S(1)}, bf16[512,128]{1,0:T(8,128)(2,1)S(1)}, u32[]{:S(2)}, u32[]{:S(2)}) collective-permute-start(bf16[512,128]{1,0:T(8,128)(2,1)S(1)} %collective-permute-done), channel_id=1, source_target_pairs={{0,8},{8,16},{16,24},{24,0},{32,40},{40,48},{48,56},{56,32},{64,72... | collective-permute-start | bytes 393224 | tf_op jit(solution)/shard_map/ppermute | solution.py:38
  50.5 32.3 %collective-permute-start.3 = (bf16[512,512]{1,0:T(8,128)(2,1)S(1)}, bf16[512,512]{1,0:T(8,128)(2,1)S(1)}, u32[]{:S(2)}, u32[]{:S(2)}) collective-permute-start(bf16[512,512]{1,0:T(8,128)(2,1)S(1)} %constant_dynamic-update-slice_fusion.8), channel_id=1, source_target_pairs={{0,32},{8,40},{16,48},{24,56},{32,64},{40,72},{48,80},{56,88},{64,... | collective-permute-start | bytes 1572872 | tf_op jit(solution)/shard_map/ppermute | solution.py:38
  56.0 28.1 %collective-permute-start.4 = (bf16[512,512]{1,0:T(8,128)(2,1)S(1)}, bf16[512,512]{1,0:T(8,128)(2,1)S(1)}, u32[]{:S(2)}, u32[]{:S(2)}) collective-permute-start(bf16[512,512]{1,0:T(8,128)(2,1)S(1)} %constant_dynamic-update-slice_fusion.8), channel_id=1, source_target_pairs={{0,224},{8,232},{16,240},{24,248},{32,0},{40,8},{48,16},{56,24},{6... | collective-permute-start | bytes 1572872 | tf_op jit(solution)/shard_map/ppermute | solution.py:41
  82.8 13.5 %collective-permute-start.5 = (bf16[512,512]{1,0:T(8,128)(2,1)S(1)}, bf16[512,512]{1,0:T(8,128)(2,1)}, u32[]{:S(2)}, u32[]{:S(2)}) collective-permute-start(bf16[512,512]{1,0:T(8,128)(2,1)S(1)} %collective-permute-done.3), channel_id=1, source_target_pairs={{0,32},{8,40},{16,48},{24,56},{32,64},{40,72},{48,80},{56,88},{64,... | collective-permute-start | bytes 1572872 | tf_op jit(solution)/shard_map/ppermute | solution.py:38
  84.1 29.3 %collective-permute-start.6 = (bf16[512,512]{1,0:T(8,128)(2,1)S(1)}, bf16[512,512]{1,0:T(8,128)(2,1)}, u32[]{:S(2)}, u32[]{:S(2)}) collective-permute-start(bf16[512,512]{1,0:T(8,128)(2,1)S(1)} %collective-permute-done.4), channel_id=1, source_target_pairs={{0,224},{8,232},{16,240},{24,248},{32,0},{40,8},{48,16},{56,24},{6... | collective-permute-start | bytes 1572872 | tf_op jit(solution)/shard_map/ppermute | solution.py:41
  96.3 21.0 %collective-permute-start.7 = (bf16[512,512]{1,0:T(8,128)(2,1)}, bf16[512,512]{1,0:T(8,128)(2,1)}, u32[]{:S(2)}, u32[]{:S(2)}) collective-permute-start(bf16[512,512]{1,0:T(8,128)(2,1)} %collective-permute-done.5), channel_id=1, source_target_pairs={{0,32},{8,40},{16,48},{24,56},{32,64},{40,72},{48,80},{56,88},{64,... | collective-permute-start | bytes 1572872 | tf_op jit(solution)/shard_map/ppermute | solution.py:38
  96.9 2.6 %copy-start.1 = (bf16[32,4,8,128]{3,2,1,0:T(8,128)(2,1)}, bf16[32,4,8,128]{3,2,1,0:T(8,128)(2,1)S(1)}, u32[]{:S(2)}) copy-start(bf16[32,4,8,128]{3,2,1,0:T(8,128)(2,1)S(1)} %get-tuple-element.12) | copy-start | bytes 786436
  100.7 34.4 %all-to-all-start.2 = ((bf16[32,16,512]{2,1,0:T(8,128)(2,1)}), bf16[32,16,512]{2,1,0:T(8,128)(2,1)S(1)}, u32[]{:S(2)}, u32[]{:S(2)}) async-start(bf16[32,16,512]{2,1,0:T(8,128)(2,1)} %bitcast.12), calls=%async_computation.2 | async-start | bytes 1048576 | tf_op jit(solution)/shard_map/all_to_all | solution.py:112
  113.4 19.5 %collective-permute-start.8 = (bf16[512,512]{1,0:T(8,128)(2,1)}, bf16[512,512]{1,0:T(8,128)(2,1)S(1)}, u32[]{:S(2)}, u32[]{:S(2)}) collective-permute-start(bf16[512,512]{1,0:T(8,128)(2,1)} %collective-permute-done.6), channel_id=1, source_target_pairs={{0,224},{8,232},{16,240},{24,248},{32,0},{40,8},{48,16},{56,24},{6... | collective-permute-start | bytes 1572872 | tf_op jit(solution)/shard_map/ppermute | solution.py:41
  117.2 17.0 %collective-permute-start.9 = (bf16[512,512]{1,0:T(8,128)(2,1)}, bf16[512,512]{1,0:T(8,128)(2,1)S(1)}, u32[]{:S(2)}, u32[]{:S(2)}) collective-permute-start(bf16[512,512]{1,0:T(8,128)(2,1)} %collective-permute-done.7), channel_id=1, source_target_pairs={{0,32},{8,40},{16,48},{24,56},{32,64},{40,72},{48,80},{56,88},{64,... | collective-permute-start | bytes 1572872 | tf_op jit(solution)/shard_map/ppermute | solution.py:38
  140.5 25.1 %all-to-all-start.3 = ((bf16[32,16,512]{2,1,0:T(8,128)(2,1)}), bf16[32,16,512]{2,1,0:T(8,128)(2,1)S(1)}, u32[]{:S(2)}, u32[]{:S(2)}) async-start(bf16[32,16,512]{2,1,0:T(8,128)(2,1)} %bitcast.14), calls=%async_computation.4 | async-start | bytes 1048576 | tf_op jit(solution)/shard_map/all_to_all | solution.py:130
  148.6 74.1 %reduce-scatter.2.cloned.1.call-start = ((), (), s32[]{:S(2)}) async-start(), calls=%async_computation.7 | async-start | bytes 2359296 | tf_op jit(solution)/shard_map/reduce_scatter | solution.py:119
  166.0 6.8 %copy-start.2 = (bf16[32,4,8,128]{3,2,1,0:T(8,128)(2,1)S(1)}, bf16[32,4,8,128]{3,2,1,0:T(8,128)(2,1)}, u32[]{:S(2)}) copy-start(bf16[32,4,8,128]{3,2,1,0:T(8,128)(2,1)} %copy-done.1) | copy-start | bytes 786436
  166.0 6.8 %copy-start.4 = (f32[4,256,256]{1,2,0:T(8,128)S(1)}, f32[4,256,256]{1,2,0:T(8,128)}, u32[]{:S(2)}) copy-start(f32[4,256,256]{1,2,0:T(8,128)} %get-tuple-element.20) | copy-start | bytes 3145732
  168.1 21.5 %all-to-all-start.5 = ((bf16[32,16,512]{2,1,0:T(8,128)(2,1)}), bf16[32,16,512]{2,1,0:T(8,128)(2,1)S(1)}, u32[]{:S(2)}, u32[]{:S(2)}) async-start(bf16[32,16,512]{2,1,0:T(8,128)(2,1)} %bitcast.26), calls=%async_computation.6 | async-start | bytes 1048576 | tf_op jit(solution)/shard_map/all_to_all | solution.py:145
  189.6 31.7 %all-to-all-start.4 = ((bf16[32,16,1024]{2,1,0:T(8,128)(2,1)}), bf16[32,16,1024]{2,1,0:T(8,128)(2,1)S(1)}, u32[]{:S(2)}, u32[]{:S(2)}) async-start(bf16[32,16,1024]{2,1,0:T(8,128)(2,1)} %bitcast.22), calls=%async_computation.5 | async-start | bytes 2097152 | tf_op jit(solution)/shard_map/all_to_all | solution.py:149
Sparse Core Ops, SparseCore 0:
  39.0 27.2 all-gather.1
  153.9 32.6 reduce-scatter.1

commit v5 on v3

--- a/solution.py
+++ b/solution.py
@@ -43,7 +43,7 @@
         return out
 
     row = ring(block, y, ny, lambda d: perm(d, 0), cols, ny * cols)
-    return ring(row, z, nz, lambda d: perm(0, d), ny * cols, n * cols)
+    return ring(row, z, nz, lambda d: perm(0, d), ny * cols, n * cols), row
 
 
 def on_device(queries, key_rows, value_rows, out_weight, grad_output, cluster_ids, block_pattern):
@@ -69,9 +69,10 @@
     ).astype(jnp.bfloat16)
 
     ring_y = 4 if groups % 4 == 0 else 1
-    full_weight = ring_gather_cols(out_weight, "seq", ring_y, groups // ring_y)
+    full_weight, weight_row = ring_gather_cols(out_weight, "seq", ring_y, groups // ring_y)
     qkv = jnp.concatenate([queries, key_rows, value_rows], axis=1)
-    qkv_in = lax.all_to_all(select_rows(to_slot, qkv), "seq", 0, 0, tiled=True)
+    qkv_slots, _ = lax.optimization_barrier((select_rows(to_slot, qkv), weight_row))
+    qkv_in = lax.all_to_all(qkv_slots, "seq", 0, 0, tiled=True)
     got_counts = lax.all_to_all(send_counts, "seq", 0, 0, tiled=True)
 
     offsets = jnp.cumsum(got_counts) - got_counts

time: 221 us -> 226 us (1.023)
  starting transfers between devices: 47.8 us -> 50.7 us
    ppermute x6, waiting for transfers between devices: 42.3 us -> 51.8 us  [ring(): fwd = lax.ppermute(fwd, axis_name, step_perm(1))]
    all_to_all x1, waiting for transfers between devices: 6.15 us -> 0.01 us  [on_device(): got_counts = lax.all_to_all(send_counts, 'seq', 0, 0, tiled=True)]
    all_to_all x1, starting transfers between devices: 3.97 us -> 8.57 us  [on_device(): qkv_in = lax.all_to_all(qkv_slots, 'seq', 0, 0, tiled=True)]
    ppermute x4, waiting for transfers between devices: 10.9 us -> 8.53 us  [ring(): bwd = lax.ppermute(bwd, axis_name, step_perm(-1))]
  transfers between devices with their start and end apart: 16 -> 16, of which waited for: 9 -> 6; matrix products, arithmetic and copies ran while one was open for 16% -> 17% of each run, Pallas kernels for 0% -> 0%
where the time goes in v5:
time: 226 us
  waiting for transfers between devices  72.7 us (32%)
  starting transfers between devices  50.7 us (22%)
  blocking collectives  43.6 us (19%)
  matrix products  20.6 us (9%)
  local copies, waits for them, and re-layouts  17 us (8%)
  between operations  14.6 us (6%)
  other arithmetic  6.66 us (3%)
    ppermute x6, waiting for transfers between devices, ring(): fwd = lax.ppermute(fwd, axis_name, step_perm(1))  51.8 us
    all_to_all x1, blocking collectives, on_device(): lax.all_to_all(select_rows_t(to_rank, grads_c), 'seq', 0, 0, tiled=True)  43.6 us
    all_to_all x1, waiting for transfers between devices, on_device(): lax.all_to_all(select_rows(to_slot, grad_attention), 'seq', 0, 0, tiled=T...  11.6 us
    all_to_all x1, starting transfers between devices, on_device(): got_counts = lax.all_to_all(send_counts, 'seq', 0, 0, tiled=True)  10.3 us
    ppermute x4, starting transfers between devices, ring(): bwd = lax.ppermute(bwd, axis_name, step_perm(-1))  9.4 us
    dot_general x4, matrix products, select_rows(): jnp.dot(onehot, rows, preferred_element_type=jnp.float32).astype(rows.dtype)  9.12 us
    all_to_all x1, starting transfers between devices, on_device(): lax.all_to_all(select_rows_t(to_rank, attn_c.reshape(ranks, width)), 'seq...  8.91 us
    all_to_all x1, starting transfers between devices, on_device(): qkv_in = lax.all_to_all(qkv_slots, 'seq', 0, 0, tiled=True)  8.57 us
  transfers between devices with their start and end apart: 16, of which 6 were waited for; matrix products, arithmetic and copies ran while one was open for 17% of the time, Pallas kernels for 0%

profile of v5, /device:TPU:4, one launch (start us, length us, event | category | flops | bytes accessed | tf_op | source)
XLA Modules:
  0.0 225.8 jit_solution(14181921366092134926)
XLA Ops:
  7.2 1.7 collective-permute-start
  8.8 1.7 collective-permute-start.1
  10.5 0.7 fusion.45
  11.2 0.6 reduce-window.18
  11.8 0.2 slice_reduce_fusion
  12.0 0.9 convert_reduce_fusion
  12.9 0.7 copy.57
  13.6 10.3 %all-to-all-start = ((s32[32,1,1]{2,1,0:T(1,128)}), s32[32,1,1]{2,1,0:T(1,128)S(1)}, u32[]{:S(2)}, u32[]{:S(2)}) async-start(s32[32,1,1]{2,1,0:T(1,128)} %copy.57), calls=%async_computation | async-start | bytes 32768 | tf_op jit(solution)/shard_map/all_to_all | solution.py:76
  23.8 0.7 multiply_add_fusion
  24.5 2.8 %convolution_convert_fusion.2 = bf16[512,1536]{1,0:T(8,128)(2,1)} fusion(bf16[256,512]{1,0:T(8,128)(2,1)} %param.9, bf16[256,512]{1,0:T(8,128)(2,1)} %param.8, bf16[256,512]{1,0:T(8,128)(2,1)} %param.7, s32[256]{0:T(256)S(1)} %multiply_add_fusion), kind=kOutput, calls=%fused_computation.3 | convolution fusion | flops 405929984 | bytes 2360320 | tf_op jit(solution)/shard_map/dot_general | solution.py:13
  27.4 0.9 constant_dynamic-update-slice_fusion.11
  28.4 1.9 collective-permute-start.2
  30.4 4.3 %collective-permute-done.2 = bf16[512,128]{1,0:T(8,128)(2,1)S(1)} collective-permute-done((bf16[512,128]{1,0:T(8,128)(2,1)S(1)}, bf16[512,128]{1,0:T(8,128)(2,1)S(1)}, u32[]{:S(2)}, u32[]{:S(2)}) %collective-permute-start.2) | collective-permute-done | bytes 131104 | tf_op jit(solution)/shard_map/ppermute | solution.py:38
  34.7 8.6 %all-to-all-start.1 = ((bf16[32,16,1536]{2,1,0:T(8,128)(2,1)}), bf16[32,16,1536]{2,1,0:T(8,128)(2,1)S(1)}, u32[]{:S(2)}, u32[]{:S(2)}) async-start(bf16[32,16,1536]{2,1,0:T(8,128)(2,1)} %bitcast.74), calls=%async_computation.1 | async-start | bytes 3145728 | tf_op jit(solution)/shard_map/all_to_all | solution.py:75
  43.4 0.7 all-gather.2.cloned.1.call-update
  44.1 1.9 collective-permute-start.3
  45.9 0.2 fusion.46
  46.2 0.6 fusion.57
  46.7 2.6 %broadcast_select_fusion = (s32[256]{0:T(256)S(1)}, s32[256]{0:T(256)S(1)}) fusion(s32[]{:T(128)} %bitcast.9, s32[]{:T(128)} %bitcast.8, s32[]{:T(128)} %bitcast.7, s32[]{:T(128)} %bitcast.6), kind=kLoop, calls=%fused_computation.93 | loop fusion | flops 2816 | bytes 2064 | tf_op jit(solution)/shard_map/jit(_where)/select_n | solution.py:98
  49.3 1.5 collective-permute-start.4
  50.9 38.4 %collective-permute-done.3 = bf16[512,512]{1,0:T(8,128)(2,1)S(1)} collective-permute-done((bf16[512,512]{1,0:T(8,128)(2,1)S(1)}, bf16[512,512]{1,0:T(8,128)(2,1)S(1)}, u32[]{:S(2)}, u32[]{:S(2)}) %collective-permute-start.3) | collective-permute-done | bytes 524320 | tf_op jit(solution)/shard_map/ppermute | solution.py:38
  89.3 0.1 fusion.36
  89.5 0.1 reduce.1
  89.6 0.7 reduce.2
  90.3 0.1 iota_add_fusion
  90.4 0.1 add.136
  90.4 0.1 iota_compare_fusion.10
  90.5 0.1 lt.104
  90.6 3.3 %collective-permute-start.6 = (bf16[512,512]{1,0:T(8,128)(2,1)S(1)}, bf16[512,512]{1,0:T(8,128)(2,1)}, u32[]{:S(2)}, u32[]{:S(2)}) collective-permute-start(bf16[512,512]{1,0:T(8,128)(2,1)S(1)} %collective-permute-done.4), channel_id=1, source_target_pairs={{0,224},{8,232},{16,240},{24,248},{32,0},{40,8},{48,16},{56,24},{6... | collective-permute-start | bytes 1572872 | tf_op jit(solution)/shard_map/ppermute | solution.py:41
  93.9 8.7 %collective-permute-done.5 = bf16[512,512]{1,0:T(8,128)(2,1)} collective-permute-done((bf16[512,512]{1,0:T(8,128)(2,1)S(1)}, bf16[512,512]{1,0:T(8,128)(2,1)}, u32[]{:S(2)}, u32[]{:S(2)}) %collective-permute-start.5) | collective-permute-done | bytes 524320 | tf_op jit(solution)/shard_map/ppermute | solution.py:38
  102.6 0.6 convolution_convert_fusion.4
  103.3 0.1 copy.78
  103.4 0.1 copy.79
  103.6 1.5 fusion.58
  105.1 0.8 convolution_convert_fusion.11
  105.9 1.2 convolution_convert_fusion.5
  107.1 8.9 %all-to-all-start.2 = ((bf16[32,16,512]{2,1,0:T(8,128)(2,1)}), bf16[32,16,512]{2,1,0:T(8,128)(2,1)S(1)}, u32[]{:S(2)}, u32[]{:S(2)}) async-start(bf16[32,16,512]{2,1,0:T(8,128)(2,1)} %bitcast.12), calls=%async_computation.2 | async-start | bytes 1048576 | tf_op jit(solution)/shard_map/all_to_all | solution.py:113
  116.1 2.4 %broadcast_in_dim.83 = bf16[512,4096]{1,0:T(8,128)(2,1)} broadcast(bf16[]{:T(256)} %constant.120.clone.1), dimensions={} | broadcast | bytes 4194306 | tf_op jit(solution)/shard_map/broadcast_in_dim | solution.py:33
  118.6 0.9 constant_dynamic-update-slice_fusion.7
  119.5 2.9 %collective-permute-start.8 = (bf16[512,512]{1,0:T(8,128)(2,1)}, bf16[512,512]{1,0:T(8,128)(2,1)S(1)}, u32[]{:S(2)}, u32[]{:S(2)}) collective-permute-start(bf16[512,512]{1,0:T(8,128)(2,1)} %collective-permute-done.6), channel_id=1, source_target_pairs={{0,224},{8,232},{16,240},{24,248},{32,0},{40,8},{48,16},{56,24},{6... | collective-permute-start | bytes 1572872 | tf_op jit(solution)/shard_map/ppermute | solution.py:41
  122.4 0.9 constant_dynamic-update-slice_fusion.6
  123.2 0.9 constant_dynamic-update-slice_fusion.5
  124.1 1.9 constant_dynamic-update-slice_fusion.4
  126.0 1.9 constant_dynamic-update-slice_fusion.3
  127.9 1.9 constant_dynamic-update-slice_fusion.2
  129.8 8.5 %collective-permute-done.8 = bf16[512,512]{1,0:T(8,128)(2,1)S(1)} collective-permute-done((bf16[512,512]{1,0:T(8,128)(2,1)}, bf16[512,512]{1,0:T(8,128)(2,1)S(1)}, u32[]{:S(2)}, u32[]{:S(2)}) %collective-permute-start.8) | collective-permute-done | bytes 524320 | tf_op jit(solution)/shard_map/ppermute | solution.py:41
  138.4 0.9 constant_dynamic-update-slice_fusion.1
  139.3 0.4 collective-permute-done.9
  139.6 0.9 constant_dynamic-update-slice_fusion
  140.6 5.4 %convolution_convert_fusion.6 = bf16[512,512]{1,0:T(8,128)(2,1)} fusion(bf16[512,4096]{1,0:T(8,128)(2,1)} %constant_dynamic-update-slice_fusion, bf16[256,4096]{1,0:T(8,128)(2,1)} %all-gather.2.cloned.1.call-done, s32[256]{0:T(256)S(1)} %multiply_add_fusion), kind=kOutput, calls=%fused_computation.14 | convolution fusion | flops 1208483840 | bytes 6816768 | tf_op jit(solution)/shard_map/dot_general | solution.py:13
  146.0 8.1 %all-to-all-start.3 = ((bf16[32,16,512]{2,1,0:T(8,128)(2,1)}), bf16[32,16,512]{2,1,0:T(8,128)(2,1)S(1)}, u32[]{:S(2)}, u32[]{:S(2)}) async-start(bf16[32,16,512]{2,1,0:T(8,128)(2,1)} %bitcast.14), calls=%async_computation.4 | async-start | bytes 1048576 | tf_op jit(solution)/shard_map/all_to_all | solution.py:131
  154.2 5.1 %convolution_convert_fusion = bf16[256,4096]{1,0:T(8,128)(2,1)} fusion(bf16[512,4096]{1,0:T(8,128)(2,1)} %constant_dynamic-update-slice_fusion, bf16[512,512]{1,0:T(8,128)(2,1)S(1)} %bitcast.73, s32[256]{0:T(256)S(1)} %multiply_add_fusion), kind=kOutput, calls=%fused_computation.1 | convolution fusion | flops 1209270272 | bytes 6816768 | tf_op jit(solution)/shard_map/dot_general | solution.py:118
  159.3 11.6 %all-to-all-done.3 = bf16[32,16,512]{2,1,0:T(8,128)(2,1)S(1)} async-done(((bf16[32,16,512]{2,1,0:T(8,128)(2,1)}), bf16[32,16,512]{2,1,0:T(8,128)(2,1)S(1)}, u32[]{:S(2)}, u32[]{:S(2)}) %all-to-all-start.3) | async-done | bytes 524320 | tf_op jit(solution)/shard_map/all_to_all | solution.py:131
  171.0 0.3 convolution_convert_fusion.8
  171.3 0.1 copy.63
  171.4 0.1 multiply_reduce_fusion
  171.5 0.3 fusion.5
  171.8 0.2 fusion.6
  172.1 0.8 convolution_convert_fusion.7
  172.9 0.3 fusion.7
  173.2 0.6 convolution_convert_fusion.1
  173.8 43.6 %all_to_all.57 = bf16[32,16,1536]{2,1,0:T(8,128)(2,1)S(1)} all-to-all(bf16[32,16,1536]{2,1,0:T(8,128)(2,1)S(1)} %bitcast.75), channel_id=1, replica_groups=mesh['seq'=32,'head'=8] {'seq'}, dimensions={0} | all-to-all | bytes 3145728 | tf_op jit(solution)/shard_map/all_to_all | solution.py:154
  217.4 0.6 convolution_convert_fusion.3
  218.0 0.9 fusion.55
  (34 shorter events, 0.5 us)
Async XLA Ops:
  7.2 38.8 %copy-start = (s32[32,2,2]{0,2,1:T(2,128)S(1)}, s32[32,2,2]{0,2,1:T(2,128)}, u32[]{:S(2)}) copy-start(s32[32,2,2]{0,2,1:T(2,128)} %param.13) | copy-start | bytes 1540
  7.2 21.2 %collective-permute-start = (bf16[512,128]{1,0:T(8,128)(2,1)}, bf16[512,128]{1,0:T(8,128)(2,1)S(1)}, u32[]{:S(2)}, u32[]{:S(2)}) collective-permute-start(bf16[512,128]{1,0:T(8,128)(2,1)} %param.10), channel_id=1, source_target_pairs={{0,8},{8,16},{16,24},{24,0},{32,40},{40,48},{48,56},{56,32},{64,72... | collective-permute-start | bytes 393224 | tf_op jit(solution)/shard_map/ppermute | solution.py:38
  8.8 21.5 %collective-permute-start.1 = (bf16[512,128]{1,0:T(8,128)(2,1)}, bf16[512,128]{1,0:T(8,128)(2,1)S(1)}, u32[]{:S(2)}, u32[]{:S(2)}) collective-permute-start(bf16[512,128]{1,0:T(8,128)(2,1)} %param.10), channel_id=1, source_target_pairs={{0,24},{8,0},{16,8},{24,16},{32,56},{40,32},{48,40},{56,48},{64,88... | collective-permute-start | bytes 393224 | tf_op jit(solution)/shard_map/ppermute | solution.py:41
  13.6 21.2 %all-to-all-start = ((s32[32,1,1]{2,1,0:T(1,128)}), s32[32,1,1]{2,1,0:T(1,128)S(1)}, u32[]{:S(2)}, u32[]{:S(2)}) async-start(s32[32,1,1]{2,1,0:T(1,128)} %copy.57), calls=%async_computation | async-start | bytes 32768 | tf_op jit(solution)/shard_map/all_to_all | solution.py:76
  28.4 6.3 %collective-permute-start.2 = (bf16[512,128]{1,0:T(8,128)(2,1)S(1)}, bf16[512,128]{1,0:T(8,128)(2,1)S(1)}, u32[]{:S(2)}, u32[]{:S(2)}) collective-permute-start(bf16[512,128]{1,0:T(8,128)(2,1)S(1)} %collective-permute-done), channel_id=1, source_target_pairs={{0,8},{8,16},{16,24},{24,0},{32,40},{40,48},{48,56},{56,32},{64,72... | collective-permute-start | bytes 393224 | tf_op jit(solution)/shard_map/ppermute | solution.py:38
  34.7 67.9 %all-to-all-start.1 = ((bf16[32,16,1536]{2,1,0:T(8,128)(2,1)}), bf16[32,16,1536]{2,1,0:T(8,128)(2,1)S(1)}, u32[]{:S(2)}, u32[]{:S(2)}) async-start(bf16[32,16,1536]{2,1,0:T(8,128)(2,1)} %bitcast.74), calls=%async_computation.1 | async-start | bytes 3145728 | tf_op jit(solution)/shard_map/all_to_all | solution.py:75
  43.3 97.3 %all-gather.2.cloned.1.call-start = ((), (), s32[]{:S(2)}) async-start(), calls=%async_computation.7 | async-start | bytes 2359296 | tf_op jit(solution)/shard_map/all_gather | solution.py:126
  44.1 45.2 %collective-permute-start.3 = (bf16[512,512]{1,0:T(8,128)(2,1)S(1)}, bf16[512,512]{1,0:T(8,128)(2,1)S(1)}, u32[]{:S(2)}, u32[]{:S(2)}) collective-permute-start(bf16[512,512]{1,0:T(8,128)(2,1)S(1)} %constant_dynamic-update-slice_fusion.8), channel_id=1, source_target_pairs={{0,32},{8,40},{16,48},{24,56},{32,64},{40,72},{48,80},{56,88},{64,... | collective-permute-start | bytes 1572872 | tf_op jit(solution)/shard_map/ppermute | solution.py:38
  49.3 41.3 %collective-permute-start.4 = (bf16[512,512]{1,0:T(8,128)(2,1)S(1)}, bf16[512,512]{1,0:T(8,128)(2,1)S(1)}, u32[]{:S(2)}, u32[]{:S(2)}) collective-permute-start(bf16[512,512]{1,0:T(8,128)(2,1)S(1)} %constant_dynamic-update-slice_fusion.8), channel_id=1, source_target_pairs={{0,224},{8,232},{16,240},{24,248},{32,0},{40,8},{48,16},{56,24},{6... | collective-permute-start | bytes 1572872 | tf_op jit(solution)/shard_map/ppermute | solution.py:41
  89.3 13.3 %collective-permute-start.5 = (bf16[512,512]{1,0:T(8,128)(2,1)S(1)}, bf16[512,512]{1,0:T(8,128)(2,1)}, u32[]{:S(2)}, u32[]{:S(2)}) collective-permute-start(bf16[512,512]{1,0:T(8,128)(2,1)S(1)} %collective-permute-done.3), channel_id=1, source_target_pairs={{0,32},{8,40},{16,48},{24,56},{32,64},{40,72},{48,80},{56,88},{64,... | collective-permute-start | bytes 1572872 | tf_op jit(solution)/shard_map/ppermute | solution.py:38
  90.6 28.8 %collective-permute-start.6 = (bf16[512,512]{1,0:T(8,128)(2,1)S(1)}, bf16[512,512]{1,0:T(8,128)(2,1)}, u32[]{:S(2)}, u32[]{:S(2)}) collective-permute-start(bf16[512,512]{1,0:T(8,128)(2,1)S(1)} %collective-permute-done.4), channel_id=1, source_target_pairs={{0,224},{8,232},{16,240},{24,248},{32,0},{40,8},{48,16},{56,24},{6... | collective-permute-start | bytes 1572872 | tf_op jit(solution)/shard_map/ppermute | solution.py:41
  102.6 20.6 %collective-permute-start.7 = (bf16[512,512]{1,0:T(8,128)(2,1)}, bf16[512,512]{1,0:T(8,128)(2,1)}, u32[]{:S(2)}, u32[]{:S(2)}) collective-permute-start(bf16[512,512]{1,0:T(8,128)(2,1)} %collective-permute-done.5), channel_id=1, source_target_pairs={{0,32},{8,40},{16,48},{24,56},{32,64},{40,72},{48,80},{56,88},{64,... | collective-permute-start | bytes 1572872 | tf_op jit(solution)/shard_map/ppermute | solution.py:38
  103.3 2.6 %copy-start.1 = (bf16[32,4,8,128]{3,2,1,0:T(8,128)(2,1)}, bf16[32,4,8,128]{3,2,1,0:T(8,128)(2,1)S(1)}, u32[]{:S(2)}) copy-start(bf16[32,4,8,128]{3,2,1,0:T(8,128)(2,1)S(1)} %get-tuple-element.17) | copy-start | bytes 786436
  107.1 33.5 %all-to-all-start.2 = ((bf16[32,16,512]{2,1,0:T(8,128)(2,1)}), bf16[32,16,512]{2,1,0:T(8,128)(2,1)S(1)}, u32[]{:S(2)}, u32[]{:S(2)}) async-start(bf16[32,16,512]{2,1,0:T(8,128)(2,1)} %bitcast.12), calls=%async_computation.2 | async-start | bytes 1048576 | tf_op jit(solution)/shard_map/all_to_all | solution.py:113
  119.5 18.9 %collective-permute-start.8 = (bf16[512,512]{1,0:T(8,128)(2,1)}, bf16[512,512]{1,0:T(8,128)(2,1)S(1)}, u32[]{:S(2)}, u32[]{:S(2)}) collective-permute-start(bf16[512,512]{1,0:T(8,128)(2,1)} %collective-permute-done.6), channel_id=1, source_target_pairs={{0,224},{8,232},{16,240},{24,248},{32,0},{40,8},{48,16},{56,24},{6... | collective-permute-start | bytes 1572872 | tf_op jit(solution)/shard_map/ppermute | solution.py:41
  123.2 16.4 %collective-permute-start.9 = (bf16[512,512]{1,0:T(8,128)(2,1)}, bf16[512,512]{1,0:T(8,128)(2,1)S(1)}, u32[]{:S(2)}, u32[]{:S(2)}) collective-permute-start(bf16[512,512]{1,0:T(8,128)(2,1)} %collective-permute-done.7), channel_id=1, source_target_pairs={{0,32},{8,40},{16,48},{24,56},{32,64},{40,72},{48,80},{56,88},{64,... | collective-permute-start | bytes 1572872 | tf_op jit(solution)/shard_map/ppermute | solution.py:38
  146.0 25.0 %all-to-all-start.3 = ((bf16[32,16,512]{2,1,0:T(8,128)(2,1)}), bf16[32,16,512]{2,1,0:T(8,128)(2,1)S(1)}, u32[]{:S(2)}, u32[]{:S(2)}) async-start(bf16[32,16,512]{2,1,0:T(8,128)(2,1)} %bitcast.14), calls=%async_computation.4 | async-start | bytes 1048576 | tf_op jit(solution)/shard_map/all_to_all | solution.py:131
  154.1 17.4 %copy-start.2 = (bf16[32,4,8,128]{3,2,1,0:T(8,128)(2,1)S(1)}, bf16[32,4,8,128]{3,2,1,0:T(8,128)(2,1)}, u32[]{:S(2)}) copy-start(bf16[32,4,8,128]{3,2,1,0:T(8,128)(2,1)} %copy-done.1) | copy-start | bytes 786436
  154.1 17.4 %copy-start.3 = (f32[4,256,256]{1,2,0:T(8,128)S(1)}, f32[4,256,256]{1,2,0:T(8,128)}, u32[]{:S(2)}) copy-start(f32[4,256,256]{1,2,0:T(8,128)} %get-tuple-element.23) | copy-start | bytes 3145732
  154.1 64.8 %reduce-scatter.2.cloned.1.call-start = ((), (), s32[]{:S(2)}) async-start(), calls=%async_computation.6 | async-start | bytes 2359296 | tf_op jit(solution)/shard_map/reduce_scatter | solution.py:120
Sparse Core Ops, SparseCore 0:
  46.0 28.1 all-gather.1
  159.4 32.7 reduce-scatter.1

commit v6 on v3

--- a/solution.py
+++ b/solution.py
@@ -62,7 +62,6 @@
     )
     earlier = jnp.cumsum(members, axis=0) - members
     local_rank = jnp.sum(earlier * members, axis=1)
-    send_counts = jnp.sum(members, axis=0)
     slot_index = cluster_ids * slot_rows + local_rank
     to_slot = (
         jnp.arange(slot_total, dtype=jnp.int32)[:, None] == slot_index[None, :]
@@ -70,13 +69,14 @@
 
     ring_y = 4 if groups % 4 == 0 else 1
     full_weight = ring_gather_cols(out_weight, "seq", ring_y, groups // ring_y)
-    qkv = jnp.concatenate([queries, key_rows, value_rows], axis=1)
+    live_flag = jnp.ones((tokens, HD), queries.dtype)
+    qkv = jnp.concatenate([queries, key_rows, value_rows, live_flag], axis=1)
     qkv_in = lax.all_to_all(select_rows(to_slot, qkv), "seq", 0, 0, tiled=True)
-    got_counts = lax.all_to_all(send_counts, "seq", 0, 0, tiled=True)
 
+    row_live = qkv_in[:, 3 * width] > 0.5
+    got_counts = jnp.sum(row_live.reshape(groups, slot_rows).astype(jnp.int32), axis=1)
     offsets = jnp.cumsum(got_counts) - got_counts
     place = jnp.arange(slot_rows, dtype=jnp.int32)
-    row_live = (place[None, :] < got_counts[:, None]).reshape(slot_total)
     rank_rows = (offsets[:, None] + place[None, :]).reshape(slot_total)
     to_rank = (
         (rank_rows[None, :] == jnp.arange(ranks, dtype=jnp.int32)[:, None]) & row_live[None, :]
@@ -84,7 +84,7 @@
     qkv_c = select_rows(to_rank, qkv_in)
     q_c = qkv_c[:, :width].reshape(ranks, head_count, HD)
     k_c = qkv_c[:, width : 2 * width].reshape(ranks, head_count, HD)
-    v_c = qkv_c[:, 2 * width :].reshape(ranks, head_count, HD)
+    v_c = qkv_c[:, 2 * width : 3 * width].reshape(ranks, head_count, HD)
 
     pattern = lax.dynamic_index_in_dim(block_pattern, owner_index, 0, keepdims=False)
     rank = jnp.arange(ranks, dtype=jnp.int32)

time: 221 us -> 217 us (0.982)
  starting transfers between devices: 47.8 us -> 43.7 us
    all_to_all x1 -> x0, starting transfers between devices: 11.5 us -> none  [on_device(): got_counts = lax.all_to_all(send_counts, 'seq', 0, 0, tiled=True)]
    all_to_all x1, starting transfers between devices: 3.97 us -> 11.5 us  [on_device(): qkv_in = lax.all_to_all(select_rows(to_slot, qkv), 'seq', 0, 0, tiled=True)]
    all_to_all x1 -> x0, waiting for transfers between devices: 6.15 us -> none  [on_device(): got_counts = lax.all_to_all(send_counts, 'seq', 0, 0, tiled=True)]
    ppermute x6, waiting for transfers between devices: 42.3 us -> 47.3 us  [ring(): fwd = lax.ppermute(fwd, axis_name, step_perm(1))]
  transfers between devices with their start and end apart: 16 -> 15, of which waited for: 9 -> 8; matrix products, arithmetic and copies ran while one was open for 16% -> 15% of each run, Pallas kernels for 0% -> 0%
where the time goes in v6:
time: 217 us; the launch traced here: 216 us
  waiting for transfers between devices  70.2 us (32%)
  starting transfers between devices  43.7 us (20%)
  blocking collectives  43.6 us (20%)
  matrix products  22.4 us (10%)
  local copies, waits for them, and re-layouts  15.5 us (7%)
  between operations  14.6 us (7%)
  other arithmetic  6.25 us (3%)
    ppermute x6, waiting for transfers between devices, ring(): fwd = lax.ppermute(fwd, axis_name, step_perm(1))  47.3 us
    all_to_all x1, blocking collectives, on_device(): lax.all_to_all(select_rows_t(to_rank, grads_c), 'seq', 0, 0, tiled=True)  43.6 us
    ppermute x4, starting transfers between devices, ring(): bwd = lax.ppermute(bwd, axis_name, step_perm(-1))  12.1 us
    all_to_all x1, waiting for transfers between devices, on_device(): lax.all_to_all(select_rows(to_slot, grad_attention), 'seq', 0, 0, tiled=T...  11.9 us
    all_to_all x1, starting transfers between devices, on_device(): qkv_in = lax.all_to_all(select_rows(to_slot, qkv), 'seq', 0, 0, tiled=True)  11.5 us
    ppermute x4, waiting for transfers between devices, ring(): bwd = lax.ppermute(bwd, axis_name, step_perm(-1))  11 us
    dot_general x4, matrix products, select_rows(): jnp.dot(onehot, rows, preferred_element_type=jnp.float32).astype(rows.dtype)  9.38 us
    all_to_all x1, starting transfers between devices, on_device(): lax.all_to_all(select_rows_t(to_rank, attn_c.reshape(ranks, width)), 'seq...  8.23 us
  transfers between devices with their start and end apart: 15, of which 8 were waited for; matrix products, arithmetic and copies ran while one was open for 15% of the time, Pallas kernels for 0%

profile of v6, /device:TPU:4, one launch (start us, length us, event | category | flops | bytes accessed | tf_op | source)
XLA Modules:
  0.0 216.3 jit_solution(9895230356073958860)
XLA Ops:
  7.2 0.7 fusion.48
  7.9 0.6 reduce-window.18
  8.4 0.2 slice_reduce_fusion
  8.7 0.8 fusion.47
  9.5 0.7 multiply_add_fusion
  10.2 3.0 %convolution_convert_fusion.2 = bf16[512,1664]{1,0:T(8,128)(2,1)} fusion(bf16[256,512]{1,0:T(8,128)(2,1)} %param.9, bf16[256,512]{1,0:T(8,128)(2,1)} %param.8, bf16[256,512]{1,0:T(8,128)(2,1)} %param.7, bf16[1664]{0:T(1024)(128)(2,1)S(1)} %pad.6.clone, s32[256]{0:T(256)S(1)} %multiply_add_fusion), kind=kOutput, calls=%fused_computation.3 | convolution fusion | flops 440598528 | bytes 2494720 | tf_op jit(solution)/shard_map/dot_general | solution.py:13
  13.2 11.5 %all-to-all-start = ((bf16[32,16,1664]{2,1,0:T(8,128)(2,1)}), bf16[32,16,1664]{2,1,0:T(8,128)(2,1)S(1)}, u32[]{:S(2)}, u32[]{:S(2)}) async-start(bf16[32,16,1664]{2,1,0:T(8,128)(2,1)} %bitcast.2), calls=%async_computation | async-start | bytes 3407872 | tf_op jit(solution)/shard_map/all_to_all | solution.py:74
  24.7 1.9 collective-permute-start
  26.6 1.4 collective-permute-start.1
  28.2 5.5 %collective-permute-done = bf16[512,128]{1,0:T(8,128)(2,1)S(1)} collective-permute-done((bf16[512,128]{1,0:T(8,128)(2,1)S(1)}, bf16[512,128]{1,0:T(8,128)(2,1)S(1)}, u32[]{:S(2)}, u32[]{:S(2)}) %collective-permute-start) | collective-permute-done | bytes 131104 | tf_op jit(solution)/shard_map/ppermute | solution.py:38
  33.7 1.7 collective-permute-start.2
  35.4 1.7 collective-permute-done.1
  37.2 6.2 %collective-permute-done.2 = bf16[512,128]{1,0:T(8,128)(2,1)S(1)} collective-permute-done((bf16[512,128]{1,0:T(8,128)(2,1)S(1)}, bf16[512,128]{1,0:T(8,128)(2,1)S(1)}, u32[]{:S(2)}, u32[]{:S(2)}) %collective-permute-start.2) | collective-permute-done | bytes 131104 | tf_op jit(solution)/shard_map/ppermute | solution.py:38
  43.4 0.1 collective-permute-start.3
  43.5 0.2 fusion.50
  43.8 4.3 %collective-permute-start.4 = (bf16[512,512]{1,0:T(8,128)(2,1)S(1)}, bf16[512,512]{1,0:T(8,128)(2,1)S(1)}, u32[]{:S(2)}, u32[]{:S(2)}) collective-permute-start(bf16[512,512]{1,0:T(8,128)(2,1)S(1)} %constant_dynamic-update-slice_fusion.8), channel_id=1, source_target_pairs={{0,224},{8,232},{16,240},{24,248},{32,0},{40,8},{48,16},{56,24},{6... | collective-permute-start | bytes 1572872 | tf_op jit(solution)/shard_map/ppermute | solution.py:41
  48.1 27.7 %collective-permute-done.3 = bf16[512,512]{1,0:T(8,128)(2,1)S(1)} collective-permute-done((bf16[512,512]{1,0:T(8,128)(2,1)S(1)}, bf16[512,512]{1,0:T(8,128)(2,1)S(1)}, u32[]{:S(2)}, u32[]{:S(2)}) %collective-permute-start.3) | collective-permute-done | bytes 524320 | tf_op jit(solution)/shard_map/ppermute | solution.py:38
  75.7 0.6 fusion.61
  76.3 2.6 %broadcast_select_fusion = (s32[256]{0:T(256)S(1)}, s32[256]{0:T(256)S(1)}) fusion(s32[]{:T(128)} %bitcast.8, s32[]{:T(128)} %bitcast.7, s32[]{:T(128)} %bitcast.6, s32[]{:T(128)} %bitcast.5), kind=kLoop, calls=%fused_computation.96 | loop fusion | flops 2816 | bytes 2064 | tf_op jit(solution)/shard_map/jit(_where)/select_n | solution.py:97
  78.9 0.1 fusion.38
  79.1 3.3 %collective-permute-start.6 = (bf16[512,512]{1,0:T(8,128)(2,1)S(1)}, bf16[512,512]{1,0:T(8,128)(2,1)}, u32[]{:S(2)}, u32[]{:S(2)}) collective-permute-start(bf16[512,512]{1,0:T(8,128)(2,1)S(1)} %collective-permute-done.4), channel_id=1, source_target_pairs={{0,224},{8,232},{16,240},{24,248},{32,0},{40,8},{48,16},{56,24},{6... | collective-permute-start | bytes 1572872 | tf_op jit(solution)/shard_map/ppermute | solution.py:41
  82.4 7.6 %collective-permute-done.5 = bf16[512,512]{1,0:T(8,128)(2,1)} collective-permute-done((bf16[512,512]{1,0:T(8,128)(2,1)S(1)}, bf16[512,512]{1,0:T(8,128)(2,1)}, u32[]{:S(2)}, u32[]{:S(2)}) %collective-permute-start.5) | collective-permute-done | bytes 524320 | tf_op jit(solution)/shard_map/ppermute | solution.py:38
  90.0 0.1 convert_reduce_fusion
  90.2 0.1 reshape.215
  90.2 0.1 reduce_sum.37
  90.4 0.1 copy.42
  90.5 0.1 reduce.2
  90.6 0.1 iota_add_fusion
  90.7 0.1 add.134
  90.8 0.2 fusion.49
  91.0 0.7 convolution_convert_fusion.4
  91.7 0.1 copy.62
  91.8 0.1 copy.63
  92.0 1.5 fusion.62
  93.5 1.6 convolution_convert_fusion.11
  95.1 1.2 convolution_convert_fusion.5
  96.3 8.2 %all-to-all-start.1 = ((bf16[32,16,512]{2,1,0:T(8,128)(2,1)}), bf16[32,16,512]{2,1,0:T(8,128)(2,1)S(1)}, u32[]{:S(2)}, u32[]{:S(2)}) async-start(bf16[32,16,512]{2,1,0:T(8,128)(2,1)} %bitcast.11), calls=%async_computation.1 | async-start | bytes 1048576 | tf_op jit(solution)/shard_map/all_to_all | solution.py:112
  104.7 2.4 %broadcast_in_dim.85 = bf16[512,4096]{1,0:T(8,128)(2,1)} broadcast(bf16[]{:T(256)} %constant.134.clone.1), dimensions={} | broadcast | bytes 4194306 | tf_op jit(solution)/shard_map/broadcast_in_dim | solution.py:33
  107.2 0.9 constant_dynamic-update-slice_fusion.7
  108.0 3.1 %collective-permute-start.8 = (bf16[512,512]{1,0:T(8,128)(2,1)}, bf16[512,512]{1,0:T(8,128)(2,1)S(1)}, u32[]{:S(2)}, u32[]{:S(2)}) collective-permute-start(bf16[512,512]{1,0:T(8,128)(2,1)} %collective-permute-done.6), channel_id=1, source_target_pairs={{0,224},{8,232},{16,240},{24,248},{32,0},{40,8},{48,16},{56,24},{6... | collective-permute-start | bytes 1572872 | tf_op jit(solution)/shard_map/ppermute | solution.py:41
  111.1 0.9 constant_dynamic-update-slice_fusion.6
  112.0 0.9 constant_dynamic-update-slice_fusion.5
  112.9 1.9 constant_dynamic-update-slice_fusion.4
  114.8 1.9 constant_dynamic-update-slice_fusion.3
  116.7 1.9 constant_dynamic-update-slice_fusion.2
  118.6 9.3 %collective-permute-done.8 = bf16[512,512]{1,0:T(8,128)(2,1)S(1)} collective-permute-done((bf16[512,512]{1,0:T(8,128)(2,1)}, bf16[512,512]{1,0:T(8,128)(2,1)S(1)}, u32[]{:S(2)}, u32[]{:S(2)}) %collective-permute-start.8) | collective-permute-done | bytes 524320 | tf_op jit(solution)/shard_map/ppermute | solution.py:41
  127.9 0.9 constant_dynamic-update-slice_fusion.1
  128.8 0.4 collective-permute-done.9
  129.1 0.9 constant_dynamic-update-slice_fusion
  130.1 5.4 %convolution_convert_fusion.6 = bf16[512,512]{1,0:T(8,128)(2,1)} fusion(bf16[512,4096]{1,0:T(8,128)(2,1)} %constant_dynamic-update-slice_fusion, bf16[256,4096]{1,0:T(8,128)(2,1)} %all-gather.2.cloned.1.call-done, s32[256]{0:T(256)S(1)} %multiply_add_fusion), kind=kOutput, calls=%fused_computation.14 | convolution fusion | flops 1208483840 | bytes 6816768 | tf_op jit(solution)/shard_map/dot_general | solution.py:13
  135.5 8.1 %all-to-all-start.2 = ((bf16[32,16,512]{2,1,0:T(8,128)(2,1)}), bf16[32,16,512]{2,1,0:T(8,128)(2,1)S(1)}, u32[]{:S(2)}, u32[]{:S(2)}) async-start(bf16[32,16,512]{2,1,0:T(8,128)(2,1)} %bitcast.13), calls=%async_computation.3 | async-start | bytes 1048576 | tf_op jit(solution)/shard_map/all_to_all | solution.py:130
  143.6 5.0 %convolution_convert_fusion = bf16[256,4096]{1,0:T(8,128)(2,1)} fusion(bf16[512,4096]{1,0:T(8,128)(2,1)} %constant_dynamic-update-slice_fusion, bf16[512,512]{1,0:T(8,128)(2,1)S(1)} %bitcast.82, s32[256]{0:T(256)S(1)} %multiply_add_fusion), kind=kOutput, calls=%fused_computation.1 | convolution fusion | flops 1209270272 | bytes 6816768 | tf_op jit(solution)/shard_map/dot_general | solution.py:117
  148.7 11.9 %all-to-all-done.2 = bf16[32,16,512]{2,1,0:T(8,128)(2,1)S(1)} async-done(((bf16[32,16,512]{2,1,0:T(8,128)(2,1)}), bf16[32,16,512]{2,1,0:T(8,128)(2,1)S(1)}, u32[]{:S(2)}, u32[]{:S(2)}) %all-to-all-start.2) | async-done | bytes 524320 | tf_op jit(solution)/shard_map/all_to_all | solution.py:130
  160.6 0.3 convolution_convert_fusion.8
  160.9 0.1 copy.47
  161.1 0.1 multiply_reduce_fusion
  161.2 0.3 fusion.5
  161.5 0.2 fusion.6
  161.7 1.6 convolution_convert_fusion.7
  163.3 0.3 fusion.7
  163.7 0.6 convolution_convert_fusion.1
  164.3 43.6 %all_to_all.48 = bf16[32,16,1536]{2,1,0:T(8,128)(2,1)S(1)} all-to-all(bf16[32,16,1536]{2,1,0:T(8,128)(2,1)S(1)} %bitcast.83), channel_id=1, replica_groups=mesh['seq'=32,'head'=8] {'seq'}, dimensions={0} | all-to-all | bytes 3145728 | tf_op jit(solution)/shard_map/all_to_all | solution.py:153
  207.9 0.6 convolution_convert_fusion.3
  208.6 0.9 fusion.60
  (43 shorter events, 0.5 us)
Async XLA Ops:
  7.2 36.4 %copy-start = (s32[32,2,2]{0,2,1:T(2,128)S(1)}, s32[32,2,2]{0,2,1:T(2,128)}, u32[]{:S(2)}) copy-start(s32[32,2,2]{0,2,1:T(2,128)} %param.13) | copy-start | bytes 1540
  10.2 14.6 %copy-start.3 = (bf16[512,128]{1,0:T(8,128)(2,1)S(1)}, bf16[512,128]{1,0:T(8,128)(2,1)}, u32[]{:S(2)}) copy-start(bf16[512,128]{1,0:T(8,128)(2,1)} %param.10) | copy-start | bytes 393220
  13.2 76.8 %all-to-all-start = ((bf16[32,16,1664]{2,1,0:T(8,128)(2,1)}), bf16[32,16,1664]{2,1,0:T(8,128)(2,1)S(1)}, u32[]{:S(2)}, u32[]{:S(2)}) async-start(bf16[32,16,1664]{2,1,0:T(8,128)(2,1)} %bitcast.2), calls=%async_computation | async-start | bytes 3407872 | tf_op jit(solution)/shard_map/all_to_all | solution.py:74
  24.7 105.4 %all-gather.2.cloned.1.call-start = ((), (), s32[]{:S(2)}) async-start(), calls=%async_computation.6 | async-start | bytes 2359296 | tf_op jit(solution)/shard_map/all_gather | solution.py:125
  24.7 8.9 %collective-permute-start = (bf16[512,128]{1,0:T(8,128)(2,1)S(1)}, bf16[512,128]{1,0:T(8,128)(2,1)S(1)}, u32[]{:S(2)}, u32[]{:S(2)}) collective-permute-start(bf16[512,128]{1,0:T(8,128)(2,1)S(1)} %copy-done.3), channel_id=1, source_target_pairs={{0,8},{8,16},{16,24},{24,0},{32,40},{40,48},{48,56},{56,32},{64,72... | collective-permute-start | bytes 393224 | tf_op jit(solution)/shard_map/ppermute | solution.py:38
  26.6 10.6 %collective-permute-start.1 = (bf16[512,128]{1,0:T(8,128)(2,1)S(1)}, bf16[512,128]{1,0:T(8,128)(2,1)S(1)}, u32[]{:S(2)}, u32[]{:S(2)}) collective-permute-start(bf16[512,128]{1,0:T(8,128)(2,1)S(1)} %copy-done.3), channel_id=1, source_target_pairs={{0,24},{8,0},{16,8},{24,16},{32,56},{40,32},{48,40},{56,48},{64,88... | collective-permute-start | bytes 393224 | tf_op jit(solution)/shard_map/ppermute | solution.py:41
  33.7 9.7 %collective-permute-start.2 = (bf16[512,128]{1,0:T(8,128)(2,1)S(1)}, bf16[512,128]{1,0:T(8,128)(2,1)S(1)}, u32[]{:S(2)}, u32[]{:S(2)}) collective-permute-start(bf16[512,128]{1,0:T(8,128)(2,1)S(1)} %collective-permute-done), channel_id=1, source_target_pairs={{0,8},{8,16},{16,24},{24,0},{32,40},{40,48},{48,56},{56,32},{64,72... | collective-permute-start | bytes 393224 | tf_op jit(solution)/shard_map/ppermute | solution.py:38
  43.4 32.3 %collective-permute-start.3 = (bf16[512,512]{1,0:T(8,128)(2,1)S(1)}, bf16[512,512]{1,0:T(8,128)(2,1)S(1)}, u32[]{:S(2)}, u32[]{:S(2)}) collective-permute-start(bf16[512,512]{1,0:T(8,128)(2,1)S(1)} %constant_dynamic-update-slice_fusion.8), channel_id=1, source_target_pairs={{0,32},{8,40},{16,48},{24,56},{32,64},{40,72},{48,80},{56,88},{64,... | collective-permute-start | bytes 1572872 | tf_op jit(solution)/shard_map/ppermute | solution.py:38
  43.8 35.3 %collective-permute-start.4 = (bf16[512,512]{1,0:T(8,128)(2,1)S(1)}, bf16[512,512]{1,0:T(8,128)(2,1)S(1)}, u32[]{:S(2)}, u32[]{:S(2)}) collective-permute-start(bf16[512,512]{1,0:T(8,128)(2,1)S(1)} %constant_dynamic-update-slice_fusion.8), channel_id=1, source_target_pairs={{0,224},{8,232},{16,240},{24,248},{32,0},{40,8},{48,16},{56,24},{6... | collective-permute-start | bytes 1572872 | tf_op jit(solution)/shard_map/ppermute | solution.py:41
  75.7 14.3 %collective-permute-start.5 = (bf16[512,512]{1,0:T(8,128)(2,1)S(1)}, bf16[512,512]{1,0:T(8,128)(2,1)}, u32[]{:S(2)}, u32[]{:S(2)}) collective-permute-start(bf16[512,512]{1,0:T(8,128)(2,1)S(1)} %collective-permute-done.3), channel_id=1, source_target_pairs={{0,32},{8,40},{16,48},{24,56},{32,64},{40,72},{48,80},{56,88},{64,... | collective-permute-start | bytes 1572872 | tf_op jit(solution)/shard_map/ppermute | solution.py:38
  79.0 14.5 %copy-start.4 = (pred[256,256]{0,1:T(8,128)(4,1)}, pred[256,256]{0,1:T(8,128)(4,1)S(1)}, u32[]{:S(2)}) copy-start(pred[256,256]{0,1:T(8,128)(4,1)S(1)} %fusion.38) | copy-start | bytes 196612
  79.1 29.0 %collective-permute-start.6 = (bf16[512,512]{1,0:T(8,128)(2,1)S(1)}, bf16[512,512]{1,0:T(8,128)(2,1)}, u32[]{:S(2)}, u32[]{:S(2)}) collective-permute-start(bf16[512,512]{1,0:T(8,128)(2,1)S(1)} %collective-permute-done.4), channel_id=1, source_target_pairs={{0,224},{8,232},{16,240},{24,248},{32,0},{40,8},{48,16},{56,24},{6... | collective-permute-start | bytes 1572872 | tf_op jit(solution)/shard_map/ppermute | solution.py:41
  90.0 22.0 %collective-permute-start.7 = (bf16[512,512]{1,0:T(8,128)(2,1)}, bf16[512,512]{1,0:T(8,128)(2,1)}, u32[]{:S(2)}, u32[]{:S(2)}) collective-permute-start(bf16[512,512]{1,0:T(8,128)(2,1)} %collective-permute-done.5), channel_id=1, source_target_pairs={{0,32},{8,40},{16,48},{24,56},{32,64},{40,72},{48,80},{56,88},{64,... | collective-permute-start | bytes 1572872 | tf_op jit(solution)/shard_map/ppermute | solution.py:38
  91.7 3.5 %copy-start.1 = (bf16[32,4,8,128]{3,2,1,0:T(8,128)(2,1)}, bf16[32,4,8,128]{3,2,1,0:T(8,128)(2,1)S(1)}, u32[]{:S(2)}) copy-start(bf16[32,4,8,128]{3,2,1,0:T(8,128)(2,1)S(1)} %get-tuple-element.10) | copy-start | bytes 786436
  93.5 2.8 %copy-start.6 = (f32[4,256]{1,0:T(4,128)}, f32[4,256]{1,0:T(4,128)S(1)}, u32[]{:S(2)}) copy-start(f32[4,256]{1,0:T(4,128)S(1)} %get-tuple-element.18) | copy-start | bytes 12292
  96.3 33.8 %all-to-all-start.1 = ((bf16[32,16,512]{2,1,0:T(8,128)(2,1)}), bf16[32,16,512]{2,1,0:T(8,128)(2,1)S(1)}, u32[]{:S(2)}, u32[]{:S(2)}) async-start(bf16[32,16,512]{2,1,0:T(8,128)(2,1)} %bitcast.11), calls=%async_computation.1 | async-start | bytes 1048576 | tf_op jit(solution)/shard_map/all_to_all | solution.py:112
  108.0 19.8 %collective-permute-start.8 = (bf16[512,512]{1,0:T(8,128)(2,1)}, bf16[512,512]{1,0:T(8,128)(2,1)S(1)}, u32[]{:S(2)}, u32[]{:S(2)}) collective-permute-start(bf16[512,512]{1,0:T(8,128)(2,1)} %collective-permute-done.6), channel_id=1, source_target_pairs={{0,224},{8,232},{16,240},{24,248},{32,0},{40,8},{48,16},{56,24},{6... | collective-permute-start | bytes 1572872 | tf_op jit(solution)/shard_map/ppermute | solution.py:41
  112.0 17.1 %collective-permute-start.9 = (bf16[512,512]{1,0:T(8,128)(2,1)}, bf16[512,512]{1,0:T(8,128)(2,1)S(1)}, u32[]{:S(2)}, u32[]{:S(2)}) collective-permute-start(bf16[512,512]{1,0:T(8,128)(2,1)} %collective-permute-done.7), channel_id=1, source_target_pairs={{0,32},{8,40},{16,48},{24,56},{32,64},{40,72},{48,80},{56,88},{64,... | collective-permute-start | bytes 1572872 | tf_op jit(solution)/shard_map/ppermute | solution.py:38
  135.5 25.1 %all-to-all-start.2 = ((bf16[32,16,512]{2,1,0:T(8,128)(2,1)}), bf16[32,16,512]{2,1,0:T(8,128)(2,1)S(1)}, u32[]{:S(2)}, u32[]{:S(2)}) async-start(bf16[32,16,512]{2,1,0:T(8,128)(2,1)} %bitcast.13), calls=%async_computation.3 | async-start | bytes 1048576 | tf_op jit(solution)/shard_map/all_to_all | solution.py:130
  143.6 65.9 %reduce-scatter.2.cloned.1.call-start = ((), (), s32[]{:S(2)}) async-start(), calls=%async_computation.5 | async-start | bytes 2359296 | tf_op jit(solution)/shard_map/reduce_scatter | solution.py:119
  148.7 12.5 %copy-start.2 = (bf16[32,4,8,128]{3,2,1,0:T(8,128)(2,1)S(1)}, bf16[32,4,8,128]{3,2,1,0:T(8,128)(2,1)}, u32[]{:S(2)}) copy-start(bf16[32,4,8,128]{3,2,1,0:T(8,128)(2,1)} %copy-done.1) | copy-start | bytes 786436
  148.7 12.5 %copy-start.5 = (f32[4,256,256]{1,2,0:T(8,128)S(1)}, f32[4,256,256]{1,2,0:T(8,128)}, u32[]{:S(2)}) copy-start(f32[4,256,256]{1,2,0:T(8,128)} %get-tuple-element.19) | copy-start | bytes 3145732
  148.7 12.5 %copy-start.7 = (f32[4,256]{1,0:T(4,128)S(1)}, f32[4,256]{1,0:T(4,128)}, u32[]{:S(2)}) copy-start(f32[4,256]{1,0:T(4,128)} %copy-done.6) | copy-start | bytes 12292
Sparse Core Ops, SparseCore 0:
  43.6 27.9 all-gather.1
  148.8 32.7 reduce-scatter.1

commit v7 on v6

--- a/solution.py
+++ b/solution.py
@@ -19,7 +19,7 @@
     ).astype(rows.dtype)
 
 
-def ring_gather_cols(block, axis_name, ny, nz):
+def ring_gather_cols(block, axis_name, ny, nz, z_first=False):
     index = lax.axis_index(axis_name)
     y = index % ny
     z = index // ny
@@ -42,8 +42,13 @@
                 out = lax.dynamic_update_slice(out, bwd, (0, ((pos + step) % count) * width))
         return out
 
-    row = ring(block, y, ny, lambda d: perm(d, 0), cols, ny * cols)
-    return ring(row, z, nz, lambda d: perm(0, d), ny * cols, n * cols)
+    if not z_first:
+        row = ring(block, y, ny, lambda d: perm(d, 0), cols, ny * cols)
+        return ring(row, z, nz, lambda d: perm(0, d), ny * cols, n * cols)
+    row = ring(block, z, nz, lambda d: perm(0, d), cols, nz * cols)
+    full = ring(row, y, ny, lambda d: perm(d, 0), nz * cols, n * cols)
+    rows = block.shape[0]
+    return full.reshape(rows, ny, nz, cols).transpose(0, 2, 1, 3).reshape(rows, n * cols)
 
 
 def on_device(queries, key_rows, value_rows, out_weight, grad_output, cluster_ids, block_pattern):
@@ -68,7 +73,14 @@
     ).astype(jnp.bfloat16)
 
     ring_y = 4 if groups % 4 == 0 else 1
-    full_weight = ring_gather_cols(out_weight, "seq", ring_y, groups // ring_y)
+    half_rows = out_weight.shape[0] // 2
+    full_weight = jnp.concatenate(
+        [
+            ring_gather_cols(out_weight[:half_rows], "seq", ring_y, groups // ring_y),
+            ring_gather_cols(out_weight[half_rows:], "seq", ring_y, groups // ring_y, True),
+        ],
+        axis=0,
+    )
     live_flag = jnp.ones((tokens, HD), queries.dtype)
     qkv = jnp.concatenate([queries, key_rows, value_rows, live_flag], axis=1)
     qkv_in = lax.all_to_all(select_rows(to_slot, qkv), "seq", 0, 0, tiled=True)

time: 217 us -> 209 us (0.963)
  waiting for transfers between devices: 70.2 us -> 59.1 us
  starting transfers between devices: 43.7 us -> 52.4 us
  blocking collectives: 43.6 us -> 35.2 us
  other arithmetic: 6.25 us -> 10.3 us
  local copies, waits for them, and re-layouts: 15.5 us -> 12.7 us
    ppermute x4 -> x8, waiting for transfers between devices: 11 us -> 0.02 us  [ring(): bwd = lax.ppermute(bwd, axis_name, step_perm(-1))]
    ppermute x4 -> x8, starting transfers between devices: 12.1 us -> 21.8 us  [ring(): bwd = lax.ppermute(bwd, axis_name, step_perm(-1))]
    all_to_all x1, blocking collectives: 43.6 us -> 35.2 us  [on_device(): lax.all_to_all(select_rows_t(to_rank, grads_c), 'seq', 0, 0, tiled=True)]
    all_to_all x1, waiting for transfers between devices: 0.01 us -> 3.83 us  [on_device(): lax.all_to_all(select_rows_t(to_rank, attn_c.reshape(ranks, width)), 'seq...]
    all_to_all x1, waiting for transfers between devices: 11.9 us -> 8.5 us  [on_device(): lax.all_to_all(select_rows(to_slot, grad_attention), 'seq', 0, 0, tiled=T...]
    broadcast_in_dim x2, local copies, waits for them, and re-layouts: 2.47 us -> 0.06 us  [ring(): out = jnp.zeros((piece.shape[0], total), piece.dtype)]
    concatenate x0 -> x1, other arithmetic: none -> 2.26 us  [on_device(): jnp.concatenate([ring_gather_cols(out_weight[:half_rows], 'seq', ring_y,...]
    all_to_all x1, starting transfers between devices: 8.1 us -> 5.9 us  [on_device(): lax.all_to_all(select_rows(to_slot, grad_attention), 'seq', 0, 0, tiled=T...]
  transfers between devices with their start and end apart: 15 -> 25, of which waited for: 8 -> 7; matrix products, arithmetic and copies ran while one was open for 15% -> 16% of each run, Pallas kernels for 0% -> 0%
where the time goes in v7:
time: 209 us; the launch traced here: 208 us
  waiting for transfers between devices  59.1 us (28%)
  starting transfers between devices  52.4 us (25%)
  blocking collectives  35.2 us (17%)
  matrix products  23.3 us (11%)
  between operations  14.9 us (7%)
  local copies, waits for them, and re-layouts  12.7 us (6%)
  other arithmetic  10.3 us (5%)
    ppermute x12, waiting for transfers between devices, ring(): fwd = lax.ppermute(fwd, axis_name, step_perm(1))  46.7 us
    all_to_all x1, blocking collectives, on_device(): lax.all_to_all(select_rows_t(to_rank, grads_c), 'seq', 0, 0, tiled=True)  35.2 us
    ppermute x8, starting transfers between devices, ring(): bwd = lax.ppermute(bwd, axis_name, step_perm(-1))  21.8 us
    all_to_all x1, starting transfers between devices, on_device(): qkv_in = lax.all_to_all(select_rows(to_slot, qkv), 'seq', 0, 0, tiled=True)  11.7 us
    dot_general x4, matrix products, select_rows(): jnp.dot(onehot, rows, preferred_element_type=jnp.float32).astype(rows.dtype)  10.8 us
    all_to_all x1, waiting for transfers between devices, on_device(): lax.all_to_all(select_rows(to_slot, grad_attention), 'seq', 0, 0, tiled=T...  8.5 us
    all_to_all x1, starting transfers between devices, on_device(): lax.all_to_all(select_rows_t(to_rank, attn_c.reshape(ranks, width)), 'seq...  7.11 us
    dynamic_update_slice x12, local copies, waits for them, and re-layouts, ring(): out = lax.dynamic_update_slice(out, fwd, (0, (pos - step) % count * width))  6.03 us
  transfers between devices with their start and end apart: 25, of which 7 were waited for; matrix products, arithmetic and copies ran while one was open for 16% of the time, Pallas kernels for 0%

profile of v7, /device:TPU:4, one launch (start us, length us, event | category | flops | bytes accessed | tf_op | source)
XLA Modules:
  0.0 207.9 jit_solution(12469129817336957259)
XLA Ops:
  7.2 0.7 fusion.48
  7.9 0.6 reduce-window.18
  8.4 0.2 slice_reduce_fusion
  8.7 0.8 fusion.47
  9.5 0.7 multiply_add_fusion
  10.2 3.0 %convolution_convert_fusion.2 = bf16[512,1664]{1,0:T(8,128)(2,1)} fusion(bf16[256,512]{1,0:T(8,128)(2,1)} %param.9, bf16[256,512]{1,0:T(8,128)(2,1)} %param.8, bf16[256,512]{1,0:T(8,128)(2,1)} %param.7, bf16[1664]{0:T(1024)(128)(2,1)S(1)} %pad.8.clone, s32[256]{0:T(256)S(1)} %multiply_add_fusion), kind=kOutput, calls=%fused_computation.4 | convolution fusion | flops 440598528 | bytes 2494720 | tf_op jit(solution)/shard_map/dot_general | solution.py:13
  13.1 11.7 %all-to-all-start = ((bf16[32,16,1664]{2,1,0:T(8,128)(2,1)}), bf16[32,16,1664]{2,1,0:T(8,128)(2,1)}, u32[]{:S(2)}, u32[]{:S(2)}) async-start(bf16[32,16,1664]{2,1,0:T(8,128)(2,1)} %bitcast.2), calls=%async_computation | async-start | bytes 3407872 | tf_op jit(solution)/shard_map/all_to_all | solution.py:86
  25.0 1.8 collective-permute-start
  26.8 1.5 collective-permute-start.1
  28.5 1.8 collective-permute-start.10
  30.3 1.5 collective-permute-start.11
  32.2 0.2 fusion.50
  32.4 0.6 fusion.62
  33.0 2.6 %broadcast_select_fusion = (s32[256]{0:T(256)S(1)}, s32[256]{0:T(256)S(1)}) fusion(s32[]{:T(128)} %bitcast.8, s32[]{:T(128)} %bitcast.7, s32[]{:T(128)} %bitcast.6, s32[]{:T(128)} %bitcast.5), kind=kLoop, calls=%fused_computation.109 | loop fusion | flops 2816 | bytes 2064 | tf_op jit(solution)/shard_map/jit(_where)/select_n | solution.py:109
  35.6 0.1 fusion.38
  35.8 0.6 collective-permute-start.2
  36.4 28.9 %collective-permute-done.10 = bf16[256,128]{0,1:T(8,128)(2,1)S(1)} collective-permute-done((bf16[256,128]{0,1:T(8,128)(2,1)S(1)}, bf16[256,128]{0,1:T(8,128)(2,1)S(1)}, u32[]{:S(2)}, u32[]{:S(2)}) %collective-permute-start.10) | collective-permute-done | bytes 65568 | tf_op jit(solution)/shard_map/ppermute | solution.py:38
  65.4 3.2 %collective-permute-start.13 = (bf16[256,128]{0,1:T(8,128)(2,1)S(1)}, bf16[256,128]{0,1:T(8,128)(2,1)S(1)}, u32[]{:S(2)}, u32[]{:S(2)}) collective-permute-start(bf16[256,128]{0,1:T(8,128)(2,1)S(1)} %collective-permute-done.11), channel_id=1, source_target_pairs={{0,224},{8,232},{16,240},{24,248},{32,0},{40,8},{48,16},{56,24},{6... | collective-permute-start | bytes 196616 | tf_op jit(solution)/shard_map/ppermute | solution.py:41
  68.8 3.2 %collective-permute-start.4 = (bf16[256,512]{0,1:T(8,128)(2,1)S(1)}, bf16[256,512]{0,1:T(8,128)(2,1)S(1)}, u32[]{:S(2)}, u32[]{:S(2)}) collective-permute-start(bf16[256,512]{0,1:T(8,128)(2,1)S(1)} %constant_dynamic-update-slice_fusion.20), channel_id=1, source_target_pairs={{0,224},{8,232},{16,240},{24,248},{32,0},{40,8},{48,16},{56,24},{6... | collective-permute-start | bytes 786440 | tf_op jit(solution)/shard_map/ppermute | solution.py:41
  72.1 3.2 %collective-permute-start.15 = (bf16[256,128]{0,1:T(8,128)(2,1)S(1)}, bf16[256,128]{0,1:T(8,128)(2,1)S(1)}, u32[]{:S(2)}, u32[]{:S(2)}) collective-permute-start(bf16[256,128]{0,1:T(8,128)(2,1)S(1)} %collective-permute-done.13), channel_id=1, source_target_pairs={{0,224},{8,232},{16,240},{24,248},{32,0},{40,8},{48,16},{56,24},{6... | collective-permute-start | bytes 196616 | tf_op jit(solution)/shard_map/ppermute | solution.py:41
  75.3 0.1 broadcast.206.clone.1
  75.5 2.4 %collective-permute-done.14 = bf16[256,128]{0,1:T(8,128)(2,1)S(1)} collective-permute-done((bf16[256,128]{0,1:T(8,128)(2,1)S(1)}, bf16[256,128]{0,1:T(8,128)(2,1)S(1)}, u32[]{:S(2)}, u32[]{:S(2)}) %collective-permute-start.14) | collective-permute-done | bytes 65568 | tf_op jit(solution)/shard_map/ppermute | solution.py:38
  77.9 5.4 %collective-permute-done.16 = bf16[256,128]{0,1:T(8,128)(2,1)S(1)} collective-permute-done((bf16[256,128]{0,1:T(8,128)(2,1)S(1)}, bf16[256,128]{0,1:T(8,128)(2,1)S(1)}, u32[]{:S(2)}, u32[]{:S(2)}) %collective-permute-start.16) | collective-permute-done | bytes 65568 | tf_op jit(solution)/shard_map/ppermute | solution.py:38
  83.4 1.1 collective-permute-start.17
  84.5 2.4 %collective-permute-start.18 = (bf16[256,1024]{0,1:T(8,128)(2,1)S(1)}, bf16[256,1024]{0,1:T(8,128)(2,1)S(1)}, u32[]{:S(2)}, u32[]{:S(2)}) collective-permute-start(bf16[256,1024]{0,1:T(8,128)(2,1)S(1)} %constant_dynamic-update-slice_fusion.4), channel_id=1, source_target_pairs={{0,24},{8,0},{16,8},{24,16},{32,56},{40,32},{48,40},{56,48},{64,88... | collective-permute-start | bytes 1572872 | tf_op jit(solution)/shard_map/ppermute | solution.py:41
  86.9 3.2 %collective-permute-start.6 = (bf16[256,512]{0,1:T(8,128)(2,1)S(1)}, bf16[256,512]{0,1:T(8,128)(2,1)S(1)}, u32[]{:S(2)}, u32[]{:S(2)}) collective-permute-start(bf16[256,512]{0,1:T(8,128)(2,1)S(1)} %collective-permute-done.4), channel_id=1, source_target_pairs={{0,224},{8,232},{16,240},{24,248},{32,0},{40,8},{48,16},{56,24},{6... | collective-permute-start | bytes 786440 | tf_op jit(solution)/shard_map/ppermute | solution.py:41
  90.1 0.1 broadcast.206.clone
  90.3 5.4 %collective-permute-done.5 = bf16[256,512]{0,1:T(8,128)(2,1)S(1)} collective-permute-done((bf16[256,512]{0,1:T(8,128)(2,1)S(1)}, bf16[256,512]{0,1:T(8,128)(2,1)S(1)}, u32[]{:S(2)}, u32[]{:S(2)}) %collective-permute-start.5) | collective-permute-done | bytes 262176 | tf_op jit(solution)/shard_map/ppermute | solution.py:38
  95.7 3.5 %collective-permute-start.8 = (bf16[256,512]{0,1:T(8,128)(2,1)S(1)}, bf16[256,512]{0,1:T(8,128)(2,1)}, u32[]{:S(2)}, u32[]{:S(2)}) collective-permute-start(bf16[256,512]{0,1:T(8,128)(2,1)S(1)} %collective-permute-done.6), channel_id=1, source_target_pairs={{0,224},{8,232},{16,240},{24,248},{32,0},{40,8},{48,16},{56,24},{6... | collective-permute-start | bytes 786440 | tf_op jit(solution)/shard_map/ppermute | solution.py:41
  99.4 1.5 constant_dynamic-update-slice_fusion.2
  101.0 4.6 %collective-permute-done.7 = bf16[256,512]{0,1:T(8,128)(2,1)} collective-permute-done((bf16[256,512]{0,1:T(8,128)(2,1)S(1)}, bf16[256,512]{0,1:T(8,128)(2,1)}, u32[]{:S(2)}, u32[]{:S(2)}) %collective-permute-start.7) | collective-permute-done | bytes 262176 | tf_op jit(solution)/shard_map/ppermute | solution.py:38
  105.5 1.1 convert_reduce_fusion
  106.7 0.1 reduce_sum.37
  107.2 1.1 fusion.49
  108.3 2.1 %convolution_convert_fusion.4 = bf16[256,1664]{1,0:T(8,128)(2,1)S(1)} fusion(bf16[512,1664]{1,0:T(8,128)(2,1)} %bitcast.3, s32[512]{0:T(512)S(1)} %add.185, pred[512]{0:T(512)(128)(4,1)S(1)} %fusion.49), kind=kOutput, calls=%fused_computation.6 | convolution fusion | flops 436895744 | bytes 2558464 | tf_op jit(solution)/shard_map/dot_general | solution.py:13
  110.5 0.1 copy.69
  110.6 0.1 copy.70
  110.7 1.5 fusion.63
  112.3 0.8 convolution_convert_fusion.11
  113.1 1.1 convolution_convert_fusion.5
  114.2 7.1 %all-to-all-start.1 = ((bf16[32,16,512]{2,1,0:T(8,128)(2,1)}), bf16[32,16,512]{2,1,0:T(8,128)(2,1)S(1)}, u32[]{:S(2)}, u32[]{:S(2)}) async-start(bf16[32,16,512]{2,1,0:T(8,128)(2,1)} %bitcast.97), calls=%async_computation.1 | async-start | bytes 1048576 | tf_op jit(solution)/shard_map/all_to_all | solution.py:124
  121.3 1.7 constant_dynamic-update-slice_fusion.14
  123.0 1.7 constant_dynamic-update-slice_fusion.13
  124.7 1.7 constant_dynamic-update-slice_fusion.12
  126.4 1.1 constant_dynamic-update-slice_fusion
  127.5 0.1 copy.51
  127.6 1.4 copy-done.2
  129.1 2.3 %pad_maximum_fusion = bf16[512,4096]{0,1:T(8,128)(2,1)} fusion(bf16[256,4096]{0,1:T(8,128)(2,1)S(1)} %bitcast.83, bf16[256,4096]{0,1:T(8,128)(2,1)S(1)} %copy-done.2), kind=kLoop, calls=%fused_computation.2 | loop fusion | flops 8388608 | bytes 8388608 | tf_op jit(solution)/shard_map/concatenate | solution.py:77
  131.3 3.8 %all-to-all-done.1 = bf16[32,16,512]{2,1,0:T(8,128)(2,1)S(1)} async-done(((bf16[32,16,512]{2,1,0:T(8,128)(2,1)}), bf16[32,16,512]{2,1,0:T(8,128)(2,1)S(1)}, u32[]{:S(2)}, u32[]{:S(2)}) %all-to-all-start.1) | async-done | bytes 524320 | tf_op jit(solution)/shard_map/all_to_all | solution.py:124
  135.2 5.4 %convolution_convert_fusion.6 = bf16[512,512]{1,0:T(8,128)(2,1)} fusion(bf16[512,4096]{0,1:T(8,128)(2,1)} %pad_maximum_fusion, bf16[256,4096]{1,0:T(8,128)(2,1)} %all-gather.2.cloned.1.call-done, s32[256]{0:T(256)S(1)} %multiply_add_fusion), kind=kOutput, calls=%fused_computation.15 | convolution fusion | flops 1208483840 | bytes 6816768 | tf_op jit(solution)/shard_map/dot_general | solution.py:13
  140.6 5.9 %all-to-all-start.2 = ((bf16[32,16,512]{2,1,0:T(8,128)(2,1)}), bf16[32,16,512]{2,1,0:T(8,128)(2,1)S(1)}, u32[]{:S(2)}, u32[]{:S(2)}) async-start(bf16[32,16,512]{2,1,0:T(8,128)(2,1)} %bitcast.16), calls=%async_computation.3 | async-start | bytes 1048576 | tf_op jit(solution)/shard_map/all_to_all | solution.py:142
  146.5 0.3 reduce-scatter.2.cloned.1.call-start
  146.7 5.0 %convolution_convert_fusion = bf16[256,4096]{1,0:T(8,128)(2,1)} fusion(bf16[512,4096]{0,1:T(8,128)(2,1)} %pad_maximum_fusion, bf16[512,512]{1,0:T(8,128)(2,1)S(1)} %bitcast.85, s32[256]{0:T(256)S(1)} %multiply_add_fusion), kind=kOutput, calls=%fused_computation.1 | convolution fusion | flops 1209270272 | bytes 6816768 | tf_op jit(solution)/shard_map/dot_general | solution.py:129
  151.8 8.5 %all-to-all-done.2 = bf16[32,16,512]{2,1,0:T(8,128)(2,1)S(1)} async-done(((bf16[32,16,512]{2,1,0:T(8,128)(2,1)}), bf16[32,16,512]{2,1,0:T(8,128)(2,1)S(1)}, u32[]{:S(2)}, u32[]{:S(2)}) %all-to-all-start.2) | async-done | bytes 524320 | tf_op jit(solution)/shard_map/all_to_all | solution.py:142
  160.3 0.3 convolution_convert_fusion.8
  160.6 0.1 copy.52
  160.9 1.5 fusion.5
  162.4 0.2 fusion.6
  162.6 0.8 convolution_convert_fusion.7
  163.4 0.3 fusion.7
  163.7 0.6 convolution_convert_fusion.1
  164.4 35.2 %all_to_all.48 = bf16[32,16,1536]{2,1,0:T(8,128)(2,1)S(1)} all-to-all(bf16[32,16,1536]{2,1,0:T(8,128)(2,1)S(1)} %bitcast.86), channel_id=1, replica_groups=mesh['seq'=32,'head'=8] {'seq'}, dimensions={0} | all-to-all | bytes 3145728 | tf_op jit(solution)/shard_map/all_to_all | solution.py:165
  199.5 0.6 convolution_convert_fusion.3
  200.2 0.9 fusion.60
  (82 shorter events, 1.7 us)
Async XLA Ops:
  7.2 25.0 %copy-start = (s32[32,2,2]{0,2,1:T(2,128)S(1)}, s32[32,2,2]{0,2,1:T(2,128)}, u32[]{:S(2)}) copy-start(s32[32,2,2]{0,2,1:T(2,128)} %param.13) | copy-start | bytes 1540
  13.1 11.8 %copy-start.7 = (bf16[512,128]{1,0:T(8,128)(2,1)S(1)}, bf16[512,128]{1,0:T(8,128)(2,1)}, u32[]{:S(2)}) copy-start(bf16[512,128]{1,0:T(8,128)(2,1)} %param.10) | copy-start | bytes 393220
  13.1 92.4 %all-to-all-start = ((bf16[32,16,1664]{2,1,0:T(8,128)(2,1)}), bf16[32,16,1664]{2,1,0:T(8,128)(2,1)}, u32[]{:S(2)}, u32[]{:S(2)}) async-start(bf16[32,16,1664]{2,1,0:T(8,128)(2,1)} %bitcast.2), calls=%async_computation | async-start | bytes 3407872 | tf_op jit(solution)/shard_map/all_to_all | solution.py:86
  24.9 110.3 %all-gather.2.cloned.1.call-start = ((), (), s32[]{:S(2)}) async-start(), calls=%async_computation.6 | async-start | bytes 2359296 | tf_op jit(solution)/shard_map/all_gather | solution.py:137
  25.0 10.8 %collective-permute-start = (bf16[256,128]{0,1:T(8,128)(2,1)S(1)}, bf16[256,128]{0,1:T(8,128)(2,1)S(1)}, u32[]{:S(2)}, u32[]{:S(2)}) collective-permute-start(bf16[256,128]{0,1:T(8,128)(2,1)S(1)} %copy.67), channel_id=1, source_target_pairs={{0,8},{8,16},{16,24},{24,0},{32,40},{40,48},{48,56},{56,32},{64,72... | collective-permute-start | bytes 196616 | tf_op jit(solution)/shard_map/ppermute | solution.py:38
  26.8 41.8 %collective-permute-start.1 = (bf16[256,128]{0,1:T(8,128)(2,1)S(1)}, bf16[256,128]{0,1:T(8,128)(2,1)S(1)}, u32[]{:S(2)}, u32[]{:S(2)}) collective-permute-start(bf16[256,128]{0,1:T(8,128)(2,1)S(1)} %copy.67), channel_id=1, source_target_pairs={{0,24},{8,0},{16,8},{24,16},{32,56},{40,32},{48,40},{56,48},{64,88... | collective-permute-start | bytes 196616 | tf_op jit(solution)/shard_map/ppermute | solution.py:41
  28.5 36.9 %collective-permute-start.10 = (bf16[256,128]{0,1:T(8,128)(2,1)S(1)}, bf16[256,128]{0,1:T(8,128)(2,1)S(1)}, u32[]{:S(2)}, u32[]{:S(2)}) collective-permute-start(bf16[256,128]{0,1:T(8,128)(2,1)S(1)} %copy.68), channel_id=1, source_target_pairs={{0,32},{8,40},{16,48},{24,56},{32,64},{40,72},{48,80},{56,88},{64,... | collective-permute-start | bytes 196616 | tf_op jit(solution)/shard_map/ppermute | solution.py:38
  30.3 35.1 %collective-permute-start.11 = (bf16[256,128]{0,1:T(8,128)(2,1)S(1)}, bf16[256,128]{0,1:T(8,128)(2,1)S(1)}, u32[]{:S(2)}, u32[]{:S(2)}) collective-permute-start(bf16[256,128]{0,1:T(8,128)(2,1)S(1)} %copy.68), channel_id=1, source_target_pairs={{0,224},{8,232},{16,240},{24,248},{32,0},{40,8},{48,16},{56,24},{6... | collective-permute-start | bytes 196616 | tf_op jit(solution)/shard_map/ppermute | solution.py:41
  35.8 32.9 %collective-permute-start.2 = (bf16[256,128]{0,1:T(8,128)(2,1)S(1)}, bf16[256,128]{0,1:T(8,128)(2,1)S(1)}, u32[]{:S(2)}, u32[]{:S(2)}) collective-permute-start(bf16[256,128]{0,1:T(8,128)(2,1)S(1)} %collective-permute-done), channel_id=1, source_target_pairs={{0,8},{8,16},{16,24},{24,0},{32,40},{40,48},{48,56},{56,32},{64,72... | collective-permute-start | bytes 196616 | tf_op jit(solution)/shard_map/ppermute | solution.py:38
  65.4 6.7 %collective-permute-start.12 = (bf16[256,128]{0,1:T(8,128)(2,1)S(1)}, bf16[256,128]{0,1:T(8,128)(2,1)S(1)}, u32[]{:S(2)}, u32[]{:S(2)}) collective-permute-start(bf16[256,128]{0,1:T(8,128)(2,1)S(1)} %collective-permute-done.10), channel_id=1, source_target_pairs={{0,32},{8,40},{16,48},{24,56},{32,64},{40,72},{48,80},{56,88},{64,... | collective-permute-start | bytes 196616 | tf_op jit(solution)/shard_map/ppermute | solution.py:38
  65.4 6.7 %collective-permute-start.13 = (bf16[256,128]{0,1:T(8,128)(2,1)S(1)}, bf16[256,128]{0,1:T(8,128)(2,1)S(1)}, u32[]{:S(2)}, u32[]{:S(2)}) collective-permute-start(bf16[256,128]{0,1:T(8,128)(2,1)S(1)} %collective-permute-done.11), channel_id=1, source_target_pairs={{0,224},{8,232},{16,240},{24,248},{32,0},{40,8},{48,16},{56,24},{6... | collective-permute-start | bytes 196616 | tf_op jit(solution)/shard_map/ppermute | solution.py:41
  68.7 18.1 %collective-permute-start.3 = (bf16[256,512]{0,1:T(8,128)(2,1)S(1)}, bf16[256,512]{0,1:T(8,128)(2,1)S(1)}, u32[]{:S(2)}, u32[]{:S(2)}) collective-permute-start(bf16[256,512]{0,1:T(8,128)(2,1)S(1)} %constant_dynamic-update-slice_fusion.20), channel_id=1, source_target_pairs={{0,32},{8,40},{16,48},{24,56},{32,64},{40,72},{48,80},{56,88},{64,... | collective-permute-start | bytes 786440 | tf_op jit(solution)/shard_map/ppermute | solution.py:38
  68.8 18.0 %collective-permute-start.4 = (bf16[256,512]{0,1:T(8,128)(2,1)S(1)}, bf16[256,512]{0,1:T(8,128)(2,1)S(1)}, u32[]{:S(2)}, u32[]{:S(2)}) collective-permute-start(bf16[256,512]{0,1:T(8,128)(2,1)S(1)} %constant_dynamic-update-slice_fusion.20), channel_id=1, source_target_pairs={{0,224},{8,232},{16,240},{24,248},{32,0},{40,8},{48,16},{56,24},{6... | collective-permute-start | bytes 786440 | tf_op jit(solution)/shard_map/ppermute | solution.py:41
  72.1 5.8 %collective-permute-start.14 = (bf16[256,128]{0,1:T(8,128)(2,1)S(1)}, bf16[256,128]{0,1:T(8,128)(2,1)S(1)}, u32[]{:S(2)}, u32[]{:S(2)}) collective-permute-start(bf16[256,128]{0,1:T(8,128)(2,1)S(1)} %collective-permute-done.12), channel_id=1, source_target_pairs={{0,32},{8,40},{16,48},{24,56},{32,64},{40,72},{48,80},{56,88},{64,... | collective-permute-start | bytes 196616 | tf_op jit(solution)/shard_map/ppermute | solution.py:38
  72.1 5.8 %collective-permute-start.15 = (bf16[256,128]{0,1:T(8,128)(2,1)S(1)}, bf16[256,128]{0,1:T(8,128)(2,1)S(1)}, u32[]{:S(2)}, u32[]{:S(2)}) collective-permute-start(bf16[256,128]{0,1:T(8,128)(2,1)S(1)} %collective-permute-done.13), channel_id=1, source_target_pairs={{0,224},{8,232},{16,240},{24,248},{32,0},{40,8},{48,16},{56,24},{6... | collective-permute-start | bytes 196616 | tf_op jit(solution)/shard_map/ppermute | solution.py:41
  77.9 5.5 %collective-permute-start.16 = (bf16[256,128]{0,1:T(8,128)(2,1)S(1)}, bf16[256,128]{0,1:T(8,128)(2,1)S(1)}, u32[]{:S(2)}, u32[]{:S(2)}) collective-permute-start(bf16[256,128]{0,1:T(8,128)(2,1)S(1)} %collective-permute-done.14), channel_id=1, source_target_pairs={{0,32},{8,40},{16,48},{24,56},{32,64},{40,72},{48,80},{56,88},{64,... | collective-permute-start | bytes 196616 | tf_op jit(solution)/shard_map/ppermute | solution.py:38
  83.4 16.0 %collective-permute-start.17 = (bf16[256,1024]{0,1:T(8,128)(2,1)S(1)}, bf16[256,1024]{0,1:T(8,128)(2,1)}, u32[]{:S(2)}, u32[]{:S(2)}) collective-permute-start(bf16[256,1024]{0,1:T(8,128)(2,1)S(1)} %constant_dynamic-update-slice_fusion.4), channel_id=1, source_target_pairs={{0,8},{8,16},{16,24},{24,0},{32,40},{40,48},{48,56},{56,32},{64,72... | collective-permute-start | bytes 1572872 | tf_op jit(solution)/shard_map/ppermute | solution.py:38
  84.5 16.4 %collective-permute-start.18 = (bf16[256,1024]{0,1:T(8,128)(2,1)S(1)}, bf16[256,1024]{0,1:T(8,128)(2,1)S(1)}, u32[]{:S(2)}, u32[]{:S(2)}) collective-permute-start(bf16[256,1024]{0,1:T(8,128)(2,1)S(1)} %constant_dynamic-update-slice_fusion.4), channel_id=1, source_target_pairs={{0,24},{8,0},{16,8},{24,16},{32,56},{40,32},{48,40},{56,48},{64,88... | collective-permute-start | bytes 1572872 | tf_op jit(solution)/shard_map/ppermute | solution.py:41
  86.8 8.9 %collective-permute-start.5 = (bf16[256,512]{0,1:T(8,128)(2,1)S(1)}, bf16[256,512]{0,1:T(8,128)(2,1)S(1)}, u32[]{:S(2)}, u32[]{:S(2)}) collective-permute-start(bf16[256,512]{0,1:T(8,128)(2,1)S(1)} %collective-permute-done.3), channel_id=1, source_target_pairs={{0,32},{8,40},{16,48},{24,56},{32,64},{40,72},{48,80},{56,88},{64,... | collective-permute-start | bytes 786440 | tf_op jit(solution)/shard_map/ppermute | solution.py:38
  86.9 8.9 %collective-permute-start.6 = (bf16[256,512]{0,1:T(8,128)(2,1)S(1)}, bf16[256,512]{0,1:T(8,128)(2,1)S(1)}, u32[]{:S(2)}, u32[]{:S(2)}) collective-permute-start(bf16[256,512]{0,1:T(8,128)(2,1)S(1)} %collective-permute-done.4), channel_id=1, source_target_pairs={{0,224},{8,232},{16,240},{24,248},{32,0},{40,8},{48,16},{56,24},{6... | collective-permute-start | bytes 786440 | tf_op jit(solution)/shard_map/ppermute | solution.py:41
  95.7 9.8 %collective-permute-start.7 = (bf16[256,512]{0,1:T(8,128)(2,1)S(1)}, bf16[256,512]{0,1:T(8,128)(2,1)}, u32[]{:S(2)}, u32[]{:S(2)}) collective-permute-start(bf16[256,512]{0,1:T(8,128)(2,1)S(1)} %collective-permute-done.5), channel_id=1, source_target_pairs={{0,32},{8,40},{16,48},{24,56},{32,64},{40,72},{48,80},{56,88},{64,... | collective-permute-start | bytes 786440 | tf_op jit(solution)/shard_map/ppermute | solution.py:38
  95.7 27.3 %collective-permute-start.8 = (bf16[256,512]{0,1:T(8,128)(2,1)S(1)}, bf16[256,512]{0,1:T(8,128)(2,1)}, u32[]{:S(2)}, u32[]{:S(2)}) collective-permute-start(bf16[256,512]{0,1:T(8,128)(2,1)S(1)} %collective-permute-done.6), channel_id=1, source_target_pairs={{0,224},{8,232},{16,240},{24,248},{32,0},{40,8},{48,16},{56,24},{6... | collective-permute-start | bytes 786440 | tf_op jit(solution)/shard_map/ppermute | solution.py:41
  99.3 1.7 copy-start.1
  99.3 27.1 %collective-permute-start.19 = (bf16[256,1024]{0,1:T(8,128)(2,1)}, bf16[256,1024]{0,1:T(8,128)(2,1)}, u32[]{:S(2)}, u32[]{:S(2)}) collective-permute-start(bf16[256,1024]{0,1:T(8,128)(2,1)} %collective-permute-done.17), channel_id=1, source_target_pairs={{0,8},{8,16},{16,24},{24,0},{32,40},{40,48},{48,56},{56,32},{64,72... | collective-permute-start | bytes 1572872 | tf_op jit(solution)/shard_map/ppermute | solution.py:38
  105.5 19.2 %collective-permute-start.9 = (bf16[256,512]{0,1:T(8,128)(2,1)}, bf16[256,512]{0,1:T(8,128)(2,1)}, u32[]{:S(2)}, u32[]{:S(2)}) collective-permute-start(bf16[256,512]{0,1:T(8,128)(2,1)} %collective-permute-done.7), channel_id=1, source_target_pairs={{0,32},{8,40},{16,48},{24,56},{32,64},{40,72},{48,80},{56,88},{64,... | collective-permute-start | bytes 786440 | tf_op jit(solution)/shard_map/ppermute | solution.py:38
  110.5 2.6 %copy-start.5 = (bf16[32,4,8,128]{3,2,1,0:T(8,128)(2,1)}, bf16[32,4,8,128]{3,2,1,0:T(8,128)(2,1)S(1)}, u32[]{:S(2)}) copy-start(bf16[32,4,8,128]{3,2,1,0:T(8,128)(2,1)S(1)} %get-tuple-element.10) | copy-start | bytes 786436
  113.1 1.2 copy-start.3
  114.2 20.9 %all-to-all-start.1 = ((bf16[32,16,512]{2,1,0:T(8,128)(2,1)}), bf16[32,16,512]{2,1,0:T(8,128)(2,1)S(1)}, u32[]{:S(2)}, u32[]{:S(2)}) async-start(bf16[32,16,512]{2,1,0:T(8,128)(2,1)} %bitcast.97), calls=%async_computation.1 | async-start | bytes 1048576 | tf_op jit(solution)/shard_map/all_to_all | solution.py:124
  127.5 1.6 copy-start.2
  140.6 19.7 %all-to-all-start.2 = ((bf16[32,16,512]{2,1,0:T(8,128)(2,1)}), bf16[32,16,512]{2,1,0:T(8,128)(2,1)S(1)}, u32[]{:S(2)}, u32[]{:S(2)}) async-start(bf16[32,16,512]{2,1,0:T(8,128)(2,1)} %bitcast.16), calls=%async_computation.3 | async-start | bytes 1048576 | tf_op jit(solution)/shard_map/all_to_all | solution.py:142
  146.5 54.6 %reduce-scatter.2.cloned.1.call-start = ((), (), s32[]{:S(2)}) async-start(), calls=%async_computation.5 | async-start | bytes 2359296 | tf_op jit(solution)/shard_map/reduce_scatter | solution.py:131
  151.8 9.0 %copy-start.4 = (bf16[4,128,256]{2,1,0:T(8,128)(2,1)S(1)}, bf16[4,128,256]{2,1,0:T(8,128)(2,1)}, u32[]{:S(2)}) copy-start(bf16[4,128,256]{2,1,0:T(8,128)(2,1)} %copy-done.3) | copy-start | bytes 786436
  151.8 9.1 %copy-start.6 = (bf16[32,4,8,128]{3,2,1,0:T(8,128)(2,1)S(1)}, bf16[32,4,8,128]{3,2,1,0:T(8,128)(2,1)}, u32[]{:S(2)}) copy-start(bf16[32,4,8,128]{3,2,1,0:T(8,128)(2,1)} %copy-done.5) | copy-start | bytes 786436
Sparse Core Ops, SparseCore 0:
  31.9 26.8 all-gather.1
  151.9 32.7 reduce-scatter.1

commit v8 on v6

--- a/solution.py
+++ b/solution.py
@@ -19,7 +19,7 @@
     ).astype(rows.dtype)
 
 
-def ring_gather_cols(block, axis_name, ny, nz):
+def ring_gather_cols(block, axis_name, ny, nz, z_first=False, take=None):
     index = lax.axis_index(axis_name)
     y = index % ny
     z = index // ny
@@ -29,21 +29,33 @@
     def perm(dy, dz):
         return [(i, ((i // ny + dz) % nz) * ny + (i % ny + dy) % ny) for i in range(n)]
 
-    def ring(piece, pos, count, step_perm, width, total):
+    def ring(piece, pos, count, step_perm, width, total, use=None):
         out = jnp.zeros((piece.shape[0], total), piece.dtype)
         out = lax.dynamic_update_slice(out, piece, (0, pos * width))
+        acc = None if use is None else use(piece, pos)
         fwd = piece
         bwd = piece
         for step in range(1, count // 2 + 1):
             fwd = lax.ppermute(fwd, axis_name, step_perm(1))
-            out = lax.dynamic_update_slice(out, fwd, (0, ((pos - step) % count) * width))
+            at = (pos - step) % count
+            out = lax.dynamic_update_slice(out, fwd, (0, at * width))
+            if use is not None:
+                acc = acc + use(fwd, at)
             if count - step != step:
                 bwd = lax.ppermute(bwd, axis_name, step_perm(-1))
-                out = lax.dynamic_update_slice(out, bwd, (0, ((pos + step) % count) * width))
-        return out
-
-    row = ring(block, y, ny, lambda d: perm(d, 0), cols, ny * cols)
-    return ring(row, z, nz, lambda d: perm(0, d), ny * cols, n * cols)
+                at = (pos + step) % count
+                out = lax.dynamic_update_slice(out, bwd, (0, at * width))
+                if use is not None:
+                    acc = acc + use(bwd, at)
+        return out, acc
+
+    rows = block.shape[0]
+    if not z_first:
+        row, _ = ring(block, y, ny, lambda d: perm(d, 0), cols, ny * cols)
+        return ring(row, z, nz, lambda d: perm(0, d), ny * cols, n * cols, take)
+    row, _ = ring(block, z, nz, lambda d: perm(0, d), cols, nz * cols)
+    full, acc = ring(row, y, ny, lambda d: perm(d, 0), nz * cols, n * cols, take)
+    return full.reshape(rows, ny, nz, cols).transpose(0, 2, 1, 3).reshape(rows, n * cols), acc
 
 
 def on_device(queries, key_rows, value_rows, out_weight, grad_output, cluster_ids, block_pattern):
@@ -68,7 +80,31 @@
     ).astype(jnp.bfloat16)
 
     ring_y = 4 if groups % 4 == 0 else 1
-    full_weight = ring_gather_cols(out_weight, "seq", ring_y, groups // ring_y)
+    half_rows = out_weight.shape[0] // 2
+    ring_z = groups // ring_y
+    cols = out_weight.shape[1]
+    grad_full = lax.all_gather(grad_output, "head", axis=1, tiled=True)
+    grad_by_y = grad_full.reshape(tokens, ring_z, ring_y, cols)
+
+    def grad_from_zblock(piece, at):
+        part = lax.dynamic_slice_in_dim(grad_full, at * ring_y * cols, ring_y * cols, axis=1)
+        return jnp.einsum("td,wd->tw", part, piece, preferred_element_type=jnp.float32)
+
+    def grad_from_yblock(piece, at):
+        part = lax.dynamic_index_in_dim(grad_by_y, at, axis=2, keepdims=False)
+        return jnp.einsum(
+            "td,wd->tw", part.reshape(tokens, ring_z * cols), piece,
+            preferred_element_type=jnp.float32,
+        )
+
+    weight_a, grad_a = ring_gather_cols(
+        out_weight[:half_rows], "seq", ring_y, ring_z, False, grad_from_zblock
+    )
+    weight_b, grad_b = ring_gather_cols(
+        out_weight[half_rows:], "seq", ring_y, ring_z, True, grad_from_yblock
+    )
+    full_weight = jnp.concatenate([weight_a, weight_b], axis=0)
+    grad_sum = jnp.concatenate([grad_a, grad_b], axis=1)
     live_flag = jnp.ones((tokens, HD), queries.dtype)
     qkv = jnp.concatenate([queries, key_rows, value_rows, live_flag], axis=1)
     qkv_in = lax.all_to_all(select_rows(to_slot, qkv), "seq", 0, 0, tiled=True)
@@ -120,12 +156,6 @@
         rounded_part.astype(jnp.bfloat16), "head", scatter_dimension=1, tiled=True
     )
 
-    grad_sum = jnp.einsum(
-        "td,wd->tw",
-        lax.all_gather(grad_output, "head", axis=1, tiled=True),
-        full_weight,
-        preferred_element_type=jnp.float32,
-    )
     grad_attention = grad_sum.astype(jnp.bfloat16)
     grad_in = lax.all_to_all(select_rows(to_slot, grad_attention), "seq", 0, 0, tiled=True)
     g_c = select_rows(to_rank, grad_in).reshape(ranks, head_count, HD)

time: 217 us -> 218 us (level)
  blocking collectives: 43.6 us -> 36.6 us
  other arithmetic: 6.25 us -> 12 us
  local copies, waits for them, and re-layouts: 15.5 us -> 11.4 us
  starting transfers between devices: 43.7 us -> 47.4 us
    ppermute x6 -> x12, starting transfers between devices: 3.71 us -> 15.3 us  [ring(): fwd = lax.ppermute(fwd, axis_name, step_perm(1))]
    all_to_all x1, waiting for transfers between devices: 0.01 us -> 9.19 us  [on_device(): lax.all_to_all(select_rows_t(to_rank, attn_c.reshape(ranks, width)), 'seq...]
    dynamic_update_slice x10 -> x20, local copies, waits for them, and re-layouts: 9.44 us -> 0.38 us  [the longest x12 0.22 us: ring(): out = lax.dynamic_update_slice(out, fwd, (0, at * width))]
    all_to_all x1, blocking collectives: 43.6 us -> 36.6 us  [on_device(): lax.all_to_all(select_rows_t(to_rank, grads_c), 'seq', 0, 0, tiled=True)]
    ppermute x4 -> x8, waiting for transfers between devices: 11 us -> 5.1 us  [ring(): bwd = lax.ppermute(bwd, axis_name, step_perm(-1))]
    unnamed x16 -> x57, local copies, waits for them, and re-layouts: 0.04 us -> 5.2 us
    all_to_all x1, starting transfers between devices: 8.23 us -> 4.19 us  [on_device(): lax.all_to_all(select_rows_t(to_rank, attn_c.reshape(ranks, width)), 'seq...]
    concatenate x0 -> x1, other arithmetic: none -> 4.01 us  [on_device(): full_weight = jnp.concatenate([weight_a, weight_b], axis=0)]
  transfers between devices with their start and end apart: 15 -> 25, of which waited for: 8 -> 9; matrix products, arithmetic and copies ran while one was open for 15% -> 12% of each run, Pallas kernels for 0% -> 0%
where the time goes in v8:
time: 218 us
  waiting for transfers between devices  72.3 us (33%)
  starting transfers between devices  47.4 us (22%)
  blocking collectives  36.6 us (17%)
  matrix products  22.5 us (10%)
  between operations  15.2 us (7%)
  other arithmetic  12 us (6%)
  local copies, waits for them, and re-layouts  11.4 us (5%)
    ppermute x12, waiting for transfers between devices, ring(): fwd = lax.ppermute(fwd, axis_name, step_perm(1))  49.6 us
    all_to_all x1, blocking collectives, on_device(): lax.all_to_all(select_rows_t(to_rank, grads_c), 'seq', 0, 0, tiled=True)  36.6 us
    ppermute x12, starting transfers between devices, ring(): fwd = lax.ppermute(fwd, axis_name, step_perm(1))  15.3 us
    ppermute x8, starting transfers between devices, ring(): bwd = lax.ppermute(bwd, axis_name, step_perm(-1))  14.4 us
    all_to_all x1, waiting for transfers between devices, on_device(): lax.all_to_all(select_rows_t(to_rank, attn_c.reshape(ranks, width)), 'seq...  9.19 us
    all_to_all x1, waiting for transfers between devices, on_device(): lax.all_to_all(select_rows(to_slot, grad_attention), 'seq', 0, 0, tiled=T...  8.42 us
    all_to_all x1, starting transfers between devices, on_device(): qkv_in = lax.all_to_all(select_rows(to_slot, qkv), 'seq', 0, 0, tiled=True)  7.68 us
    dot_general x4, matrix products, select_rows(): jnp.dot(onehot, rows, preferred_element_type=jnp.float32).astype(rows.dtype)  7.57 us
  transfers between devices with their start and end apart: 25, of which 9 were waited for; matrix products, arithmetic and copies ran while one was open for 12% of the time, Pallas kernels for 0%

profile of v8, /device:TPU:4, one launch (start us, length us, event | category | flops | bytes accessed | tf_op | source)
XLA Modules:
  0.0 217.5 jit_solution(700282632761426820)
XLA Ops:
  7.2 0.9 fusion.91
  8.2 1.7 collective-permute-start
  9.9 1.7 collective-permute-start.1
  11.7 2.0 collective-permute-start.10
  13.6 4.0 %collective-permute-start.11 = (bf16[256,128]{0,1:T(8,128)(2,1)S(1)}, bf16[256,128]{0,1:T(8,128)(2,1)S(1)}, u32[]{:S(2)}, u32[]{:S(2)}) collective-permute-start(bf16[256,128]{0,1:T(8,128)(2,1)S(1)} %copy.69), channel_id=1, source_target_pairs={{0,224},{8,232},{16,240},{24,248},{32,0},{40,8},{48,16},{56,24},{6... | collective-permute-start | bytes 196616 | tf_op jit(solution)/shard_map/ppermute | solution.py:45
  17.7 1.8 copy.52
  19.5 0.7 fusion.69
  20.2 0.6 reduce-window.18
  21.0 0.8 fusion.68
  21.8 0.7 multiply_add_fusion
  22.5 3.0 %convolution_convert_fusion.2 = bf16[512,1664]{1,0:T(8,128)(2,1)} fusion(bf16[256,512]{1,0:T(8,128)(2,1)} %param.9, bf16[256,512]{1,0:T(8,128)(2,1)} %param.8, bf16[256,512]{1,0:T(8,128)(2,1)} %param.7, bf16[1664]{0:T(1024)(128)(2,1)S(1)} %pad.10.clone, s32[256]{0:T(256)S(1)} %multiply_add_fusion), kind=kOutput, calls=%fused_computation.4 | convolution fusion | flops 440598528 | bytes 2494720 | tf_op jit(solution)/shard_map/dot_general | solution.py:13
  25.4 7.7 %all-to-all-start = ((bf16[32,16,1664]{2,1,0:T(8,128)(2,1)}), bf16[32,16,1664]{2,1,0:T(8,128)(2,1)}, u32[]{:S(2)}, u32[]{:S(2)}) async-start(bf16[32,16,1664]{2,1,0:T(8,128)(2,1)} %bitcast.2), calls=%async_computation | async-start | bytes 3407872 | tf_op jit(solution)/shard_map/all_to_all | solution.py:110
  33.7 0.7 fusion.92
  34.4 2.6 %broadcast_select_fusion = (s32[256]{0:T(256)S(1)}, s32[256]{0:T(256)S(1)}) fusion(s32[]{:T(128)} %bitcast.8, s32[]{:T(128)} %bitcast.7, s32[]{:T(128)} %bitcast.6, s32[]{:T(128)} %bitcast.5), kind=kLoop, calls=%fused_computation.147 | loop fusion | flops 2816 | bytes 2064 | tf_op jit(solution)/shard_map/jit(_where)/select_n | solution.py:133
  37.3 1.8 collective-permute-start.2
  39.1 1.5 collective-permute-start.12
  40.5 1.8 collective-permute-start.13
  42.4 2.2 %collective-permute-done.2 = bf16[256,128]{0,1:T(8,128)(2,1)S(1)} collective-permute-done((bf16[256,128]{0,1:T(8,128)(2,1)S(1)}, bf16[256,128]{0,1:T(8,128)(2,1)S(1)}, u32[]{:S(2)}, u32[]{:S(2)}) %collective-permute-start.2) | collective-permute-done | bytes 65568 | tf_op jit(solution)/shard_map/ppermute | solution.py:39
  44.6 1.3 collective-permute-start.4
  45.9 0.8 collective-permute-start.3
  46.7 27.8 %collective-permute-done.12 = bf16[256,128]{0,1:T(8,128)(2,1)S(1)} collective-permute-done((bf16[256,128]{0,1:T(8,128)(2,1)S(1)}, bf16[256,128]{0,1:T(8,128)(2,1)S(1)}, u32[]{:S(2)}, u32[]{:S(2)}) %collective-permute-start.12) | collective-permute-done | bytes 65568 | tf_op jit(solution)/shard_map/ppermute | solution.py:39
  74.6 3.2 %collective-permute-start.15 = (bf16[256,128]{0,1:T(8,128)(2,1)S(1)}, bf16[256,128]{0,1:T(8,128)(2,1)S(1)}, u32[]{:S(2)}, u32[]{:S(2)}) collective-permute-start(bf16[256,128]{0,1:T(8,128)(2,1)S(1)} %collective-permute-done.13), channel_id=1, source_target_pairs={{0,224},{8,232},{16,240},{24,248},{32,0},{40,8},{48,16},{56,24},{6... | collective-permute-start | bytes 196616 | tf_op jit(solution)/shard_map/ppermute | solution.py:45
  78.0 2.1 collective-permute-done.14
  80.2 5.4 %collective-permute-done.16 = bf16[256,128]{0,1:T(8,128)(2,1)S(1)} collective-permute-done((bf16[256,128]{0,1:T(8,128)(2,1)S(1)}, bf16[256,128]{0,1:T(8,128)(2,1)S(1)}, u32[]{:S(2)}, u32[]{:S(2)}) %collective-permute-start.16) | collective-permute-done | bytes 65568 | tf_op jit(solution)/shard_map/ppermute | solution.py:39
  85.6 1.7 collective-permute-start.17
  87.3 1.8 collective-permute-start.18
  89.3 1.8 collective-permute-start.5
  91.4 5.1 %collective-permute-done.6 = bf16[256,512]{0,1:T(8,128)(2,1)S(1)} collective-permute-done((bf16[256,512]{0,1:T(8,128)(2,1)S(1)}, bf16[256,512]{0,1:T(8,128)(2,1)S(1)}, u32[]{:S(2)}, u32[]{:S(2)}) %collective-permute-start.6) | collective-permute-done | bytes 262176 | tf_op jit(solution)/shard_map/ppermute | solution.py:45
  96.5 0.4 collective-permute-start.8
  96.9 1.9 collective-permute-start.7
  98.9 0.4 collective-permute-start.19
  99.3 6.3 %collective-permute-done.7 = bf16[256,512]{0,1:T(8,128)(2,1)S(1)} collective-permute-done((bf16[256,512]{0,1:T(8,128)(2,1)S(1)}, bf16[256,512]{0,1:T(8,128)(2,1)S(1)}, u32[]{:S(2)}, u32[]{:S(2)}) %collective-permute-start.7) | collective-permute-done | bytes 262176 | tf_op jit(solution)/shard_map/ppermute | solution.py:39
  105.6 1.7 collective-permute-start.9
  107.5 5.7 %collective-permute-done.9 = bf16[256,512]{0,1:T(8,128)(2,1)S(1)} collective-permute-done((bf16[256,512]{0,1:T(8,128)(2,1)S(1)}, bf16[256,512]{0,1:T(8,128)(2,1)S(1)}, u32[]{:S(2)}, u32[]{:S(2)}) %collective-permute-start.9) | collective-permute-done | bytes 262176 | tf_op jit(solution)/shard_map/ppermute | solution.py:39
  113.3 0.6 copy-done.11
  113.9 0.7 copy-done.2
  115.0 1.1 convert_reduce_fusion
  116.5 1.7 constant_dynamic-slice_fusion
  118.3 0.3 fusion.94
  118.7 0.4 fusion.95
  119.1 0.3 fusion.11
  119.4 0.5 copy-done.1
  121.6 0.3 fusion.8
  122.4 0.4 fusion.13
  122.8 1.1 convolution_convert_fusion.6
  123.9 5.8 %all-to-all-start.2 = ((bf16[32,16,512]{2,1,0:T(8,128)(2,1)}), bf16[32,16,512]{2,1,0:T(8,128)(2,1)}, u32[]{:S(2)}, u32[]{:S(2)}) async-start(bf16[32,16,512]{2,1,0:T(8,128)(2,1)} %bitcast.21), calls=%async_computation.3 | async-start | bytes 1048576 | tf_op jit(solution)/shard_map/all_to_all | solution.py:160
  129.9 1.1 fusion.78
  131.0 2.1 convolution_convert_fusion.4
  133.4 1.5 fusion.93
  134.9 8.4 %all-to-all-done.2 = bf16[32,16,512]{2,1,0:T(8,128)(2,1)} async-done(((bf16[32,16,512]{2,1,0:T(8,128)(2,1)}), bf16[32,16,512]{2,1,0:T(8,128)(2,1)}, u32[]{:S(2)}, u32[]{:S(2)}) %all-to-all-start.2) | async-done | bytes 524320 | tf_op jit(solution)/shard_map/all_to_all | solution.py:160
  143.3 1.4 convolution_convert_fusion.8
  144.9 0.8 multiply_reduce_fusion
  145.6 1.2 convolution_convert_fusion.5
  146.8 4.2 %all-to-all-start.1 = ((bf16[32,16,512]{2,1,0:T(8,128)(2,1)}), bf16[32,16,512]{2,1,0:T(8,128)(2,1)S(1)}, u32[]{:S(2)}, u32[]{:S(2)}) async-start(bf16[32,16,512]{2,1,0:T(8,128)(2,1)} %bitcast.121), calls=%async_computation.1 | async-start | bytes 1048576 | tf_op jit(solution)/shard_map/all_to_all | solution.py:148
  151.1 4.0 %pad_maximum_fusion = bf16[512,4096]{0,1:T(8,128)(2,1)} fusion(bf16[256,4096]{0,1:T(8,128)(2,1)S(1)} %bitcast.105, bf16[256,4096]{0,1:T(8,128)(2,1)} %copy-done.2), kind=kLoop, calls=%fused_computation.2 | loop fusion | flops 8388608 | bytes 8388608 | tf_op jit(solution)/shard_map/concatenate | solution.py:106
  155.7 9.2 %all-to-all-done.1 = bf16[32,16,512]{2,1,0:T(8,128)(2,1)S(1)} async-done(((bf16[32,16,512]{2,1,0:T(8,128)(2,1)}), bf16[32,16,512]{2,1,0:T(8,128)(2,1)S(1)}, u32[]{:S(2)}, u32[]{:S(2)}) %all-to-all-start.1) | async-done | bytes 524320 | tf_op jit(solution)/shard_map/all_to_all | solution.py:148
  164.9 5.0 %convolution_convert_fusion = bf16[256,4096]{1,0:T(8,128)(2,1)} fusion(bf16[512,4096]{0,1:T(8,128)(2,1)} %pad_maximum_fusion, bf16[512,512]{1,0:T(8,128)(2,1)S(1)} %bitcast.107, s32[256]{0:T(256)S(1)} %multiply_add_fusion), kind=kOutput, calls=%fused_computation.1 | convolution fusion | flops 1209270272 | bytes 6816768 | tf_op jit(solution)/shard_map/dot_general | solution.py:153
  169.9 0.9 copy-done.23
  170.8 0.8 convolution_convert_fusion.7
  171.6 0.3 fusion.7
  172.0 0.6 convolution_convert_fusion.1
  172.6 36.6 %all_to_all.48 = bf16[32,16,1536]{2,1,0:T(8,128)(2,1)S(1)} all-to-all(bf16[32,16,1536]{2,1,0:T(8,128)(2,1)S(1)} %bitcast.112), channel_id=1, replica_groups=mesh['seq'=32,'head'=8] {'seq'}, dimensions={0} | all-to-all | bytes 3145728 | tf_op jit(solution)/shard_map/all_to_all | solution.py:183
  209.1 0.6 convolution_convert_fusion.3
  209.8 0.9 fusion.90
  (133 shorter events, 6.3 us)
Async XLA Ops:
  7.2 26.3 %copy-start = (s32[32,2,2]{0,2,1:T(2,128)S(1)}, s32[32,2,2]{0,2,1:T(2,128)}, u32[]{:S(2)}) copy-start(s32[32,2,2]{0,2,1:T(2,128)} %param.13) | copy-start | bytes 1540
  7.2 109.3 %all-gather.2.cloned.1.call-start = ((), (), s32[]{:S(2)}) async-start(), calls=%async_computation.6 | async-start | bytes 2359296 | tf_op jit(solution)/shard_map/all_gather | solution.py:86
  8.2 29.0 %collective-permute-start = (bf16[256,128]{0,1:T(8,128)(2,1)S(1)}, bf16[256,128]{0,1:T(8,128)(2,1)S(1)}, u32[]{:S(2)}, u32[]{:S(2)}) collective-permute-start(bf16[256,128]{0,1:T(8,128)(2,1)S(1)} %copy.68), channel_id=1, source_target_pairs={{0,8},{8,16},{16,24},{24,0},{32,40},{40,48},{48,56},{56,32},{64,72... | collective-permute-start | bytes 196616 | tf_op jit(solution)/shard_map/ppermute | solution.py:39
  9.9 32.5 %collective-permute-start.1 = (bf16[256,128]{0,1:T(8,128)(2,1)S(1)}, bf16[256,128]{0,1:T(8,128)(2,1)S(1)}, u32[]{:S(2)}, u32[]{:S(2)}) collective-permute-start(bf16[256,128]{0,1:T(8,128)(2,1)S(1)} %copy.68), channel_id=1, source_target_pairs={{0,24},{8,0},{16,8},{24,16},{32,56},{40,32},{48,40},{56,48},{64,88... | collective-permute-start | bytes 196616 | tf_op jit(solution)/shard_map/ppermute | solution.py:45
  11.7 27.4 %collective-permute-start.10 = (bf16[256,128]{0,1:T(8,128)(2,1)S(1)}, bf16[256,128]{0,1:T(8,128)(2,1)S(1)}, u32[]{:S(2)}, u32[]{:S(2)}) collective-permute-start(bf16[256,128]{0,1:T(8,128)(2,1)S(1)} %copy.69), channel_id=1, source_target_pairs={{0,32},{8,40},{16,48},{24,56},{32,64},{40,72},{48,80},{56,88},{64,... | collective-permute-start | bytes 196616 | tf_op jit(solution)/shard_map/ppermute | solution.py:39
  13.6 26.9 %collective-permute-start.11 = (bf16[256,128]{0,1:T(8,128)(2,1)S(1)}, bf16[256,128]{0,1:T(8,128)(2,1)S(1)}, u32[]{:S(2)}, u32[]{:S(2)}) collective-permute-start(bf16[256,128]{0,1:T(8,128)(2,1)S(1)} %copy.69), channel_id=1, source_target_pairs={{0,224},{8,232},{16,240},{24,248},{32,0},{40,8},{48,16},{56,24},{6... | collective-permute-start | bytes 196616 | tf_op jit(solution)/shard_map/ppermute | solution.py:45
  25.4 89.5 %all-to-all-start = ((bf16[32,16,1664]{2,1,0:T(8,128)(2,1)}), bf16[32,16,1664]{2,1,0:T(8,128)(2,1)}, u32[]{:S(2)}, u32[]{:S(2)}) async-start(bf16[32,16,1664]{2,1,0:T(8,128)(2,1)} %bitcast.2), calls=%async_computation | async-start | bytes 3407872 | tf_op jit(solution)/shard_map/all_to_all | solution.py:110
  37.3 7.4 %collective-permute-start.2 = (bf16[256,128]{0,1:T(8,128)(2,1)S(1)}, bf16[256,128]{0,1:T(8,128)(2,1)S(1)}, u32[]{:S(2)}, u32[]{:S(2)}) collective-permute-start(bf16[256,128]{0,1:T(8,128)(2,1)S(1)} %collective-permute-done), channel_id=1, source_target_pairs={{0,8},{8,16},{16,24},{24,0},{32,40},{40,48},{48,56},{56,32},{64,72... | collective-permute-start | bytes 196616 | tf_op jit(solution)/shard_map/ppermute | solution.py:39
  39.1 35.5 %collective-permute-start.12 = (bf16[256,128]{0,1:T(8,128)(2,1)S(1)}, bf16[256,128]{0,1:T(8,128)(2,1)S(1)}, u32[]{:S(2)}, u32[]{:S(2)}) collective-permute-start(bf16[256,128]{0,1:T(8,128)(2,1)S(1)} %collective-permute-done.10), channel_id=1, source_target_pairs={{0,32},{8,40},{16,48},{24,56},{32,64},{40,72},{48,80},{56,88},{64,... | collective-permute-start | bytes 196616 | tf_op jit(solution)/shard_map/ppermute | solution.py:39
  40.5 34.0 %collective-permute-start.13 = (bf16[256,128]{0,1:T(8,128)(2,1)S(1)}, bf16[256,128]{0,1:T(8,128)(2,1)S(1)}, u32[]{:S(2)}, u32[]{:S(2)}) collective-permute-start(bf16[256,128]{0,1:T(8,128)(2,1)S(1)} %collective-permute-done.11), channel_id=1, source_target_pairs={{0,224},{8,232},{16,240},{24,248},{32,0},{40,8},{48,16},{56,24},{6... | collective-permute-start | bytes 196616 | tf_op jit(solution)/shard_map/ppermute | solution.py:45
  44.6 44.5 %collective-permute-start.4 = (bf16[256,512]{0,1:T(8,128)(2,1)S(1)}, bf16[256,512]{0,1:T(8,128)(2,1)S(1)}, u32[]{:S(2)}, u32[]{:S(2)}) collective-permute-start(bf16[256,512]{0,1:T(8,128)(2,1)S(1)} %constant_dynamic-update-slice_fusion.20), channel_id=1, source_target_pairs={{0,224},{8,232},{16,240},{24,248},{32,0},{40,8},{48,16},{56,24},{6... | collective-permute-start | bytes 786440 | tf_op jit(solution)/shard_map/ppermute | solution.py:45
  45.9 43.4 %collective-permute-start.3 = (bf16[256,512]{0,1:T(8,128)(2,1)S(1)}, bf16[256,512]{0,1:T(8,128)(2,1)S(1)}, u32[]{:S(2)}, u32[]{:S(2)}) collective-permute-start(bf16[256,512]{0,1:T(8,128)(2,1)S(1)} %constant_dynamic-update-slice_fusion.20), channel_id=1, source_target_pairs={{0,32},{8,40},{16,48},{24,56},{32,64},{40,72},{48,80},{56,88},{64,... | collective-permute-start | bytes 786440 | tf_op jit(solution)/shard_map/ppermute | solution.py:39
  74.6 5.6 %collective-permute-start.14 = (bf16[256,128]{0,1:T(8,128)(2,1)S(1)}, bf16[256,128]{0,1:T(8,128)(2,1)S(1)}, u32[]{:S(2)}, u32[]{:S(2)}) collective-permute-start(bf16[256,128]{0,1:T(8,128)(2,1)S(1)} %collective-permute-done.12), channel_id=1, source_target_pairs={{0,32},{8,40},{16,48},{24,56},{32,64},{40,72},{48,80},{56,88},{64,... | collective-permute-start | bytes 196616 | tf_op jit(solution)/shard_map/ppermute | solution.py:39
  74.6 5.6 %collective-permute-start.15 = (bf16[256,128]{0,1:T(8,128)(2,1)S(1)}, bf16[256,128]{0,1:T(8,128)(2,1)S(1)}, u32[]{:S(2)}, u32[]{:S(2)}) collective-permute-start(bf16[256,128]{0,1:T(8,128)(2,1)S(1)} %collective-permute-done.13), channel_id=1, source_target_pairs={{0,224},{8,232},{16,240},{24,248},{32,0},{40,8},{48,16},{56,24},{6... | collective-permute-start | bytes 196616 | tf_op jit(solution)/shard_map/ppermute | solution.py:45
  80.1 5.5 %collective-permute-start.16 = (bf16[256,128]{0,1:T(8,128)(2,1)S(1)}, bf16[256,128]{0,1:T(8,128)(2,1)S(1)}, u32[]{:S(2)}, u32[]{:S(2)}) collective-permute-start(bf16[256,128]{0,1:T(8,128)(2,1)S(1)} %collective-permute-done.14), channel_id=1, source_target_pairs={{0,32},{8,40},{16,48},{24,56},{32,64},{40,72},{48,80},{56,88},{64,... | collective-permute-start | bytes 196616 | tf_op jit(solution)/shard_map/ppermute | solution.py:39
  85.6 13.3 %collective-permute-start.17 = (bf16[256,1024]{0,1:T(8,128)(2,1)S(1)}, bf16[256,1024]{0,1:T(8,128)(2,1)S(1)}, u32[]{:S(2)}, u32[]{:S(2)}) collective-permute-start(bf16[256,1024]{0,1:T(8,128)(2,1)S(1)} %constant_dynamic-update-slice_fusion.4), channel_id=1, source_target_pairs={{0,8},{8,16},{16,24},{24,0},{32,40},{40,48},{48,56},{56,32},{64,72... | collective-permute-start | bytes 1572872 | tf_op jit(solution)/shard_map/ppermute | solution.py:39
  87.3 20.0 %collective-permute-start.18 = (bf16[256,1024]{0,1:T(8,128)(2,1)S(1)}, bf16[256,1024]{0,1:T(8,128)(2,1)S(1)}, u32[]{:S(2)}, u32[]{:S(2)}) collective-permute-start(bf16[256,1024]{0,1:T(8,128)(2,1)S(1)} %constant_dynamic-update-slice_fusion.4), channel_id=1, source_target_pairs={{0,24},{8,0},{16,8},{24,16},{32,56},{40,32},{48,40},{56,48},{64,88... | collective-permute-start | bytes 1572872 | tf_op jit(solution)/shard_map/ppermute | solution.py:45
  89.1 2.3 %copy-start.13 = (bf16[256,512]{0,1:T(8,128)(2,1)}, bf16[256,512]{0,1:T(8,128)(2,1)S(1)}, u32[]{:S(2)}) copy-start(bf16[256,512]{0,1:T(8,128)(2,1)S(1)} %collective-permute-done.4) | copy-start | bytes 786436
  89.1 7.4 %collective-permute-start.6 = (bf16[256,512]{0,1:T(8,128)(2,1)S(1)}, bf16[256,512]{0,1:T(8,128)(2,1)S(1)}, u32[]{:S(2)}, u32[]{:S(2)}) collective-permute-start(bf16[256,512]{0,1:T(8,128)(2,1)S(1)} %collective-permute-done.4), channel_id=1, source_target_pairs={{0,224},{8,232},{16,240},{24,248},{32,0},{40,8},{48,16},{56,24},{6... | collective-permute-start | bytes 786440 | tf_op jit(solution)/shard_map/ppermute | solution.py:45
  89.3 2.1 copy-start.15
  89.3 7.6 %collective-permute-start.5 = (bf16[256,512]{0,1:T(8,128)(2,1)S(1)}, bf16[256,512]{0,1:T(8,128)(2,1)S(1)}, u32[]{:S(2)}, u32[]{:S(2)}) collective-permute-start(bf16[256,512]{0,1:T(8,128)(2,1)S(1)} %collective-permute-done.3), channel_id=1, source_target_pairs={{0,32},{8,40},{16,48},{24,56},{32,64},{40,72},{48,80},{56,88},{64,... | collective-permute-start | bytes 786440 | tf_op jit(solution)/shard_map/ppermute | solution.py:39
  96.5 11.0 %copy-start.17 = (bf16[256,512]{0,1:T(8,128)(2,1)}, bf16[256,512]{0,1:T(8,128)(2,1)S(1)}, u32[]{:S(2)}) copy-start(bf16[256,512]{0,1:T(8,128)(2,1)S(1)} %collective-permute-done.6) | copy-start | bytes 786436
  96.5 10.9 %collective-permute-start.8 = (bf16[256,512]{0,1:T(8,128)(2,1)S(1)}, bf16[256,512]{0,1:T(8,128)(2,1)S(1)}, u32[]{:S(2)}, u32[]{:S(2)}) collective-permute-start(bf16[256,512]{0,1:T(8,128)(2,1)S(1)} %collective-permute-done.6), channel_id=1, source_target_pairs={{0,224},{8,232},{16,240},{24,248},{32,0},{40,8},{48,16},{56,24},{6... | collective-permute-start | bytes 786440 | tf_op jit(solution)/shard_map/ppermute | solution.py:45
  96.9 10.6 %copy-start.7 = (bf16[256,512]{0,1:T(8,128)(2,1)}, bf16[256,512]{0,1:T(8,128)(2,1)S(1)}, u32[]{:S(2)}) copy-start(bf16[256,512]{0,1:T(8,128)(2,1)S(1)} %collective-permute-done.5) | copy-start | bytes 786436
  96.9 8.7 %collective-permute-start.7 = (bf16[256,512]{0,1:T(8,128)(2,1)S(1)}, bf16[256,512]{0,1:T(8,128)(2,1)S(1)}, u32[]{:S(2)}, u32[]{:S(2)}) collective-permute-start(bf16[256,512]{0,1:T(8,128)(2,1)S(1)} %collective-permute-done.5), channel_id=1, source_target_pairs={{0,32},{8,40},{16,48},{24,56},{32,64},{40,72},{48,80},{56,88},{64,... | collective-permute-start | bytes 786440 | tf_op jit(solution)/shard_map/ppermute | solution.py:39
  98.9 14.3 %collective-permute-start.19 = (bf16[256,1024]{0,1:T(8,128)(2,1)S(1)}, bf16[256,1024]{0,1:T(8,128)(2,1)S(1)}, u32[]{:S(2)}, u32[]{:S(2)}) collective-permute-start(bf16[256,1024]{0,1:T(8,128)(2,1)S(1)} %collective-permute-done.17), channel_id=1, source_target_pairs={{0,8},{8,16},{16,24},{24,0},{32,40},{40,48},{48,56},{56,32},{64,72... | collective-permute-start | bytes 1572872 | tf_op jit(solution)/shard_map/ppermute | solution.py:39
  105.6 7.7 %copy-start.9 = (bf16[256,512]{0,1:T(8,128)(2,1)}, bf16[256,512]{0,1:T(8,128)(2,1)S(1)}, u32[]{:S(2)}) copy-start(bf16[256,512]{0,1:T(8,128)(2,1)S(1)} %collective-permute-done.7) | copy-start | bytes 786436
  105.6 7.6 %collective-permute-start.9 = (bf16[256,512]{0,1:T(8,128)(2,1)S(1)}, bf16[256,512]{0,1:T(8,128)(2,1)S(1)}, u32[]{:S(2)}, u32[]{:S(2)}) collective-permute-start(bf16[256,512]{0,1:T(8,128)(2,1)S(1)} %collective-permute-done.7), channel_id=1, source_target_pairs={{0,32},{8,40},{16,48},{24,56},{32,64},{40,72},{48,80},{56,88},{64,... | collective-permute-start | bytes 786440 | tf_op jit(solution)/shard_map/ppermute | solution.py:39
  107.3 6.0 %copy-start.3 = (bf16[256,1024]{0,1:T(8,128)(2,1)}, bf16[256,1024]{0,1:T(8,128)(2,1)S(1)}, u32[]{:S(2)}) copy-start(bf16[256,1024]{0,1:T(8,128)(2,1)S(1)} %collective-permute-done.18) | copy-start | bytes 1572868
  107.4 5.9 %copy-start.19 = (bf16[256,512]{0,1:T(8,128)(2,1)}, bf16[256,512]{0,1:T(8,128)(2,1)S(1)}, u32[]{:S(2)}) copy-start(bf16[256,512]{0,1:T(8,128)(2,1)S(1)} %collective-permute-done.8) | copy-start | bytes 786436
  113.2 0.7 copy-start.11
  113.2 1.4 copy-start.2
  113.2 1.6 copy-start.5
  116.5 2.1 copy-start.4
  118.3 1.6 copy-start.1
  118.3 1.6 copy-start.14
  118.6 1.5 copy-start.16
  118.7 1.8 copy-start.18
  119.0 1.7 copy-start.20
  119.9 1.5 copy-start.8
  120.4 1.2 copy-start.10
  121.0 1.0 copy-start.12
  121.3 1.1 copy-start.6
  123.9 19.4 %all-to-all-start.2 = ((bf16[32,16,512]{2,1,0:T(8,128)(2,1)}), bf16[32,16,512]{2,1,0:T(8,128)(2,1)}, u32[]{:S(2)}, u32[]{:S(2)}) async-start(bf16[32,16,512]{2,1,0:T(8,128)(2,1)} %bitcast.21), calls=%async_computation.3 | async-start | bytes 1048576 | tf_op jit(solution)/shard_map/all_to_all | solution.py:160
  133.1 11.7 %copy-start.24 = (bf16[32,4,8,128]{3,2,1,0:T(8,128)(2,1)}, bf16[32,4,8,128]{3,2,1,0:T(8,128)(2,1)S(1)}, u32[]{:S(2)}) copy-start(bf16[32,4,8,128]{3,2,1,0:T(8,128)(2,1)S(1)} %get-tuple-element.14) | copy-start | bytes 786436
  144.8 0.8 copy-start.21
  146.8 18.0 %all-to-all-start.1 = ((bf16[32,16,512]{2,1,0:T(8,128)(2,1)}), bf16[32,16,512]{2,1,0:T(8,128)(2,1)S(1)}, u32[]{:S(2)}, u32[]{:S(2)}) async-start(bf16[32,16,512]{2,1,0:T(8,128)(2,1)} %bitcast.121), calls=%async_computation.1 | async-start | bytes 1048576 | tf_op jit(solution)/shard_map/all_to_all | solution.py:148
  151.0 59.6 %reduce-scatter.2.cloned.1.call-start = ((), (), s32[]{:S(2)}) async-start(), calls=%async_computation.5 | async-start | bytes 2359296 | tf_op jit(solution)/shard_map/reduce_scatter | solution.py:155
  151.1 4.0 %copy-start.22 = (bf16[256,512]{0,1:T(8,128)(2,1)S(1)}, bf16[256,512]{0,1:T(8,128)(2,1)}, u32[]{:S(2)}) copy-start(bf16[256,512]{0,1:T(8,128)(2,1)} %copy-done.21) | copy-start | bytes 786436
  151.1 4.0 %copy-start.25 = (bf16[32,4,8,128]{3,2,1,0:T(8,128)(2,1)S(1)}, bf16[32,4,8,128]{3,2,1,0:T(8,128)(2,1)}, u32[]{:S(2)}) copy-start(bf16[32,4,8,128]{3,2,1,0:T(8,128)(2,1)} %copy-done.24) | copy-start | bytes 786436
  151.1 4.0 %copy-start.26 = (f32[4,256,256]{1,2,0:T(8,128)S(1)}, f32[4,256,256]{1,2,0:T(8,128)}, u32[]{:S(2)}) copy-start(f32[4,256,256]{1,2,0:T(8,128)} %get-tuple-element.25) | copy-start | bytes 3145732
  169.9 0.9 copy-start.23
Sparse Core Ops, SparseCore 0:
  19.6 25.9 all-gather.1
  170.0 27.3 reduce-scatter.1

commit v9 on v7

--- a/solution.py
+++ b/solution.py
@@ -121,17 +121,6 @@
         jnp.bfloat16
     )
 
-    attn_back = lax.all_to_all(
-        select_rows_t(to_rank, attn_c.reshape(ranks, width)), "seq", 0, 0, tiled=True
-    )
-    attn_back, full_weight = lax.optimization_barrier((attn_back, full_weight))
-    attn_local = select_rows_t(to_slot, attn_back)
-    partial_value = jnp.dot(attn_local, full_weight, preferred_element_type=jnp.float32)
-    rounded_part = lax.optimization_barrier(partial_value.astype(jnp.bfloat16)).astype(jnp.float32)
-    layer_out = lax.psum_scatter(
-        rounded_part.astype(jnp.bfloat16), "head", scatter_dimension=1, tiled=True
-    )
-
     grad_sum = jnp.einsum(
         "td,wd->tw",
         lax.all_gather(grad_output, "head", axis=1, tiled=True),
@@ -139,8 +128,21 @@
         preferred_element_type=jnp.float32,
     )
     grad_attention = grad_sum.astype(jnp.bfloat16)
-    grad_in = lax.all_to_all(select_rows(to_slot, grad_attention), "seq", 0, 0, tiled=True)
-    g_c = select_rows(to_rank, grad_in).reshape(ranks, head_count, HD)
+    both = jnp.concatenate(
+        [
+            select_rows_t(to_rank, attn_c.reshape(ranks, width)),
+            select_rows(to_slot, grad_attention),
+        ],
+        axis=1,
+    )
+    both_in = lax.all_to_all(both, "seq", 0, 0, tiled=True)
+    attn_local = select_rows_t(to_slot, both_in[:, :width])
+    partial_value = jnp.dot(attn_local, full_weight, preferred_element_type=jnp.float32)
+    rounded_part = lax.optimization_barrier(partial_value.astype(jnp.bfloat16)).astype(jnp.float32)
+    layer_out = lax.psum_scatter(
+        rounded_part.astype(jnp.bfloat16), "head", scatter_dimension=1, tiled=True
+    )
+    g_c = select_rows(to_rank, both_in[:, width:]).reshape(ranks, head_count, HD)
 
     delta = jnp.sum(g_c.astype(jnp.float32) * attn_c.astype(jnp.float32), axis=2).T[:, :, None]
     dprobs = jnp.einsum("qhd,khd->hqk", g_c, v_c, preferred_element_type=jnp.float32)

time: 209 us -> 210 us (level)
  blocking collectives: 35.2 us -> 69 us
  starting transfers between devices: 52.4 us -> 40.4 us
  waiting for transfers between devices: 59.1 us -> 51.5 us
  matrix products: 23.3 us -> 19.1 us
  other arithmetic: 10.3 us -> 6.32 us
  local copies, waits for them, and re-layouts: 12.7 us -> 8.72 us
    all_to_all x0 -> x1, blocking collectives: none -> 28.3 us  [on_device(): both_in = lax.all_to_all(both, 'seq', 0, 0, tiled=True)]
    all_to_all x2 -> x0, starting transfers between devices: 13 us -> none  [the longest x1 7.11 us: on_device(): lax.all_to_all(select_rows_t(to_rank, attn_c.reshape(ranks, width)), 'seq...]
    all_to_all x2 -> x0, waiting for transfers between devices: 12.3 us -> none  [the longest x1 8.5 us: on_device(): lax.all_to_all(select_rows(to_slot, grad_attention), 'seq', 0, 0, tiled=T...]
    dynamic_update_slice x12, local copies, waits for them, and re-layouts: 6.03 us -> 0.22 us  [ring(): out = lax.dynamic_update_slice(out, fwd, (0, (pos - step) % count * width))]
    all_to_all x1, blocking collectives: 35.2 us -> 40.7 us  [on_device(): lax.all_to_all(select_rows_t(to_rank, grads_c), 'seq', 0, 0, tiled=True)]
    ppermute x12, waiting for transfers between devices: 46.7 us -> 51.5 us  [ring(): fwd = lax.ppermute(fwd, axis_name, step_perm(1))]
    ppermute x12, starting transfers between devices: 5.49 us -> 10.1 us  [ring(): fwd = lax.ppermute(fwd, axis_name, step_perm(1))]
    all_to_all x1, starting transfers between devices: 11.7 us -> 7.56 us  [on_device(): qkv_in = lax.all_to_all(select_rows(to_slot, qkv), 'seq', 0, 0, tiled=True)]
  transfers between devices with their start and end apart: 25 -> 23, of which waited for: 7 -> 7; matrix products, arithmetic and copies ran while one was open for 16% -> 10% of each run, Pallas kernels for 0% -> 0%
where the time goes in v9:
time: 210 us
  blocking collectives  69 us (33%)
  waiting for transfers between devices  51.5 us (25%)
  starting transfers between devices  40.4 us (19%)
  matrix products  19.1 us (9%)
  between operations  14.9 us (7%)
  local copies, waits for them, and re-layouts  8.72 us (4%)
  other arithmetic  6.32 us (3%)
    ppermute x12, waiting for transfers between devices, ring(): fwd = lax.ppermute(fwd, axis_name, step_perm(1))  51.5 us
    all_to_all x1, blocking collectives, on_device(): lax.all_to_all(select_rows_t(to_rank, grads_c), 'seq', 0, 0, tiled=True)  40.7 us
    all_to_all x1, blocking collectives, on_device(): both_in = lax.all_to_all(both, 'seq', 0, 0, tiled=True)  28.3 us
    ppermute x8, starting transfers between devices, ring(): bwd = lax.ppermute(bwd, axis_name, step_perm(-1))  22.6 us
    ppermute x12, starting transfers between devices, ring(): fwd = lax.ppermute(fwd, axis_name, step_perm(1))  10.1 us
    dot_general x4, matrix products, select_rows(): jnp.dot(onehot, rows, preferred_element_type=jnp.float32).astype(rows.dtype)  8.45 us
    all_to_all x1, starting transfers between devices, on_device(): qkv_in = lax.all_to_all(select_rows(to_slot, qkv), 'seq', 0, 0, tiled=True)  7.56 us
    dot_general x1, matrix products, on_device(): jnp.dot(attn_local, full_weight, preferred_element_type=jnp.float32)  5.09 us
  transfers between devices with their start and end apart: 23, of which 7 were waited for; matrix products, arithmetic and copies ran while one was open for 10% of the time, Pallas kernels for 0%

profile of v9, /device:TPU:4, one launch (start us, length us, event | category | flops | bytes accessed | tf_op | source)
XLA Modules:
  0.0 209.9 jit_solution(18215570823188207101)
XLA Ops:
  7.2 0.9 fusion.69
  8.1 0.1 copy.70
  8.2 2.0 collective-permute-start.10
  10.2 4.0 %collective-permute-start.11 = (bf16[256,128]{0,1:T(8,128)(2,1)S(1)}, bf16[256,128]{0,1:T(8,128)(2,1)S(1)}, u32[]{:S(2)}, u32[]{:S(2)}) collective-permute-start(bf16[256,128]{0,1:T(8,128)(2,1)S(1)} %copy.70), channel_id=1, source_target_pairs={{0,224},{8,232},{16,240},{24,248},{32,0},{40,8},{48,16},{56,24},{6... | collective-permute-start | bytes 196616 | tf_op jit(solution)/shard_map/ppermute | solution.py:41
  14.4 1.7 collective-permute-start
  16.0 1.7 collective-permute-start.1
  17.7 0.7 fusion.53
  18.4 0.6 reduce-window.18
  19.0 0.2 slice_reduce_fusion
  19.2 0.8 fusion.52
  20.0 0.7 multiply_add_fusion
  20.7 3.0 %convolution_convert_fusion.2 = bf16[512,1664]{1,0:T(8,128)(2,1)} fusion(bf16[256,512]{1,0:T(8,128)(2,1)} %param.9, bf16[256,512]{1,0:T(8,128)(2,1)} %param.8, bf16[256,512]{1,0:T(8,128)(2,1)} %param.7, bf16[1664]{0:T(1024)(128)(2,1)S(1)} %pad.10.clone, s32[256]{0:T(256)S(1)} %multiply_add_fusion), kind=kOutput, calls=%fused_computation.4 | convolution fusion | flops 440598528 | bytes 2494720 | tf_op jit(solution)/shard_map/dot_general | solution.py:13
  23.6 7.6 %all-to-all-start = ((bf16[32,16,1664]{2,1,0:T(8,128)(2,1)}), bf16[32,16,1664]{2,1,0:T(8,128)(2,1)S(1)}, u32[]{:S(2)}, u32[]{:S(2)}) async-start(bf16[32,16,1664]{2,1,0:T(8,128)(2,1)} %bitcast.2), calls=%async_computation | async-start | bytes 3407872 | tf_op jit(solution)/shard_map/all_to_all | solution.py:86
  31.6 0.2 fusion.55
  31.8 0.6 fusion.70
  32.4 2.6 %broadcast_select_fusion = (s32[256]{0:T(256)S(1)}, s32[256]{0:T(256)S(1)}) fusion(s32[]{:T(128)} %bitcast.8, s32[]{:T(128)} %bitcast.7, s32[]{:T(128)} %bitcast.6, s32[]{:T(128)} %bitcast.5), kind=kLoop, calls=%fused_computation.113 | loop fusion | flops 2816 | bytes 2064 | tf_op jit(solution)/shard_map/jit(_where)/select_n | solution.py:109
  35.1 0.1 fusion.43
  35.3 1.9 collective-permute-start.12
  37.2 1.4 collective-permute-start.13
  38.6 1.8 collective-permute-start.2
  40.5 4.4 %collective-permute-done.2 = bf16[256,128]{0,1:T(8,128)(2,1)S(1)} collective-permute-done((bf16[256,128]{0,1:T(8,128)(2,1)S(1)}, bf16[256,128]{0,1:T(8,128)(2,1)S(1)}, u32[]{:S(2)}, u32[]{:S(2)}) %collective-permute-start.2) | collective-permute-done | bytes 65568 | tf_op jit(solution)/shard_map/ppermute | solution.py:38
  44.9 0.4 collective-permute-start.3
  45.3 3.9 %collective-permute-start.4 = (bf16[256,512]{0,1:T(8,128)(2,1)S(1)}, bf16[256,512]{0,1:T(8,128)(2,1)S(1)}, u32[]{:S(2)}, u32[]{:S(2)}) collective-permute-start(bf16[256,512]{0,1:T(8,128)(2,1)S(1)} %constant_dynamic-update-slice_fusion.20), channel_id=1, source_target_pairs={{0,224},{8,232},{16,240},{24,248},{32,0},{40,8},{48,16},{56,24},{6... | collective-permute-start | bytes 786440 | tf_op jit(solution)/shard_map/ppermute | solution.py:41
  49.2 23.6 %collective-permute-done.12 = bf16[256,128]{0,1:T(8,128)(2,1)S(1)} collective-permute-done((bf16[256,128]{0,1:T(8,128)(2,1)S(1)}, bf16[256,128]{0,1:T(8,128)(2,1)S(1)}, u32[]{:S(2)}, u32[]{:S(2)}) %collective-permute-start.12) | collective-permute-done | bytes 65568 | tf_op jit(solution)/shard_map/ppermute | solution.py:38
  72.8 3.2 %collective-permute-start.15 = (bf16[256,128]{0,1:T(8,128)(2,1)S(1)}, bf16[256,128]{0,1:T(8,128)(2,1)S(1)}, u32[]{:S(2)}, u32[]{:S(2)}) collective-permute-start(bf16[256,128]{0,1:T(8,128)(2,1)S(1)} %collective-permute-done.13), channel_id=1, source_target_pairs={{0,224},{8,232},{16,240},{24,248},{32,0},{40,8},{48,16},{56,24},{6... | collective-permute-start | bytes 196616 | tf_op jit(solution)/shard_map/ppermute | solution.py:41
  76.0 0.1 broadcast.206.clone.1
  76.2 2.1 %collective-permute-done.14 = bf16[256,128]{0,1:T(8,128)(2,1)S(1)} collective-permute-done((bf16[256,128]{0,1:T(8,128)(2,1)S(1)}, bf16[256,128]{0,1:T(8,128)(2,1)S(1)}, u32[]{:S(2)}, u32[]{:S(2)}) %collective-permute-start.14) | collective-permute-done | bytes 65568 | tf_op jit(solution)/shard_map/ppermute | solution.py:38
  78.4 5.4 %collective-permute-done.16 = bf16[256,128]{0,1:T(8,128)(2,1)S(1)} collective-permute-done((bf16[256,128]{0,1:T(8,128)(2,1)S(1)}, bf16[256,128]{0,1:T(8,128)(2,1)S(1)}, u32[]{:S(2)}, u32[]{:S(2)}) %collective-permute-start.16) | collective-permute-done | bytes 65568 | tf_op jit(solution)/shard_map/ppermute | solution.py:38
  83.8 1.7 collective-permute-start.17
  85.5 1.8 collective-permute-start.18
  87.3 3.2 %collective-permute-start.6 = (bf16[256,512]{0,1:T(8,128)(2,1)S(1)}, bf16[256,512]{0,1:T(8,128)(2,1)S(1)}, u32[]{:S(2)}, u32[]{:S(2)}) collective-permute-start(bf16[256,512]{0,1:T(8,128)(2,1)S(1)} %collective-permute-done.4), channel_id=1, source_target_pairs={{0,224},{8,232},{16,240},{24,248},{32,0},{40,8},{48,16},{56,24},{6... | collective-permute-start | bytes 786440 | tf_op jit(solution)/shard_map/ppermute | solution.py:41
  90.5 0.1 broadcast.206.clone
  90.8 4.1 %collective-permute-done.5 = bf16[256,512]{0,1:T(8,128)(2,1)S(1)} collective-permute-done((bf16[256,512]{0,1:T(8,128)(2,1)S(1)}, bf16[256,512]{0,1:T(8,128)(2,1)S(1)}, u32[]{:S(2)}, u32[]{:S(2)}) %collective-permute-start.5) | collective-permute-done | bytes 262176 | tf_op jit(solution)/shard_map/ppermute | solution.py:38
  94.9 3.3 %collective-permute-start.8 = (bf16[256,512]{0,1:T(8,128)(2,1)S(1)}, bf16[256,512]{0,1:T(8,128)(2,1)S(1)}, u32[]{:S(2)}, u32[]{:S(2)}) collective-permute-start(bf16[256,512]{0,1:T(8,128)(2,1)S(1)} %collective-permute-done.6), channel_id=1, source_target_pairs={{0,224},{8,232},{16,240},{24,248},{32,0},{40,8},{48,16},{56,24},{6... | collective-permute-start | bytes 786440 | tf_op jit(solution)/shard_map/ppermute | solution.py:41
  98.3 0.7 collective-permute-start.19
  99.1 4.4 %collective-permute-done.7 = bf16[256,512]{0,1:T(8,128)(2,1)S(1)} collective-permute-done((bf16[256,512]{0,1:T(8,128)(2,1)S(1)}, bf16[256,512]{0,1:T(8,128)(2,1)S(1)}, u32[]{:S(2)}, u32[]{:S(2)}) %collective-permute-start.7) | collective-permute-done | bytes 262176 | tf_op jit(solution)/shard_map/ppermute | solution.py:38
  103.6 7.5 %collective-permute-done.9 = bf16[256,512]{0,1:T(8,128)(2,1)S(1)} collective-permute-done((bf16[256,512]{0,1:T(8,128)(2,1)S(1)}, bf16[256,512]{0,1:T(8,128)(2,1)S(1)}, u32[]{:S(2)}, u32[]{:S(2)}) %collective-permute-start.9) | collective-permute-done | bytes 262176 | tf_op jit(solution)/shard_map/ppermute | solution.py:38
  111.1 1.3 copy-done.1
  112.4 1.4 copy.52
  113.8 0.1 convert_reduce_fusion
  114.0 0.1 reduce_sum.37
  114.3 0.1 reduce.2
  114.6 0.2 fusion.54
  114.8 0.7 convolution_convert_fusion.4
  115.5 0.1 copy.71
  115.6 0.1 copy.72
  115.8 1.5 fusion.71
  117.3 0.8 convolution_convert_fusion.10
  118.1 0.4 convolution_convert_fusion.6
  118.5 4.5 %convolution_convert_fusion.5 = bf16[512,512]{0,1:T(8,128)(2,1)S(1)} fusion(bf16[256,4096]{1,0:T(8,128)(2,1)} %all-gather.2.cloned.1.call-done, bf16[256,4096]{0,1:T(8,128)(2,1)} %bitcast.82, bf16[256,4096]{0,1:T(8,128)(2,1)} %copy-done.1, s32[256]{0:T(256)S(1)} %multiply_add_fusion), kind=kOutput, calls=%fused_computation.15 | convolution fusion | flops 1216872448 | bytes 6816768 | tf_op jit(solution)/shard_map/dot_general | solution.py:13
  123.1 0.5 copy.53
  123.6 28.3 %all_to_all.36 = bf16[32,16,1024]{2,1,0:T(8,128)(2,1)S(1)} all-to-all(bf16[32,16,1024]{2,1,0:T(8,128)(2,1)S(1)} %bitcast.81), channel_id=1, replica_groups=mesh['seq'=32,'head'=8] {'seq'}, dimensions={0} | all-to-all | bytes 2097152 | tf_op jit(solution)/shard_map/all_to_all | solution.py:138
  151.9 5.1 %convolution_convert_fusion = bf16[256,4096]{1,0:T(8,128)(2,1)} fusion(bf16[256,4096]{0,1:T(8,128)(2,1)} %bitcast.83, bf16[256,4096]{0,1:T(8,128)(2,1)} %copy-done.1, bf16[512,1024]{1,0:T(8,128)(2,1)S(1)} %bitcast.85, s32[256]{0:T(256)S(1)} %multiply_add_fusion), kind=kOutput, calls=%fused_computation.1 | convolution fusion | flops 1217658880 | bytes 6816768 | tf_op jit(solution)/shard_map/dot_general | solution.py:140
  157.0 0.3 convolution_convert_fusion.8
  157.3 0.1 copy.54
  157.6 1.0 copy-done.2
  158.5 0.3 fusion.6
  158.8 0.3 fusion.8
  159.1 0.8 convolution_convert_fusion.7
  159.9 0.2 fusion.7
  160.2 0.6 convolution_convert_fusion.1
  160.8 40.7 %all_to_all.37 = bf16[32,16,1536]{2,1,0:T(8,128)(2,1)S(1)} all-to-all(bf16[32,16,1536]{2,1,0:T(8,128)(2,1)S(1)} %bitcast.84), channel_id=1, replica_groups=mesh['seq'=32,'head'=8] {'seq'}, dimensions={0} | all-to-all | bytes 3145728 | tf_op jit(solution)/shard_map/all_to_all | solution.py:167
  201.5 0.6 convolution_convert_fusion.3
  202.2 0.9 fusion.68
  (70 shorter events, 1.5 us)
Async XLA Ops:
  7.2 24.4 %copy-start = (s32[32,2,2]{0,2,1:T(2,128)S(1)}, s32[32,2,2]{0,2,1:T(2,128)}, u32[]{:S(2)}) copy-start(s32[32,2,2]{0,2,1:T(2,128)} %param.13) | copy-start | bytes 1540
  7.2 111.3 %all-gather.2.cloned.1.call-start = ((), (), s32[]{:S(2)}) async-start(), calls=%async_computation.4 | async-start | bytes 2359296 | tf_op jit(solution)/shard_map/all_gather | solution.py:126
  8.2 27.1 %collective-permute-start.10 = (bf16[256,128]{0,1:T(8,128)(2,1)S(1)}, bf16[256,128]{0,1:T(8,128)(2,1)S(1)}, u32[]{:S(2)}, u32[]{:S(2)}) collective-permute-start(bf16[256,128]{0,1:T(8,128)(2,1)S(1)} %copy.70), channel_id=1, source_target_pairs={{0,32},{8,40},{16,48},{24,56},{32,64},{40,72},{48,80},{56,88},{64,... | collective-permute-start | bytes 196616 | tf_op jit(solution)/shard_map/ppermute | solution.py:38
  10.2 27.0 %collective-permute-start.11 = (bf16[256,128]{0,1:T(8,128)(2,1)S(1)}, bf16[256,128]{0,1:T(8,128)(2,1)S(1)}, u32[]{:S(2)}, u32[]{:S(2)}) collective-permute-start(bf16[256,128]{0,1:T(8,128)(2,1)S(1)} %copy.70), channel_id=1, source_target_pairs={{0,224},{8,232},{16,240},{24,248},{32,0},{40,8},{48,16},{56,24},{6... | collective-permute-start | bytes 196616 | tf_op jit(solution)/shard_map/ppermute | solution.py:41
  14.4 24.3 %collective-permute-start = (bf16[256,128]{0,1:T(8,128)(2,1)S(1)}, bf16[256,128]{0,1:T(8,128)(2,1)S(1)}, u32[]{:S(2)}, u32[]{:S(2)}) collective-permute-start(bf16[256,128]{0,1:T(8,128)(2,1)S(1)} %copy.69), channel_id=1, source_target_pairs={{0,8},{8,16},{16,24},{24,0},{32,40},{40,48},{48,56},{56,32},{64,72... | collective-permute-start | bytes 196616 | tf_op jit(solution)/shard_map/ppermute | solution.py:38
  16.0 24.5 %collective-permute-start.1 = (bf16[256,128]{0,1:T(8,128)(2,1)S(1)}, bf16[256,128]{0,1:T(8,128)(2,1)S(1)}, u32[]{:S(2)}, u32[]{:S(2)}) collective-permute-start(bf16[256,128]{0,1:T(8,128)(2,1)S(1)} %copy.69), channel_id=1, source_target_pairs={{0,24},{8,0},{16,8},{24,16},{32,56},{40,32},{48,40},{56,48},{64,88... | collective-permute-start | bytes 196616 | tf_op jit(solution)/shard_map/ppermute | solution.py:41
  23.6 90.2 %all-to-all-start = ((bf16[32,16,1664]{2,1,0:T(8,128)(2,1)}), bf16[32,16,1664]{2,1,0:T(8,128)(2,1)S(1)}, u32[]{:S(2)}, u32[]{:S(2)}) async-start(bf16[32,16,1664]{2,1,0:T(8,128)(2,1)} %bitcast.2), calls=%async_computation | async-start | bytes 3407872 | tf_op jit(solution)/shard_map/all_to_all | solution.py:86
  31.2 171.8 %reduce-scatter.2.cloned.1.call-start = ((), (), s32[]{:S(2)}) async-start(), calls=%async_computation.5 | async-start | bytes 2359296 | tf_op jit(solution)/shard_map/reduce_scatter | solution.py:142
  35.3 37.5 %collective-permute-start.12 = (bf16[256,128]{0,1:T(8,128)(2,1)S(1)}, bf16[256,128]{0,1:T(8,128)(2,1)S(1)}, u32[]{:S(2)}, u32[]{:S(2)}) collective-permute-start(bf16[256,128]{0,1:T(8,128)(2,1)S(1)} %collective-permute-done.10), channel_id=1, source_target_pairs={{0,32},{8,40},{16,48},{24,56},{32,64},{40,72},{48,80},{56,88},{64,... | collective-permute-start | bytes 196616 | tf_op jit(solution)/shard_map/ppermute | solution.py:38
  37.2 35.6 %collective-permute-start.13 = (bf16[256,128]{0,1:T(8,128)(2,1)S(1)}, bf16[256,128]{0,1:T(8,128)(2,1)S(1)}, u32[]{:S(2)}, u32[]{:S(2)}) collective-permute-start(bf16[256,128]{0,1:T(8,128)(2,1)S(1)} %collective-permute-done.11), channel_id=1, source_target_pairs={{0,224},{8,232},{16,240},{24,248},{32,0},{40,8},{48,16},{56,24},{6... | collective-permute-start | bytes 196616 | tf_op jit(solution)/shard_map/ppermute | solution.py:41
  38.6 6.3 %collective-permute-start.2 = (bf16[256,128]{0,1:T(8,128)(2,1)S(1)}, bf16[256,128]{0,1:T(8,128)(2,1)S(1)}, u32[]{:S(2)}, u32[]{:S(2)}) collective-permute-start(bf16[256,128]{0,1:T(8,128)(2,1)S(1)} %collective-permute-done), channel_id=1, source_target_pairs={{0,8},{8,16},{16,24},{24,0},{32,40},{40,48},{48,56},{56,32},{64,72... | collective-permute-start | bytes 196616 | tf_op jit(solution)/shard_map/ppermute | solution.py:38
  44.9 42.4 %collective-permute-start.3 = (bf16[256,512]{0,1:T(8,128)(2,1)S(1)}, bf16[256,512]{0,1:T(8,128)(2,1)S(1)}, u32[]{:S(2)}, u32[]{:S(2)}) collective-permute-start(bf16[256,512]{0,1:T(8,128)(2,1)S(1)} %constant_dynamic-update-slice_fusion.20), channel_id=1, source_target_pairs={{0,32},{8,40},{16,48},{24,56},{32,64},{40,72},{48,80},{56,88},{64,... | collective-permute-start | bytes 786440 | tf_op jit(solution)/shard_map/ppermute | solution.py:38
  45.3 42.0 %collective-permute-start.4 = (bf16[256,512]{0,1:T(8,128)(2,1)S(1)}, bf16[256,512]{0,1:T(8,128)(2,1)S(1)}, u32[]{:S(2)}, u32[]{:S(2)}) collective-permute-start(bf16[256,512]{0,1:T(8,128)(2,1)S(1)} %constant_dynamic-update-slice_fusion.20), channel_id=1, source_target_pairs={{0,224},{8,232},{16,240},{24,248},{32,0},{40,8},{48,16},{56,24},{6... | collective-permute-start | bytes 786440 | tf_op jit(solution)/shard_map/ppermute | solution.py:41
  72.8 5.6 %collective-permute-start.14 = (bf16[256,128]{0,1:T(8,128)(2,1)S(1)}, bf16[256,128]{0,1:T(8,128)(2,1)S(1)}, u32[]{:S(2)}, u32[]{:S(2)}) collective-permute-start(bf16[256,128]{0,1:T(8,128)(2,1)S(1)} %collective-permute-done.12), channel_id=1, source_target_pairs={{0,32},{8,40},{16,48},{24,56},{32,64},{40,72},{48,80},{56,88},{64,... | collective-permute-start | bytes 196616 | tf_op jit(solution)/shard_map/ppermute | solution.py:38
  72.8 5.6 %collective-permute-start.15 = (bf16[256,128]{0,1:T(8,128)(2,1)S(1)}, bf16[256,128]{0,1:T(8,128)(2,1)S(1)}, u32[]{:S(2)}, u32[]{:S(2)}) collective-permute-start(bf16[256,128]{0,1:T(8,128)(2,1)S(1)} %collective-permute-done.13), channel_id=1, source_target_pairs={{0,224},{8,232},{16,240},{24,248},{32,0},{40,8},{48,16},{56,24},{6... | collective-permute-start | bytes 196616 | tf_op jit(solution)/shard_map/ppermute | solution.py:41
  78.3 5.5 %collective-permute-start.16 = (bf16[256,128]{0,1:T(8,128)(2,1)S(1)}, bf16[256,128]{0,1:T(8,128)(2,1)S(1)}, u32[]{:S(2)}, u32[]{:S(2)}) collective-permute-start(bf16[256,128]{0,1:T(8,128)(2,1)S(1)} %collective-permute-done.14), channel_id=1, source_target_pairs={{0,32},{8,40},{16,48},{24,56},{32,64},{40,72},{48,80},{56,88},{64,... | collective-permute-start | bytes 196616 | tf_op jit(solution)/shard_map/ppermute | solution.py:38
  83.8 14.5 %collective-permute-start.17 = (bf16[256,1024]{0,1:T(8,128)(2,1)S(1)}, bf16[256,1024]{0,1:T(8,128)(2,1)S(1)}, u32[]{:S(2)}, u32[]{:S(2)}) collective-permute-start(bf16[256,1024]{0,1:T(8,128)(2,1)S(1)} %constant_dynamic-update-slice_fusion.4), channel_id=1, source_target_pairs={{0,8},{8,16},{16,24},{24,0},{32,40},{40,48},{48,56},{56,32},{64,72... | collective-permute-start | bytes 1572872 | tf_op jit(solution)/shard_map/ppermute | solution.py:38
  85.5 17.9 %collective-permute-start.18 = (bf16[256,1024]{0,1:T(8,128)(2,1)S(1)}, bf16[256,1024]{0,1:T(8,128)(2,1)S(1)}, u32[]{:S(2)}, u32[]{:S(2)}) collective-permute-start(bf16[256,1024]{0,1:T(8,128)(2,1)S(1)} %constant_dynamic-update-slice_fusion.4), channel_id=1, source_target_pairs={{0,24},{8,0},{16,8},{24,16},{32,56},{40,32},{48,40},{56,48},{64,88... | collective-permute-start | bytes 1572872 | tf_op jit(solution)/shard_map/ppermute | solution.py:41
  87.3 7.6 %collective-permute-start.5 = (bf16[256,512]{0,1:T(8,128)(2,1)S(1)}, bf16[256,512]{0,1:T(8,128)(2,1)S(1)}, u32[]{:S(2)}, u32[]{:S(2)}) collective-permute-start(bf16[256,512]{0,1:T(8,128)(2,1)S(1)} %collective-permute-done.3), channel_id=1, source_target_pairs={{0,32},{8,40},{16,48},{24,56},{32,64},{40,72},{48,80},{56,88},{64,... | collective-permute-start | bytes 786440 | tf_op jit(solution)/shard_map/ppermute | solution.py:38
  87.3 7.6 %collective-permute-start.6 = (bf16[256,512]{0,1:T(8,128)(2,1)S(1)}, bf16[256,512]{0,1:T(8,128)(2,1)S(1)}, u32[]{:S(2)}, u32[]{:S(2)}) collective-permute-start(bf16[256,512]{0,1:T(8,128)(2,1)S(1)} %collective-permute-done.4), channel_id=1, source_target_pairs={{0,224},{8,232},{16,240},{24,248},{32,0},{40,8},{48,16},{56,24},{6... | collective-permute-start | bytes 786440 | tf_op jit(solution)/shard_map/ppermute | solution.py:41
  94.9 8.5 %collective-permute-start.7 = (bf16[256,512]{0,1:T(8,128)(2,1)S(1)}, bf16[256,512]{0,1:T(8,128)(2,1)S(1)}, u32[]{:S(2)}, u32[]{:S(2)}) collective-permute-start(bf16[256,512]{0,1:T(8,128)(2,1)S(1)} %collective-permute-done.5), channel_id=1, source_target_pairs={{0,32},{8,40},{16,48},{24,56},{32,64},{40,72},{48,80},{56,88},{64,... | collective-permute-start | bytes 786440 | tf_op jit(solution)/shard_map/ppermute | solution.py:38
  94.9 8.6 %collective-permute-start.8 = (bf16[256,512]{0,1:T(8,128)(2,1)S(1)}, bf16[256,512]{0,1:T(8,128)(2,1)S(1)}, u32[]{:S(2)}, u32[]{:S(2)}) collective-permute-start(bf16[256,512]{0,1:T(8,128)(2,1)S(1)} %collective-permute-done.6), channel_id=1, source_target_pairs={{0,224},{8,232},{16,240},{24,248},{32,0},{40,8},{48,16},{56,24},{6... | collective-permute-start | bytes 786440 | tf_op jit(solution)/shard_map/ppermute | solution.py:41
  98.3 12.8 %collective-permute-start.19 = (bf16[256,1024]{0,1:T(8,128)(2,1)S(1)}, bf16[256,1024]{0,1:T(8,128)(2,1)S(1)}, u32[]{:S(2)}, u32[]{:S(2)}) collective-permute-start(bf16[256,1024]{0,1:T(8,128)(2,1)S(1)} %collective-permute-done.17), channel_id=1, source_target_pairs={{0,8},{8,16},{16,24},{24,0},{32,40},{40,48},{48,56},{56,32},{64,72... | collective-permute-start | bytes 1572872 | tf_op jit(solution)/shard_map/ppermute | solution.py:38
  103.4 7.6 %collective-permute-start.9 = (bf16[256,512]{0,1:T(8,128)(2,1)S(1)}, bf16[256,512]{0,1:T(8,128)(2,1)S(1)}, u32[]{:S(2)}, u32[]{:S(2)}) collective-permute-start(bf16[256,512]{0,1:T(8,128)(2,1)S(1)} %collective-permute-done.7), channel_id=1, source_target_pairs={{0,32},{8,40},{16,48},{24,56},{32,64},{40,72},{48,80},{56,88},{64,... | collective-permute-start | bytes 786440 | tf_op jit(solution)/shard_map/ppermute | solution.py:38
  111.0 1.3 copy-start.1
  157.3 1.2 copy-start.2
Sparse Core Ops, SparseCore 0:
  17.8 25.8 all-gather.1
  157.4 28.3 reduce-scatter.1

commit v10 on v7

--- a/solution.py
+++ b/solution.py
@@ -72,19 +72,20 @@
         jnp.arange(slot_total, dtype=jnp.int32)[:, None] == slot_index[None, :]
     ).astype(jnp.bfloat16)
 
+    live_flag = jnp.ones((tokens, HD), queries.dtype)
+    qkv = jnp.concatenate([queries, key_rows, value_rows, live_flag], axis=1)
+    qkv_in = lax.all_to_all(select_rows(to_slot, qkv), "seq", 0, 0, tiled=True)
+
+    qkv_in, weight_in = lax.optimization_barrier((qkv_in, out_weight))
     ring_y = 4 if groups % 4 == 0 else 1
     half_rows = out_weight.shape[0] // 2
     full_weight = jnp.concatenate(
         [
-            ring_gather_cols(out_weight[:half_rows], "seq", ring_y, groups // ring_y),
-            ring_gather_cols(out_weight[half_rows:], "seq", ring_y, groups // ring_y, True),
+            ring_gather_cols(weight_in[:half_rows], "seq", ring_y, groups // ring_y),
+            ring_gather_cols(weight_in[half_rows:], "seq", ring_y, groups // ring_y, True),
         ],
         axis=0,
     )
-    live_flag = jnp.ones((tokens, HD), queries.dtype)
-    qkv = jnp.concatenate([queries, key_rows, value_rows, live_flag], axis=1)
-    qkv_in = lax.all_to_all(select_rows(to_slot, qkv), "seq", 0, 0, tiled=True)
-
     row_live = qkv_in[:, 3 * width] > 0.5
     got_counts = jnp.sum(row_live.reshape(groups, slot_rows).astype(jnp.int32), axis=1)
     offsets = jnp.cumsum(got_counts) - got_counts

time: 209 us -> 214 us (1.024)
  waiting for transfers between devices: 59.1 us -> 77.7 us
  local copies, waits for them, and re-layouts: 12.7 us -> 3.68 us
  matrix products: 23.3 us -> 20.7 us
    all_to_all x1, waiting for transfers between devices: 0.01 us -> 37.2 us  [on_device(): qkv_in = lax.all_to_all(select_rows(to_slot, qkv), 'seq', 0, 0, tiled=True)]
    ppermute x12, waiting for transfers between devices: 46.7 us -> 31.3 us  [ring(): fwd = lax.ppermute(fwd, axis_name, step_perm(1))]
    dynamic_update_slice x12, local copies, waits for them, and re-layouts: 6.03 us -> 0.22 us  [ring(): out = lax.dynamic_update_slice(out, fwd, (0, (pos - step) % count * width))]
    all_to_all x1, waiting for transfers between devices: 3.83 us -> 0.01 us  [on_device(): lax.all_to_all(select_rows_t(to_rank, attn_c.reshape(ranks, width)), 'seq...]
    ppermute x12, starting transfers between devices: 5.49 us -> 8.62 us  [ring(): fwd = lax.ppermute(fwd, axis_name, step_perm(1))]
    all_to_all x1, starting transfers between devices: 7.11 us -> 4.5 us  [on_device(): lax.all_to_all(select_rows_t(to_rank, attn_c.reshape(ranks, width)), 'seq...]
  transfers between devices with their start and end apart: 25 -> 25, of which waited for: 7 -> 9; matrix products, arithmetic and copies ran while one was open for 16% -> 10% of each run, Pallas kernels for 0% -> 0%
where the time goes in v10:
time: 214 us
  waiting for transfers between devices  77.7 us (36%)
  starting transfers between devices  51.2 us (24%)
  blocking collectives  37 us (17%)
  matrix products  20.7 us (10%)
  between operations  14.8 us (7%)
  other arithmetic  8.5 us (4%)
  local copies, waits for them, and re-layouts  3.68 us (2%)
    all_to_all x1, waiting for transfers between devices, on_device(): qkv_in = lax.all_to_all(select_rows(to_slot, qkv), 'seq', 0, 0, tiled=True)  37.2 us
    all_to_all x1, blocking collectives, on_device(): lax.all_to_all(select_rows_t(to_rank, grads_c), 'seq', 0, 0, tiled=True)  37 us
    ppermute x12, waiting for transfers between devices, ring(): fwd = lax.ppermute(fwd, axis_name, step_perm(1))  31.3 us
    ppermute x8, starting transfers between devices, ring(): bwd = lax.ppermute(bwd, axis_name, step_perm(-1))  20.4 us
    all_to_all x1, starting transfers between devices, on_device(): qkv_in = lax.all_to_all(select_rows(to_slot, qkv), 'seq', 0, 0, tiled=True)  11.6 us
    dot_general x4, matrix products, select_rows(): jnp.dot(onehot, rows, preferred_element_type=jnp.float32).astype(rows.dtype)  9.33 us
    ppermute x12, starting transfers between devices, ring(): fwd = lax.ppermute(fwd, axis_name, step_perm(1))  8.62 us
    all_to_all x1, waiting for transfers between devices, on_device(): lax.all_to_all(select_rows(to_slot, grad_attention), 'seq', 0, 0, tiled=T...  8.49 us
  transfers between devices with their start and end apart: 25, of which 9 were waited for; matrix products, arithmetic and copies ran while one was open for 10% of the time, Pallas kernels for 0%

profile of v10, /device:TPU:4, one launch (start us, length us, event | category | flops | bytes accessed | tf_op | source)
XLA Modules:
  0.0 213.6 jit_solution(10597423072538498265)
XLA Ops:
  7.2 0.7 fusion.48
  7.9 0.6 reduce-window.18
  8.4 0.2 slice_reduce_fusion
  8.7 0.8 fusion.47
  9.5 0.7 multiply_add_fusion
  10.2 3.0 %convolution_convert_fusion.2 = bf16[512,1664]{1,0:T(8,128)(2,1)} fusion(bf16[256,512]{1,0:T(8,128)(2,1)} %param.9, bf16[256,512]{1,0:T(8,128)(2,1)} %param.8, bf16[256,512]{1,0:T(8,128)(2,1)} %param.7, bf16[1664]{0:T(1024)(128)(2,1)S(1)} %pad.8.clone, s32[256]{0:T(256)S(1)} %multiply_add_fusion), kind=kOutput, calls=%fused_computation.4 | convolution fusion | flops 440598528 | bytes 2494720 | tf_op jit(solution)/shard_map/dot_general | solution.py:13
  13.1 11.6 %all-to-all-start = ((bf16[32,16,1664]{2,1,0:T(8,128)(2,1)}), bf16[32,16,1664]{2,1,0:T(8,128)(2,1)S(1)}, u32[]{:S(2)}, u32[]{:S(2)}) async-start(bf16[32,16,1664]{2,1,0:T(8,128)(2,1)} %bitcast.2), calls=%async_computation | async-start | bytes 3407872 | tf_op jit(solution)/shard_map/all_to_all | solution.py:77
  24.8 0.7 all-gather.2.cloned.1.call-update
  25.8 0.2 fusion.50
  26.1 0.6 fusion.62
  26.7 2.6 %broadcast_select_fusion = (s32[256]{0:T(256)S(1)}, s32[256]{0:T(256)S(1)}) fusion(s32[]{:T(128)} %bitcast.8, s32[]{:T(128)} %bitcast.7, s32[]{:T(128)} %bitcast.6, s32[]{:T(128)} %bitcast.5), kind=kLoop, calls=%fused_computation.109 | loop fusion | flops 2816 | bytes 2064 | tf_op jit(solution)/shard_map/jit(_where)/select_n | solution.py:110
  29.3 0.1 fusion.38
  29.4 37.2 %all-to-all-done = bf16[32,16,1664]{2,1,0:T(8,128)(2,1)S(1)} async-done(((bf16[32,16,1664]{2,1,0:T(8,128)(2,1)}), bf16[32,16,1664]{2,1,0:T(8,128)(2,1)S(1)}, u32[]{:S(2)}, u32[]{:S(2)}) %all-to-all-start) | async-done | bytes 1703968 | tf_op jit(solution)/shard_map/all_to_all | solution.py:77
  66.8 1.1 collective-permute-start
  67.9 2.3 %collective-permute-start.1 = (bf16[256,128]{0,1:T(8,128)(2,1)S(1)}, bf16[256,128]{0,1:T(8,128)(2,1)S(1)}, u32[]{:S(2)}, u32[]{:S(2)}) collective-permute-start(bf16[256,128]{0,1:T(8,128)(2,1)S(1)} %get-tuple-element.18), channel_id=1, source_target_pairs={{0,24},{8,0},{16,8},{24,16},{32,56},{40,32},{48,40},{56,48},{64,88... | collective-permute-start | bytes 196616 | tf_op jit(solution)/shard_map/ppermute | solution.py:41
  70.3 1.0 collective-permute-start.10
  71.3 2.2 %collective-permute-start.11 = (bf16[256,128]{0,1:T(8,128)(2,1)S(1)}, bf16[256,128]{0,1:T(8,128)(2,1)S(1)}, u32[]{:S(2)}, u32[]{:S(2)}) collective-permute-start(bf16[256,128]{0,1:T(8,128)(2,1)S(1)} %get-tuple-element.21), channel_id=1, source_target_pairs={{0,224},{8,232},{16,240},{24,248},{32,0},{40,8},{48,16},{56,24},{6... | collective-permute-start | bytes 196616 | tf_op jit(solution)/shard_map/ppermute | solution.py:41
  73.5 0.1 convert_reduce_fusion
  73.6 0.2 fusion.49
  73.9 0.1 reduce_sum.37
  74.4 0.7 convolution_convert_fusion.4
  75.2 0.1 copy.67
  75.3 0.1 copy.68
  75.4 1.5 fusion.63
  77.0 0.8 convolution_convert_fusion.11
  77.8 1.1 convolution_convert_fusion.5
  78.9 4.5 %all-to-all-start.1 = ((bf16[32,16,512]{2,1,0:T(8,128)(2,1)}), bf16[32,16,512]{2,1,0:T(8,128)(2,1)S(1)}, u32[]{:S(2)}, u32[]{:S(2)}) async-start(bf16[32,16,512]{2,1,0:T(8,128)(2,1)} %bitcast.11), calls=%async_computation.1 | async-start | bytes 1048576 | tf_op jit(solution)/shard_map/all_to_all | solution.py:125
  83.4 1.9 collective-permute-start.2
  85.3 1.5 collective-permute-start.12
  86.8 1.8 collective-permute-start.13
  88.6 1.4 collective-permute-done.2
  90.0 1.0 collective-permute-start.3
  91.1 2.4 %collective-permute-start.4 = (bf16[256,512]{0,1:T(8,128)(2,1)S(1)}, bf16[256,512]{0,1:T(8,128)(2,1)S(1)}, u32[]{:S(2)}, u32[]{:S(2)}) collective-permute-start(bf16[256,512]{0,1:T(8,128)(2,1)S(1)} %constant_dynamic-update-slice_fusion.20), channel_id=1, source_target_pairs={{0,224},{8,232},{16,240},{24,248},{32,0},{40,8},{48,16},{56,24},{6... | collective-permute-start | bytes 786440 | tf_op jit(solution)/shard_map/ppermute | solution.py:41
  93.4 5.5 %collective-permute-done.12 = bf16[256,128]{0,1:T(8,128)(2,1)S(1)} collective-permute-done((bf16[256,128]{0,1:T(8,128)(2,1)S(1)}, bf16[256,128]{0,1:T(8,128)(2,1)S(1)}, u32[]{:S(2)}, u32[]{:S(2)}) %collective-permute-start.12) | collective-permute-done | bytes 65568 | tf_op jit(solution)/shard_map/ppermute | solution.py:38
  99.0 3.2 %collective-permute-start.15 = (bf16[256,128]{0,1:T(8,128)(2,1)S(1)}, bf16[256,128]{0,1:T(8,128)(2,1)S(1)}, u32[]{:S(2)}, u32[]{:S(2)}) collective-permute-start(bf16[256,128]{0,1:T(8,128)(2,1)S(1)} %collective-permute-done.13), channel_id=1, source_target_pairs={{0,224},{8,232},{16,240},{24,248},{32,0},{40,8},{48,16},{56,24},{6... | collective-permute-start | bytes 196616 | tf_op jit(solution)/shard_map/ppermute | solution.py:41
  102.2 0.1 broadcast.206.clone.1
  102.4 2.0 collective-permute-done.14
  104.5 5.4 %collective-permute-done.16 = bf16[256,128]{0,1:T(8,128)(2,1)S(1)} collective-permute-done((bf16[256,128]{0,1:T(8,128)(2,1)S(1)}, bf16[256,128]{0,1:T(8,128)(2,1)S(1)}, u32[]{:S(2)}, u32[]{:S(2)}) %collective-permute-start.16) | collective-permute-done | bytes 65568 | tf_op jit(solution)/shard_map/ppermute | solution.py:38
  109.9 1.5 collective-permute-start.17
  111.4 1.8 collective-permute-start.18
  113.2 3.2 %collective-permute-start.6 = (bf16[256,512]{0,1:T(8,128)(2,1)S(1)}, bf16[256,512]{0,1:T(8,128)(2,1)S(1)}, u32[]{:S(2)}, u32[]{:S(2)}) collective-permute-start(bf16[256,512]{0,1:T(8,128)(2,1)S(1)} %collective-permute-done.4), channel_id=1, source_target_pairs={{0,224},{8,232},{16,240},{24,248},{32,0},{40,8},{48,16},{56,24},{6... | collective-permute-start | bytes 786440 | tf_op jit(solution)/shard_map/ppermute | solution.py:41
  116.5 0.1 broadcast.206.clone
  116.7 4.5 %collective-permute-done.5 = bf16[256,512]{0,1:T(8,128)(2,1)S(1)} collective-permute-done((bf16[256,512]{0,1:T(8,128)(2,1)S(1)}, bf16[256,512]{0,1:T(8,128)(2,1)S(1)}, u32[]{:S(2)}, u32[]{:S(2)}) %collective-permute-start.5) | collective-permute-done | bytes 262176 | tf_op jit(solution)/shard_map/ppermute | solution.py:38
  121.2 3.5 %collective-permute-start.8 = (bf16[256,512]{0,1:T(8,128)(2,1)S(1)}, bf16[256,512]{0,1:T(8,128)(2,1)S(1)}, u32[]{:S(2)}, u32[]{:S(2)}) collective-permute-start(bf16[256,512]{0,1:T(8,128)(2,1)S(1)} %collective-permute-done.6), channel_id=1, source_target_pairs={{0,224},{8,232},{16,240},{24,248},{32,0},{40,8},{48,16},{56,24},{6... | collective-permute-start | bytes 786440 | tf_op jit(solution)/shard_map/ppermute | solution.py:41
  124.8 0.6 collective-permute-start.19
  125.4 4.9 %collective-permute-done.7 = bf16[256,512]{0,1:T(8,128)(2,1)S(1)} collective-permute-done((bf16[256,512]{0,1:T(8,128)(2,1)S(1)}, bf16[256,512]{0,1:T(8,128)(2,1)S(1)}, u32[]{:S(2)}, u32[]{:S(2)}) %collective-permute-start.7) | collective-permute-done | bytes 262176 | tf_op jit(solution)/shard_map/ppermute | solution.py:38
  130.5 7.5 %collective-permute-done.9 = bf16[256,512]{0,1:T(8,128)(2,1)S(1)} collective-permute-done((bf16[256,512]{0,1:T(8,128)(2,1)S(1)}, bf16[256,512]{0,1:T(8,128)(2,1)S(1)}, u32[]{:S(2)}, u32[]{:S(2)}) %collective-permute-start.9) | collective-permute-done | bytes 262176 | tf_op jit(solution)/shard_map/ppermute | solution.py:38
  138.0 0.1 copy.51
  138.2 2.3 %pad_maximum_fusion = bf16[512,4096]{0,1:T(8,128)(2,1)} fusion(bf16[256,4096]{0,1:T(8,128)(2,1)S(1)} %bitcast.83, bf16[256,4096]{0,1:T(8,128)(2,1)S(1)} %constant_dynamic-update-slice_fusion.12), kind=kLoop, calls=%fused_computation.2 | loop fusion | flops 8388608 | bytes 8388608 | tf_op jit(solution)/shard_map/concatenate | solution.py:82
  140.5 5.4 %convolution_convert_fusion.6 = bf16[512,512]{1,0:T(8,128)(2,1)} fusion(bf16[512,4096]{0,1:T(8,128)(2,1)} %pad_maximum_fusion, bf16[256,4096]{1,0:T(8,128)(2,1)} %all-gather.2.cloned.1.call-done, s32[256]{0:T(256)S(1)} %multiply_add_fusion), kind=kOutput, calls=%fused_computation.15 | convolution fusion | flops 1208483840 | bytes 6816768 | tf_op jit(solution)/shard_map/dot_general | solution.py:13
  145.8 5.7 %all-to-all-start.2 = ((bf16[32,16,512]{2,1,0:T(8,128)(2,1)}), bf16[32,16,512]{2,1,0:T(8,128)(2,1)S(1)}, u32[]{:S(2)}, u32[]{:S(2)}) async-start(bf16[32,16,512]{2,1,0:T(8,128)(2,1)} %bitcast.16), calls=%async_computation.3 | async-start | bytes 1048576 | tf_op jit(solution)/shard_map/all_to_all | solution.py:143
  151.5 0.3 reduce-scatter.2.cloned.1.call-start
  151.8 5.0 %convolution_convert_fusion = bf16[256,4096]{1,0:T(8,128)(2,1)} fusion(bf16[512,4096]{0,1:T(8,128)(2,1)} %pad_maximum_fusion, bf16[512,512]{1,0:T(8,128)(2,1)S(1)} %bitcast.88, s32[256]{0:T(256)S(1)} %multiply_add_fusion), kind=kOutput, calls=%fused_computation.1 | convolution fusion | flops 1209270272 | bytes 6816768 | tf_op jit(solution)/shard_map/dot_general | solution.py:130
  156.9 8.5 %all-to-all-done.2 = bf16[32,16,512]{2,1,0:T(8,128)(2,1)S(1)} async-done(((bf16[32,16,512]{2,1,0:T(8,128)(2,1)}), bf16[32,16,512]{2,1,0:T(8,128)(2,1)S(1)}, u32[]{:S(2)}, u32[]{:S(2)}) %all-to-all-start.2) | async-done | bytes 524320 | tf_op jit(solution)/shard_map/all_to_all | solution.py:143
  165.4 0.3 convolution_convert_fusion.8
  165.7 0.1 copy.52
  165.9 0.3 fusion.5
  166.2 0.2 fusion.6
  166.5 0.8 convolution_convert_fusion.7
  167.3 0.3 fusion.7
  167.6 0.6 convolution_convert_fusion.1
  168.2 37.0 %all_to_all.48 = bf16[32,16,1536]{2,1,0:T(8,128)(2,1)S(1)} all-to-all(bf16[32,16,1536]{2,1,0:T(8,128)(2,1)S(1)} %bitcast.89), channel_id=1, replica_groups=mesh['seq'=32,'head'=8] {'seq'}, dimensions={0} | all-to-all | bytes 3145728 | tf_op jit(solution)/shard_map/all_to_all | solution.py:166
  205.3 0.6 convolution_convert_fusion.3
  205.9 0.9 fusion.60
  (69 shorter events, 1.5 us)
Async XLA Ops:
  7.2 18.7 %copy-start = (s32[32,2,2]{0,2,1:T(2,128)S(1)}, s32[32,2,2]{0,2,1:T(2,128)}, u32[]{:S(2)}) copy-start(s32[32,2,2]{0,2,1:T(2,128)} %param.13) | copy-start | bytes 1540
  13.1 53.5 %copy-start.1 = (bf16[512,128]{1,0:T(8,128)(2,1)S(1)}, bf16[512,128]{1,0:T(8,128)(2,1)}, u32[]{:S(2)}) copy-start(bf16[512,128]{1,0:T(8,128)(2,1)} %param.10) | copy-start | bytes 393220
  13.1 53.5 %all-to-all-start = ((bf16[32,16,1664]{2,1,0:T(8,128)(2,1)}), bf16[32,16,1664]{2,1,0:T(8,128)(2,1)S(1)}, u32[]{:S(2)}, u32[]{:S(2)}) async-start(bf16[32,16,1664]{2,1,0:T(8,128)(2,1)} %bitcast.2), calls=%async_computation | async-start | bytes 3407872 | tf_op jit(solution)/shard_map/all_to_all | solution.py:77
  24.8 115.7 %all-gather.2.cloned.1.call-start = ((), (), s32[]{:S(2)}) async-start(), calls=%async_computation.6 | async-start | bytes 2359296 | tf_op jit(solution)/shard_map/all_gather | solution.py:138
  66.8 16.6 %collective-permute-start = (bf16[256,128]{0,1:T(8,128)(2,1)S(1)}, bf16[256,128]{0,1:T(8,128)(2,1)S(1)}, u32[]{:S(2)}, u32[]{:S(2)}) collective-permute-start(bf16[256,128]{0,1:T(8,128)(2,1)S(1)} %get-tuple-element.18), channel_id=1, source_target_pairs={{0,8},{8,16},{16,24},{24,0},{32,40},{40,48},{48,56},{56,32},{64,72... | collective-permute-start | bytes 196616 | tf_op jit(solution)/shard_map/ppermute | solution.py:38
  67.9 20.7 %collective-permute-start.1 = (bf16[256,128]{0,1:T(8,128)(2,1)S(1)}, bf16[256,128]{0,1:T(8,128)(2,1)S(1)}, u32[]{:S(2)}, u32[]{:S(2)}) collective-permute-start(bf16[256,128]{0,1:T(8,128)(2,1)S(1)} %get-tuple-element.18), channel_id=1, source_target_pairs={{0,24},{8,0},{16,8},{24,16},{32,56},{40,32},{48,40},{56,48},{64,88... | collective-permute-start | bytes 196616 | tf_op jit(solution)/shard_map/ppermute | solution.py:41
  70.3 15.1 %collective-permute-start.10 = (bf16[256,128]{0,1:T(8,128)(2,1)S(1)}, bf16[256,128]{0,1:T(8,128)(2,1)S(1)}, u32[]{:S(2)}, u32[]{:S(2)}) collective-permute-start(bf16[256,128]{0,1:T(8,128)(2,1)S(1)} %get-tuple-element.21), channel_id=1, source_target_pairs={{0,32},{8,40},{16,48},{24,56},{32,64},{40,72},{48,80},{56,88},{64,... | collective-permute-start | bytes 196616 | tf_op jit(solution)/shard_map/ppermute | solution.py:38
  71.3 15.5 %collective-permute-start.11 = (bf16[256,128]{0,1:T(8,128)(2,1)S(1)}, bf16[256,128]{0,1:T(8,128)(2,1)S(1)}, u32[]{:S(2)}, u32[]{:S(2)}) collective-permute-start(bf16[256,128]{0,1:T(8,128)(2,1)S(1)} %get-tuple-element.21), channel_id=1, source_target_pairs={{0,224},{8,232},{16,240},{24,248},{32,0},{40,8},{48,16},{56,24},{6... | collective-permute-start | bytes 196616 | tf_op jit(solution)/shard_map/ppermute | solution.py:41
  78.9 61.5 %all-to-all-start.1 = ((bf16[32,16,512]{2,1,0:T(8,128)(2,1)}), bf16[32,16,512]{2,1,0:T(8,128)(2,1)S(1)}, u32[]{:S(2)}, u32[]{:S(2)}) async-start(bf16[32,16,512]{2,1,0:T(8,128)(2,1)} %bitcast.11), calls=%async_computation.1 | async-start | bytes 1048576 | tf_op jit(solution)/shard_map/all_to_all | solution.py:125
  83.4 6.6 %collective-permute-start.2 = (bf16[256,128]{0,1:T(8,128)(2,1)S(1)}, bf16[256,128]{0,1:T(8,128)(2,1)S(1)}, u32[]{:S(2)}, u32[]{:S(2)}) collective-permute-start(bf16[256,128]{0,1:T(8,128)(2,1)S(1)} %collective-permute-done), channel_id=1, source_target_pairs={{0,8},{8,16},{16,24},{24,0},{32,40},{40,48},{48,56},{56,32},{64,72... | collective-permute-start | bytes 196616 | tf_op jit(solution)/shard_map/ppermute | solution.py:38
  85.3 13.6 %collective-permute-start.12 = (bf16[256,128]{0,1:T(8,128)(2,1)S(1)}, bf16[256,128]{0,1:T(8,128)(2,1)S(1)}, u32[]{:S(2)}, u32[]{:S(2)}) collective-permute-start(bf16[256,128]{0,1:T(8,128)(2,1)S(1)} %collective-permute-done.10), channel_id=1, source_target_pairs={{0,32},{8,40},{16,48},{24,56},{32,64},{40,72},{48,80},{56,88},{64,... | collective-permute-start | bytes 196616 | tf_op jit(solution)/shard_map/ppermute | solution.py:38
  86.8 12.2 %collective-permute-start.13 = (bf16[256,128]{0,1:T(8,128)(2,1)S(1)}, bf16[256,128]{0,1:T(8,128)(2,1)S(1)}, u32[]{:S(2)}, u32[]{:S(2)}) collective-permute-start(bf16[256,128]{0,1:T(8,128)(2,1)S(1)} %collective-permute-done.11), channel_id=1, source_target_pairs={{0,224},{8,232},{16,240},{24,248},{32,0},{40,8},{48,16},{56,24},{6... | collective-permute-start | bytes 196616 | tf_op jit(solution)/shard_map/ppermute | solution.py:41
  90.0 23.2 %collective-permute-start.3 = (bf16[256,512]{0,1:T(8,128)(2,1)S(1)}, bf16[256,512]{0,1:T(8,128)(2,1)S(1)}, u32[]{:S(2)}, u32[]{:S(2)}) collective-permute-start(bf16[256,512]{0,1:T(8,128)(2,1)S(1)} %constant_dynamic-update-slice_fusion.20), channel_id=1, source_target_pairs={{0,32},{8,40},{16,48},{24,56},{32,64},{40,72},{48,80},{56,88},{64,... | collective-permute-start | bytes 786440 | tf_op jit(solution)/shard_map/ppermute | solution.py:38
  91.1 22.2 %collective-permute-start.4 = (bf16[256,512]{0,1:T(8,128)(2,1)S(1)}, bf16[256,512]{0,1:T(8,128)(2,1)S(1)}, u32[]{:S(2)}, u32[]{:S(2)}) collective-permute-start(bf16[256,512]{0,1:T(8,128)(2,1)S(1)} %constant_dynamic-update-slice_fusion.20), channel_id=1, source_target_pairs={{0,224},{8,232},{16,240},{24,248},{32,0},{40,8},{48,16},{56,24},{6... | collective-permute-start | bytes 786440 | tf_op jit(solution)/shard_map/ppermute | solution.py:41
  98.9 5.5 %collective-permute-start.14 = (bf16[256,128]{0,1:T(8,128)(2,1)S(1)}, bf16[256,128]{0,1:T(8,128)(2,1)S(1)}, u32[]{:S(2)}, u32[]{:S(2)}) collective-permute-start(bf16[256,128]{0,1:T(8,128)(2,1)S(1)} %collective-permute-done.12), channel_id=1, source_target_pairs={{0,32},{8,40},{16,48},{24,56},{32,64},{40,72},{48,80},{56,88},{64,... | collective-permute-start | bytes 196616 | tf_op jit(solution)/shard_map/ppermute | solution.py:38
  99.0 5.5 %collective-permute-start.15 = (bf16[256,128]{0,1:T(8,128)(2,1)S(1)}, bf16[256,128]{0,1:T(8,128)(2,1)S(1)}, u32[]{:S(2)}, u32[]{:S(2)}) collective-permute-start(bf16[256,128]{0,1:T(8,128)(2,1)S(1)} %collective-permute-done.13), channel_id=1, source_target_pairs={{0,224},{8,232},{16,240},{24,248},{32,0},{40,8},{48,16},{56,24},{6... | collective-permute-start | bytes 196616 | tf_op jit(solution)/shard_map/ppermute | solution.py:41
  104.4 5.5 %collective-permute-start.16 = (bf16[256,128]{0,1:T(8,128)(2,1)S(1)}, bf16[256,128]{0,1:T(8,128)(2,1)S(1)}, u32[]{:S(2)}, u32[]{:S(2)}) collective-permute-start(bf16[256,128]{0,1:T(8,128)(2,1)S(1)} %collective-permute-done.14), channel_id=1, source_target_pairs={{0,32},{8,40},{16,48},{24,56},{32,64},{40,72},{48,80},{56,88},{64,... | collective-permute-start | bytes 196616 | tf_op jit(solution)/shard_map/ppermute | solution.py:38
  109.9 14.9 %collective-permute-start.17 = (bf16[256,1024]{0,1:T(8,128)(2,1)S(1)}, bf16[256,1024]{0,1:T(8,128)(2,1)S(1)}, u32[]{:S(2)}, u32[]{:S(2)}) collective-permute-start(bf16[256,1024]{0,1:T(8,128)(2,1)S(1)} %constant_dynamic-update-slice_fusion.4), channel_id=1, source_target_pairs={{0,8},{8,16},{16,24},{24,0},{32,40},{40,48},{48,56},{56,32},{64,72... | collective-permute-start | bytes 1572872 | tf_op jit(solution)/shard_map/ppermute | solution.py:38
  111.4 18.9 %collective-permute-start.18 = (bf16[256,1024]{0,1:T(8,128)(2,1)S(1)}, bf16[256,1024]{0,1:T(8,128)(2,1)S(1)}, u32[]{:S(2)}, u32[]{:S(2)}) collective-permute-start(bf16[256,1024]{0,1:T(8,128)(2,1)S(1)} %constant_dynamic-update-slice_fusion.4), channel_id=1, source_target_pairs={{0,24},{8,0},{16,8},{24,16},{32,56},{40,32},{48,40},{56,48},{64,88... | collective-permute-start | bytes 1572872 | tf_op jit(solution)/shard_map/ppermute | solution.py:41
  113.2 8.0 %collective-permute-start.5 = (bf16[256,512]{0,1:T(8,128)(2,1)S(1)}, bf16[256,512]{0,1:T(8,128)(2,1)S(1)}, u32[]{:S(2)}, u32[]{:S(2)}) collective-permute-start(bf16[256,512]{0,1:T(8,128)(2,1)S(1)} %collective-permute-done.3), channel_id=1, source_target_pairs={{0,32},{8,40},{16,48},{24,56},{32,64},{40,72},{48,80},{56,88},{64,... | collective-permute-start | bytes 786440 | tf_op jit(solution)/shard_map/ppermute | solution.py:38
  113.2 8.0 %collective-permute-start.6 = (bf16[256,512]{0,1:T(8,128)(2,1)S(1)}, bf16[256,512]{0,1:T(8,128)(2,1)S(1)}, u32[]{:S(2)}, u32[]{:S(2)}) collective-permute-start(bf16[256,512]{0,1:T(8,128)(2,1)S(1)} %collective-permute-done.4), channel_id=1, source_target_pairs={{0,224},{8,232},{16,240},{24,248},{32,0},{40,8},{48,16},{56,24},{6... | collective-permute-start | bytes 786440 | tf_op jit(solution)/shard_map/ppermute | solution.py:41
  121.2 9.1 %collective-permute-start.7 = (bf16[256,512]{0,1:T(8,128)(2,1)S(1)}, bf16[256,512]{0,1:T(8,128)(2,1)S(1)}, u32[]{:S(2)}, u32[]{:S(2)}) collective-permute-start(bf16[256,512]{0,1:T(8,128)(2,1)S(1)} %collective-permute-done.5), channel_id=1, source_target_pairs={{0,32},{8,40},{16,48},{24,56},{32,64},{40,72},{48,80},{56,88},{64,... | collective-permute-start | bytes 786440 | tf_op jit(solution)/shard_map/ppermute | solution.py:38
  121.2 9.2 %collective-permute-start.8 = (bf16[256,512]{0,1:T(8,128)(2,1)S(1)}, bf16[256,512]{0,1:T(8,128)(2,1)S(1)}, u32[]{:S(2)}, u32[]{:S(2)}) collective-permute-start(bf16[256,512]{0,1:T(8,128)(2,1)S(1)} %collective-permute-done.6), channel_id=1, source_target_pairs={{0,224},{8,232},{16,240},{24,248},{32,0},{40,8},{48,16},{56,24},{6... | collective-permute-start | bytes 786440 | tf_op jit(solution)/shard_map/ppermute | solution.py:41
  124.8 13.2 %collective-permute-start.19 = (bf16[256,1024]{0,1:T(8,128)(2,1)S(1)}, bf16[256,1024]{0,1:T(8,128)(2,1)S(1)}, u32[]{:S(2)}, u32[]{:S(2)}) collective-permute-start(bf16[256,1024]{0,1:T(8,128)(2,1)S(1)} %collective-permute-done.17), channel_id=1, source_target_pairs={{0,8},{8,16},{16,24},{24,0},{32,40},{40,48},{48,56},{56,32},{64,72... | collective-permute-start | bytes 1572872 | tf_op jit(solution)/shard_map/ppermute | solution.py:38
  130.4 7.6 %collective-permute-start.9 = (bf16[256,512]{0,1:T(8,128)(2,1)S(1)}, bf16[256,512]{0,1:T(8,128)(2,1)S(1)}, u32[]{:S(2)}, u32[]{:S(2)}) collective-permute-start(bf16[256,512]{0,1:T(8,128)(2,1)S(1)} %collective-permute-done.7), channel_id=1, source_target_pairs={{0,32},{8,40},{16,48},{24,56},{32,64},{40,72},{48,80},{56,88},{64,... | collective-permute-start | bytes 786440 | tf_op jit(solution)/shard_map/ppermute | solution.py:38
  145.8 19.5 %all-to-all-start.2 = ((bf16[32,16,512]{2,1,0:T(8,128)(2,1)}), bf16[32,16,512]{2,1,0:T(8,128)(2,1)S(1)}, u32[]{:S(2)}, u32[]{:S(2)}) async-start(bf16[32,16,512]{2,1,0:T(8,128)(2,1)} %bitcast.16), calls=%async_computation.3 | async-start | bytes 1048576 | tf_op jit(solution)/shard_map/all_to_all | solution.py:143
  151.5 55.2 %reduce-scatter.2.cloned.1.call-start = ((), (), s32[]{:S(2)}) async-start(), calls=%async_computation.5 | async-start | bytes 2359296 | tf_op jit(solution)/shard_map/reduce_scatter | solution.py:132
  156.9 9.1 %copy-start.2 = (f32[4,256,256]{1,2,0:T(8,128)S(1)}, f32[4,256,256]{1,2,0:T(8,128)}, u32[]{:S(2)}) copy-start(f32[4,256,256]{1,2,0:T(8,128)} %get-tuple-element.27) | copy-start | bytes 3145732
Sparse Core Ops, SparseCore 0:
  27.4 28.1 all-gather.1
  157.0 32.7 reduce-scatter.1

commit v11 on v7

--- a/solution.py
+++ b/solution.py
@@ -74,13 +74,8 @@
 
     ring_y = 4 if groups % 4 == 0 else 1
     half_rows = out_weight.shape[0] // 2
-    full_weight = jnp.concatenate(
-        [
-            ring_gather_cols(out_weight[:half_rows], "seq", ring_y, groups // ring_y),
-            ring_gather_cols(out_weight[half_rows:], "seq", ring_y, groups // ring_y, True),
-        ],
-        axis=0,
-    )
+    weight_a = ring_gather_cols(out_weight[:half_rows], "seq", ring_y, groups // ring_y)
+    weight_b = ring_gather_cols(out_weight[half_rows:], "seq", ring_y, groups // ring_y, True)
     live_flag = jnp.ones((tokens, HD), queries.dtype)
     qkv = jnp.concatenate([queries, key_rows, value_rows, live_flag], axis=1)
     qkv_in = lax.all_to_all(select_rows(to_slot, qkv), "seq", 0, 0, tiled=True)
@@ -124,19 +119,23 @@
     attn_back = lax.all_to_all(
         select_rows_t(to_rank, attn_c.reshape(ranks, width)), "seq", 0, 0, tiled=True
     )
-    attn_back, full_weight = lax.optimization_barrier((attn_back, full_weight))
+    attn_back, weight_a, weight_b = lax.optimization_barrier((attn_back, weight_a, weight_b))
     attn_local = select_rows_t(to_slot, attn_back)
-    partial_value = jnp.dot(attn_local, full_weight, preferred_element_type=jnp.float32)
+    partial_value = jnp.dot(
+        attn_local[:, :half_rows], weight_a, preferred_element_type=jnp.float32
+    ) + jnp.dot(attn_local[:, half_rows:], weight_b, preferred_element_type=jnp.float32)
     rounded_part = lax.optimization_barrier(partial_value.astype(jnp.bfloat16)).astype(jnp.float32)
     layer_out = lax.psum_scatter(
         rounded_part.astype(jnp.bfloat16), "head", scatter_dimension=1, tiled=True
     )
 
-    grad_sum = jnp.einsum(
-        "td,wd->tw",
-        lax.all_gather(grad_output, "head", axis=1, tiled=True),
-        full_weight,
-        preferred_element_type=jnp.float32,
+    grad_full = lax.all_gather(grad_output, "head", axis=1, tiled=True)
+    grad_sum = jnp.concatenate(
+        [
+            jnp.einsum("td,wd->tw", grad_full, weight_a, preferred_element_type=jnp.float32),
+            jnp.einsum("td,wd->tw", grad_full, weight_b, preferred_element_type=jnp.float32),
+        ],
+        axis=1,
     )
     grad_attention = grad_sum.astype(jnp.bfloat16)
     grad_in = lax.all_to_all(select_rows(to_slot, grad_attention), "seq", 0, 0, tiled=True)

time: 209 us -> 221 us (1.057)
  local copies, waits for them, and re-layouts: 12.7 us -> 20.3 us
  blocking collectives: 35.2 us -> 40.3 us
    all_to_all x1, blocking collectives: 35.2 us -> 40.3 us  [on_device(): lax.all_to_all(select_rows_t(to_rank, grads_c), 'seq', 0, 0, tiled=True)]
    dot_general x1 -> x4, matrix products: 5.03 us -> 9.32 us  [the longest x1 3.72 us: on_device(): jnp.dot(attn_local[:, :half_rows], weight_a, preferred_element_type=jnp.f...]
    dot_general x4, matrix products: 10.8 us -> 6.57 us  [select_rows(): jnp.dot(onehot, rows, preferred_element_type=jnp.float32).astype(rows.dtype)]
    all_to_all x1, waiting for transfers between devices: 3.83 us -> 0.01 us  [on_device(): lax.all_to_all(select_rows_t(to_rank, attn_c.reshape(ranks, width)), 'seq...]
    dynamic_update_slice x8, local copies, waits for them, and re-layouts: 1.82 us -> 5.2 us  [ring(): out = lax.dynamic_update_slice(out, bwd, (0, (pos + step) % count * width))]
    ppermute x12, starting transfers between devices: 5.49 us -> 8.32 us  [ring(): fwd = lax.ppermute(fwd, axis_name, step_perm(1))]
    ppermute x12, waiting for transfers between devices: 46.7 us -> 49 us  [ring(): fwd = lax.ppermute(fwd, axis_name, step_perm(1))]
    concatenate x1 -> x0, other arithmetic: 2.26 us -> none  [on_device(): jnp.concatenate([ring_gather_cols(out_weight[:half_rows], 'seq', ring_y,...]
  transfers between devices with their start and end apart: 25 -> 25, of which waited for: 7 -> 7; matrix products, arithmetic and copies ran while one was open for 16% -> 18% of each run, Pallas kernels for 0% -> 0%
where the time goes in v11:
time: 221 us; the launch traced here: 220 us
  waiting for transfers between devices  57.9 us (26%)
  starting transfers between devices  53.5 us (24%)
  blocking collectives  40.3 us (18%)
  matrix products  24.6 us (11%)
  local copies, waits for them, and re-layouts  20.3 us (9%)
  between operations  14.9 us (7%)
  other arithmetic  8.69 us (4%)
    ppermute x12, waiting for transfers between devices, ring(): fwd = lax.ppermute(fwd, axis_name, step_perm(1))  49 us
    all_to_all x1, blocking collectives, on_device(): lax.all_to_all(select_rows_t(to_rank, grads_c), 'seq', 0, 0, tiled=True)  40.3 us
    ppermute x8, starting transfers between devices, ring(): bwd = lax.ppermute(bwd, axis_name, step_perm(-1))  20.7 us
    all_to_all x1, starting transfers between devices, on_device(): qkv_in = lax.all_to_all(select_rows(to_slot, qkv), 'seq', 0, 0, tiled=True)  11.7 us
    all_to_all x1, waiting for transfers between devices, on_device(): lax.all_to_all(select_rows(to_slot, grad_attention), 'seq', 0, 0, tiled=T...  8.82 us
    ppermute x12, starting transfers between devices, ring(): fwd = lax.ppermute(fwd, axis_name, step_perm(1))  8.32 us
    all_to_all x1, starting transfers between devices, on_device(): lax.all_to_all(select_rows(to_slot, grad_attention), 'seq', 0, 0, tiled=T...  7.18 us
    dot_general x4, matrix products, select_rows(): jnp.dot(onehot, rows, preferred_element_type=jnp.float32).astype(rows.dtype)  6.57 us
  transfers between devices with their start and end apart: 25, of which 7 were waited for; matrix products, arithmetic and copies ran while one was open for 18% of the time, Pallas kernels for 0%

profile of v11, /device:TPU:4, one launch (start us, length us, event | category | flops | bytes accessed | tf_op | source)
XLA Modules:
  0.0 220.1 jit_solution(955604662533348634)
XLA Ops:
  7.2 0.7 fusion.56
  7.9 0.6 reduce-window.18
  8.7 0.8 fusion.55
  9.5 0.7 multiply_add_fusion
  10.2 3.0 %convolution_convert_fusion.1 = bf16[512,1664]{1,0:T(8,128)(2,1)} fusion(bf16[256,512]{1,0:T(8,128)(2,1)} %param.9, bf16[256,512]{1,0:T(8,128)(2,1)} %param.8, bf16[256,512]{1,0:T(8,128)(2,1)} %param.7, bf16[1664]{0:T(1024)(128)(2,1)S(1)} %pad.8.clone, s32[256]{0:T(256)S(1)} %multiply_add_fusion), kind=kOutput, calls=%fused_computation.4 | convolution fusion | flops 440598528 | bytes 2494720 | tf_op jit(solution)/shard_map/dot_general | solution.py:13
  13.1 11.7 %all-to-all-start = ((bf16[32,16,1664]{2,1,0:T(8,128)(2,1)}), bf16[32,16,1664]{2,1,0:T(8,128)(2,1)}, u32[]{:S(2)}, u32[]{:S(2)}) async-start(bf16[32,16,1664]{2,1,0:T(8,128)(2,1)} %bitcast.2), calls=%async_computation | async-start | bytes 3407872 | tf_op jit(solution)/shard_map/all_to_all | solution.py:81
  25.1 1.8 collective-permute-start.10
  26.9 1.5 collective-permute-start.11
  28.5 1.8 collective-permute-start
  30.3 1.5 collective-permute-start.1
  32.4 0.6 fusion.71
  33.0 2.6 %broadcast_select_fusion = (s32[256]{0:T(256)S(1)}, s32[256]{0:T(256)S(1)}) fusion(s32[]{:T(128)} %bitcast.8, s32[]{:T(128)} %bitcast.7, s32[]{:T(128)} %bitcast.6, s32[]{:T(128)} %bitcast.5), kind=kLoop, calls=%fused_computation.118 | loop fusion | flops 2816 | bytes 2064 | tf_op jit(solution)/shard_map/jit(_where)/select_n | solution.py:104
  35.7 0.8 fusion.43
  36.5 28.9 %collective-permute-done.10 = bf16[256,128]{0,1:T(8,128)(2,1)S(1)} collective-permute-done((bf16[256,128]{0,1:T(8,128)(2,1)S(1)}, bf16[256,128]{0,1:T(8,128)(2,1)S(1)}, u32[]{:S(2)}, u32[]{:S(2)}) %collective-permute-start.10) | collective-permute-done | bytes 65568 | tf_op jit(solution)/shard_map/ppermute | solution.py:38
  65.4 3.2 %collective-permute-start.13 = (bf16[256,128]{0,1:T(8,128)(2,1)S(1)}, bf16[256,128]{0,1:T(8,128)(2,1)S(1)}, u32[]{:S(2)}, u32[]{:S(2)}) collective-permute-start(bf16[256,128]{0,1:T(8,128)(2,1)S(1)} %collective-permute-done.11), channel_id=1, source_target_pairs={{0,224},{8,232},{16,240},{24,248},{32,0},{40,8},{48,16},{56,24},{6... | collective-permute-start | bytes 196616 | tf_op jit(solution)/shard_map/ppermute | solution.py:41
  68.7 0.8 collective-permute-start.2
  69.6 4.6 %collective-permute-done.2 = bf16[256,128]{0,1:T(8,128)(2,1)S(1)} collective-permute-done((bf16[256,128]{0,1:T(8,128)(2,1)S(1)}, bf16[256,128]{0,1:T(8,128)(2,1)S(1)}, u32[]{:S(2)}, u32[]{:S(2)}) %collective-permute-start.2) | collective-permute-done | bytes 65568 | tf_op jit(solution)/shard_map/ppermute | solution.py:38
  74.2 3.2 %collective-permute-start.4 = (bf16[256,512]{0,1:T(8,128)(2,1)S(1)}, bf16[256,512]{0,1:T(8,128)(2,1)}, u32[]{:S(2)}, u32[]{:S(2)}) collective-permute-start(bf16[256,512]{0,1:T(8,128)(2,1)S(1)} %constant_dynamic-update-slice_fusion.20), channel_id=1, source_target_pairs={{0,224},{8,232},{16,240},{24,248},{32,0},{40,8},{48,16},{56,24},{6... | collective-permute-start | bytes 786440 | tf_op jit(solution)/shard_map/ppermute | solution.py:41
  77.5 3.2 %collective-permute-start.15 = (bf16[256,128]{0,1:T(8,128)(2,1)S(1)}, bf16[256,128]{0,1:T(8,128)(2,1)S(1)}, u32[]{:S(2)}, u32[]{:S(2)}) collective-permute-start(bf16[256,128]{0,1:T(8,128)(2,1)S(1)} %collective-permute-done.13), channel_id=1, source_target_pairs={{0,224},{8,232},{16,240},{24,248},{32,0},{40,8},{48,16},{56,24},{6... | collective-permute-start | bytes 196616 | tf_op jit(solution)/shard_map/ppermute | solution.py:41
  80.7 1.4 broadcast.206.clone
  82.1 0.7 constant_dynamic-update-slice_fusion.19
  82.9 0.6 collective-permute-done.14
  83.6 5.4 %collective-permute-done.16 = bf16[256,128]{0,1:T(8,128)(2,1)S(1)} collective-permute-done((bf16[256,128]{0,1:T(8,128)(2,1)S(1)}, bf16[256,128]{0,1:T(8,128)(2,1)S(1)}, u32[]{:S(2)}, u32[]{:S(2)}) %collective-permute-start.16) | collective-permute-done | bytes 65568 | tf_op jit(solution)/shard_map/ppermute | solution.py:38
  89.3 3.2 %collective-permute-start.18 = (bf16[256,1024]{0,1:T(8,128)(2,1)S(1)}, bf16[256,1024]{0,1:T(8,128)(2,1)}, u32[]{:S(2)}, u32[]{:S(2)}) collective-permute-start(bf16[256,1024]{0,1:T(8,128)(2,1)S(1)} %constant_dynamic-update-slice_fusion.4), channel_id=1, source_target_pairs={{0,24},{8,0},{16,8},{24,16},{32,56},{40,32},{48,40},{56,48},{64,88... | collective-permute-start | bytes 1572872 | tf_op jit(solution)/shard_map/ppermute | solution.py:41
  92.8 3.2 %collective-permute-start.6 = (bf16[256,512]{0,1:T(8,128)(2,1)}, bf16[256,512]{0,1:T(8,128)(2,1)}, u32[]{:S(2)}, u32[]{:S(2)}) collective-permute-start(bf16[256,512]{0,1:T(8,128)(2,1)} %collective-permute-done.4), channel_id=1, source_target_pairs={{0,224},{8,232},{16,240},{24,248},{32,0},{40,8},{48,16},{56,24},{6... | collective-permute-start | bytes 786440 | tf_op jit(solution)/shard_map/ppermute | solution.py:41
  96.0 1.7 constant_dynamic-update-slice_fusion.18
  97.7 1.1 convert_reduce_fusion
  99.4 1.1 fusion.57
  100.5 2.1 convolution_convert_fusion.3
  102.6 0.8 fusion.68
  103.7 1.5 fusion.72
  105.2 1.7 convolution_convert_fusion.9
  106.9 1.2 convolution_convert_fusion.4
  108.1 5.3 %all-to-all-start.1 = ((bf16[32,16,512]{2,1,0:T(8,128)(2,1)}), bf16[32,16,512]{2,1,0:T(8,128)(2,1)}, u32[]{:S(2)}, u32[]{:S(2)}) async-start(bf16[32,16,512]{2,1,0:T(8,128)(2,1)} %bitcast.104), calls=%async_computation.1 | async-start | bytes 1048576 | tf_op jit(solution)/shard_map/all_to_all | solution.py:119
  113.5 1.7 constant_dynamic-update-slice_fusion.17
  115.1 1.7 collective-permute-start.7
  116.9 1.5 collective-permute-start.8
  118.4 1.7 constant_dynamic-update-slice_fusion.16
  120.0 1.7 constant_dynamic-update-slice_fusion.15
  121.7 1.7 collective-permute-start.19
  123.4 1.1 constant_dynamic-update-slice_fusion.2
  124.5 4.4 %collective-permute-done.7 = bf16[256,512]{0,1:T(8,128)(2,1)S(1)} collective-permute-done((bf16[256,512]{0,1:T(8,128)(2,1)}, bf16[256,512]{0,1:T(8,128)(2,1)S(1)}, u32[]{:S(2)}, u32[]{:S(2)}) %collective-permute-start.7) | collective-permute-done | bytes 262176 | tf_op jit(solution)/shard_map/ppermute | solution.py:38
  128.9 1.1 constant_dynamic-update-slice_fusion.1
  130.0 0.7 constant_dynamic-update-slice_fusion.14
  130.8 0.7 constant_dynamic-update-slice_fusion.13
  131.5 5.0 %collective-permute-done.9 = bf16[256,512]{0,1:T(8,128)(2,1)S(1)} collective-permute-done((bf16[256,512]{0,1:T(8,128)(2,1)S(1)}, bf16[256,512]{0,1:T(8,128)(2,1)S(1)}, u32[]{:S(2)}, u32[]{:S(2)}) %collective-permute-start.9) | collective-permute-done | bytes 262176 | tf_op jit(solution)/shard_map/ppermute | solution.py:38
  136.5 0.7 constant_dynamic-update-slice_fusion.12
  137.3 1.3 copy-done.1
  138.6 1.7 copy.49
  140.4 2.5 %fusion.10 = bf16[256,256]{0,1:T(8,128)(2,1)S(1)} fusion(bf16[256,4096]{0,1:T(8,128)(2,1)S(1)} %bitcast.89, bf16[256,4096]{1,0:T(8,128)(2,1)} %all-gather.2.cloned.1.call-done), kind=kOutput, calls=%fused_computation.27 | convolution fusion | flops 536936448 | bytes 4325376 | tf_op jit(solution)/shard_map/td,wd->tw/dot_general | solution.py:136
  142.9 2.3 %fusion.9 = bf16[256,256]{0,1:T(8,128)(2,1)S(1)} fusion(bf16[256,4096]{0,1:T(8,128)(2,1)} %constant_dynamic-update-slice_fusion.12, bf16[256,4096]{1,0:T(8,128)(2,1)S(1)} %copy-done.5), kind=kOutput, calls=%fused_computation.26 | convolution fusion | flops 536936448 | bytes 4325376 | tf_op jit(solution)/shard_map/td,wd->tw/dot_general | solution.py:135
  145.3 1.1 convolution_convert_fusion.5
  146.4 7.2 %all-to-all-start.2 = ((bf16[32,16,512]{2,1,0:T(8,128)(2,1)}), bf16[32,16,512]{2,1,0:T(8,128)(2,1)S(1)}, u32[]{:S(2)}, u32[]{:S(2)}) async-start(bf16[32,16,512]{2,1,0:T(8,128)(2,1)} %bitcast.106), calls=%async_computation.3 | async-start | bytes 1048576 | tf_op jit(solution)/shard_map/all_to_all | solution.py:141
  153.9 1.4 convolution_convert_fusion.8
  155.3 0.7 fusion.50
  156.0 3.7 %fusion.1 = bf16[256,4096]{1,0:T(8,128)(2,1)} fusion(f32[256,4096]{1,0:T(8,128)S(1)} %fusion.50, bf16[256,4096]{0,1:T(8,128)(2,1)} %constant_dynamic-update-slice_fusion.12, bf16[256,512]{1,0:T(8,128)(2,1)S(1)} %convolution_convert_fusion.8), kind=kOutput, calls=%fused_computation.2 | convolution fusion | flops 538968064 | bytes 8519680 | tf_op jit(solution)/shard_map/dot_general | solution.py:124
  159.8 8.8 %all-to-all-done.2 = bf16[32,16,512]{2,1,0:T(8,128)(2,1)S(1)} async-done(((bf16[32,16,512]{2,1,0:T(8,128)(2,1)}), bf16[32,16,512]{2,1,0:T(8,128)(2,1)S(1)}, u32[]{:S(2)}, u32[]{:S(2)}) %all-to-all-start.2) | async-done | bytes 524320 | tf_op jit(solution)/shard_map/all_to_all | solution.py:141
  168.6 0.3 convolution_convert_fusion.7
  169.7 0.8 convolution_convert_fusion.6
  170.5 0.3 fusion.8
  170.8 0.6 convolution_convert_fusion
  171.4 40.3 %all_to_all.48 = bf16[32,16,1536]{2,1,0:T(8,128)(2,1)S(1)} all-to-all(bf16[32,16,1536]{2,1,0:T(8,128)(2,1)S(1)} %bitcast.93), channel_id=1, replica_groups=mesh['seq'=32,'head'=8] {'seq'}, dimensions={0} | all-to-all | bytes 3145728 | tf_op jit(solution)/shard_map/all_to_all | solution.py:164
  211.8 0.6 convolution_convert_fusion.2
  212.4 0.9 fusion.69
  (83 shorter events, 3.6 us)
Async XLA Ops:
  7.2 25.0 %copy-start = (s32[32,2,2]{0,2,1:T(2,128)S(1)}, s32[32,2,2]{0,2,1:T(2,128)}, u32[]{:S(2)}) copy-start(s32[32,2,2]{0,2,1:T(2,128)} %param.13) | copy-start | bytes 1540
  13.1 11.8 %copy-start.3 = (bf16[512,128]{1,0:T(8,128)(2,1)S(1)}, bf16[512,128]{1,0:T(8,128)(2,1)}, u32[]{:S(2)}) copy-start(bf16[512,128]{1,0:T(8,128)(2,1)} %param.10) | copy-start | bytes 393220
  13.1 84.6 %all-to-all-start = ((bf16[32,16,1664]{2,1,0:T(8,128)(2,1)}), bf16[32,16,1664]{2,1,0:T(8,128)(2,1)}, u32[]{:S(2)}, u32[]{:S(2)}) async-start(bf16[32,16,1664]{2,1,0:T(8,128)(2,1)} %bitcast.2), calls=%async_computation | async-start | bytes 3407872 | tf_op jit(solution)/shard_map/all_to_all | solution.py:81
  24.9 115.5 %all-gather.2.cloned.1.call-start = ((), (), s32[]{:S(2)}) async-start(), calls=%async_computation.6 | async-start | bytes 2359296 | tf_op jit(solution)/shard_map/all_gather | solution.py:132
  25.1 40.3 %collective-permute-start.10 = (bf16[256,128]{0,1:T(8,128)(2,1)S(1)}, bf16[256,128]{0,1:T(8,128)(2,1)S(1)}, u32[]{:S(2)}, u32[]{:S(2)}) collective-permute-start(bf16[256,128]{0,1:T(8,128)(2,1)S(1)} %copy.66), channel_id=1, source_target_pairs={{0,32},{8,40},{16,48},{24,56},{32,64},{40,72},{48,80},{56,88},{64,... | collective-permute-start | bytes 196616 | tf_op jit(solution)/shard_map/ppermute | solution.py:38
  26.9 38.5 %collective-permute-start.11 = (bf16[256,128]{0,1:T(8,128)(2,1)S(1)}, bf16[256,128]{0,1:T(8,128)(2,1)S(1)}, u32[]{:S(2)}, u32[]{:S(2)}) collective-permute-start(bf16[256,128]{0,1:T(8,128)(2,1)S(1)} %copy.66), channel_id=1, source_target_pairs={{0,224},{8,232},{16,240},{24,248},{32,0},{40,8},{48,16},{56,24},{6... | collective-permute-start | bytes 196616 | tf_op jit(solution)/shard_map/ppermute | solution.py:41
  28.5 40.2 %collective-permute-start = (bf16[256,128]{0,1:T(8,128)(2,1)S(1)}, bf16[256,128]{0,1:T(8,128)(2,1)S(1)}, u32[]{:S(2)}, u32[]{:S(2)}) collective-permute-start(bf16[256,128]{0,1:T(8,128)(2,1)S(1)} %copy.65), channel_id=1, source_target_pairs={{0,8},{8,16},{16,24},{24,0},{32,40},{40,48},{48,56},{56,32},{64,72... | collective-permute-start | bytes 196616 | tf_op jit(solution)/shard_map/ppermute | solution.py:38
  30.3 39.2 %collective-permute-start.1 = (bf16[256,128]{0,1:T(8,128)(2,1)S(1)}, bf16[256,128]{0,1:T(8,128)(2,1)S(1)}, u32[]{:S(2)}, u32[]{:S(2)}) collective-permute-start(bf16[256,128]{0,1:T(8,128)(2,1)S(1)} %copy.65), channel_id=1, source_target_pairs={{0,24},{8,0},{16,8},{24,16},{32,56},{40,32},{48,40},{56,48},{64,88... | collective-permute-start | bytes 196616 | tf_op jit(solution)/shard_map/ppermute | solution.py:41
  65.4 12.1 %collective-permute-start.12 = (bf16[256,128]{0,1:T(8,128)(2,1)S(1)}, bf16[256,128]{0,1:T(8,128)(2,1)S(1)}, u32[]{:S(2)}, u32[]{:S(2)}) collective-permute-start(bf16[256,128]{0,1:T(8,128)(2,1)S(1)} %collective-permute-done.10), channel_id=1, source_target_pairs={{0,32},{8,40},{16,48},{24,56},{32,64},{40,72},{48,80},{56,88},{64,... | collective-permute-start | bytes 196616 | tf_op jit(solution)/shard_map/ppermute | solution.py:38
  65.4 12.1 %collective-permute-start.13 = (bf16[256,128]{0,1:T(8,128)(2,1)S(1)}, bf16[256,128]{0,1:T(8,128)(2,1)S(1)}, u32[]{:S(2)}, u32[]{:S(2)}) collective-permute-start(bf16[256,128]{0,1:T(8,128)(2,1)S(1)} %collective-permute-done.11), channel_id=1, source_target_pairs={{0,224},{8,232},{16,240},{24,248},{32,0},{40,8},{48,16},{56,24},{6... | collective-permute-start | bytes 196616 | tf_op jit(solution)/shard_map/ppermute | solution.py:41
  68.7 5.5 %collective-permute-start.2 = (bf16[256,128]{0,1:T(8,128)(2,1)S(1)}, bf16[256,128]{0,1:T(8,128)(2,1)S(1)}, u32[]{:S(2)}, u32[]{:S(2)}) collective-permute-start(bf16[256,128]{0,1:T(8,128)(2,1)S(1)} %collective-permute-done), channel_id=1, source_target_pairs={{0,8},{8,16},{16,24},{24,0},{32,40},{40,48},{48,56},{56,32},{64,72... | collective-permute-start | bytes 196616 | tf_op jit(solution)/shard_map/ppermute | solution.py:38
  74.1 18.6 %collective-permute-start.3 = (bf16[256,512]{0,1:T(8,128)(2,1)S(1)}, bf16[256,512]{0,1:T(8,128)(2,1)}, u32[]{:S(2)}, u32[]{:S(2)}) collective-permute-start(bf16[256,512]{0,1:T(8,128)(2,1)S(1)} %constant_dynamic-update-slice_fusion.20), channel_id=1, source_target_pairs={{0,32},{8,40},{16,48},{24,56},{32,64},{40,72},{48,80},{56,88},{64,... | collective-permute-start | bytes 786440 | tf_op jit(solution)/shard_map/ppermute | solution.py:38
  74.2 18.6 %collective-permute-start.4 = (bf16[256,512]{0,1:T(8,128)(2,1)S(1)}, bf16[256,512]{0,1:T(8,128)(2,1)}, u32[]{:S(2)}, u32[]{:S(2)}) collective-permute-start(bf16[256,512]{0,1:T(8,128)(2,1)S(1)} %constant_dynamic-update-slice_fusion.20), channel_id=1, source_target_pairs={{0,224},{8,232},{16,240},{24,248},{32,0},{40,8},{48,16},{56,24},{6... | collective-permute-start | bytes 786440 | tf_op jit(solution)/shard_map/ppermute | solution.py:41
  77.5 6.1 %collective-permute-start.14 = (bf16[256,128]{0,1:T(8,128)(2,1)S(1)}, bf16[256,128]{0,1:T(8,128)(2,1)S(1)}, u32[]{:S(2)}, u32[]{:S(2)}) collective-permute-start(bf16[256,128]{0,1:T(8,128)(2,1)S(1)} %collective-permute-done.12), channel_id=1, source_target_pairs={{0,32},{8,40},{16,48},{24,56},{32,64},{40,72},{48,80},{56,88},{64,... | collective-permute-start | bytes 196616 | tf_op jit(solution)/shard_map/ppermute | solution.py:38
  77.5 6.1 %collective-permute-start.15 = (bf16[256,128]{0,1:T(8,128)(2,1)S(1)}, bf16[256,128]{0,1:T(8,128)(2,1)S(1)}, u32[]{:S(2)}, u32[]{:S(2)}) collective-permute-start(bf16[256,128]{0,1:T(8,128)(2,1)S(1)} %collective-permute-done.13), channel_id=1, source_target_pairs={{0,224},{8,232},{16,240},{24,248},{32,0},{40,8},{48,16},{56,24},{6... | collective-permute-start | bytes 196616 | tf_op jit(solution)/shard_map/ppermute | solution.py:41
  83.5 5.5 %collective-permute-start.16 = (bf16[256,128]{0,1:T(8,128)(2,1)S(1)}, bf16[256,128]{0,1:T(8,128)(2,1)S(1)}, u32[]{:S(2)}, u32[]{:S(2)}) collective-permute-start(bf16[256,128]{0,1:T(8,128)(2,1)S(1)} %collective-permute-done.14), channel_id=1, source_target_pairs={{0,32},{8,40},{16,48},{24,56},{32,64},{40,72},{48,80},{56,88},{64,... | collective-permute-start | bytes 196616 | tf_op jit(solution)/shard_map/ppermute | solution.py:38
  89.0 32.7 %collective-permute-start.17 = (bf16[256,1024]{0,1:T(8,128)(2,1)S(1)}, bf16[256,1024]{0,1:T(8,128)(2,1)}, u32[]{:S(2)}, u32[]{:S(2)}) collective-permute-start(bf16[256,1024]{0,1:T(8,128)(2,1)S(1)} %constant_dynamic-update-slice_fusion.4), channel_id=1, source_target_pairs={{0,8},{8,16},{16,24},{24,0},{32,40},{40,48},{48,56},{56,32},{64,72... | collective-permute-start | bytes 1572872 | tf_op jit(solution)/shard_map/ppermute | solution.py:38
  89.3 39.6 %collective-permute-start.18 = (bf16[256,1024]{0,1:T(8,128)(2,1)S(1)}, bf16[256,1024]{0,1:T(8,128)(2,1)}, u32[]{:S(2)}, u32[]{:S(2)}) collective-permute-start(bf16[256,1024]{0,1:T(8,128)(2,1)S(1)} %constant_dynamic-update-slice_fusion.4), channel_id=1, source_target_pairs={{0,24},{8,0},{16,8},{24,16},{32,56},{40,32},{48,40},{56,48},{64,88... | collective-permute-start | bytes 1572872 | tf_op jit(solution)/shard_map/ppermute | solution.py:41
  92.7 22.4 %collective-permute-start.5 = (bf16[256,512]{0,1:T(8,128)(2,1)}, bf16[256,512]{0,1:T(8,128)(2,1)}, u32[]{:S(2)}, u32[]{:S(2)}) collective-permute-start(bf16[256,512]{0,1:T(8,128)(2,1)} %collective-permute-done.3), channel_id=1, source_target_pairs={{0,32},{8,40},{16,48},{24,56},{32,64},{40,72},{48,80},{56,88},{64,... | collective-permute-start | bytes 786440 | tf_op jit(solution)/shard_map/ppermute | solution.py:38
  92.8 24.0 %collective-permute-start.6 = (bf16[256,512]{0,1:T(8,128)(2,1)}, bf16[256,512]{0,1:T(8,128)(2,1)}, u32[]{:S(2)}, u32[]{:S(2)}) collective-permute-start(bf16[256,512]{0,1:T(8,128)(2,1)} %collective-permute-done.4), channel_id=1, source_target_pairs={{0,224},{8,232},{16,240},{24,248},{32,0},{40,8},{48,16},{56,24},{6... | collective-permute-start | bytes 786440 | tf_op jit(solution)/shard_map/ppermute | solution.py:41
  100.5 3.2 %copy-start.4 = (pred[256,256]{0,1:T(8,128)(4,1)S(1)}, pred[256,256]{0,1:T(8,128)(4,1)}, u32[]{:S(2)}) copy-start(pred[256,256]{0,1:T(8,128)(4,1)} %fusion.43) | copy-start | bytes 196612
  108.1 32.2 %all-to-all-start.1 = ((bf16[32,16,512]{2,1,0:T(8,128)(2,1)}), bf16[32,16,512]{2,1,0:T(8,128)(2,1)}, u32[]{:S(2)}, u32[]{:S(2)}) async-start(bf16[32,16,512]{2,1,0:T(8,128)(2,1)} %bitcast.104), calls=%async_computation.1 | async-start | bytes 1048576 | tf_op jit(solution)/shard_map/all_to_all | solution.py:119
  115.1 13.8 %collective-permute-start.7 = (bf16[256,512]{0,1:T(8,128)(2,1)}, bf16[256,512]{0,1:T(8,128)(2,1)S(1)}, u32[]{:S(2)}, u32[]{:S(2)}) collective-permute-start(bf16[256,512]{0,1:T(8,128)(2,1)} %collective-permute-done.5), channel_id=1, source_target_pairs={{0,32},{8,40},{16,48},{24,56},{32,64},{40,72},{48,80},{56,88},{64,... | collective-permute-start | bytes 786440 | tf_op jit(solution)/shard_map/ppermute | solution.py:38
  116.9 13.9 %collective-permute-start.8 = (bf16[256,512]{0,1:T(8,128)(2,1)}, bf16[256,512]{0,1:T(8,128)(2,1)S(1)}, u32[]{:S(2)}, u32[]{:S(2)}) collective-permute-start(bf16[256,512]{0,1:T(8,128)(2,1)} %collective-permute-done.6), channel_id=1, source_target_pairs={{0,224},{8,232},{16,240},{24,248},{32,0},{40,8},{48,16},{56,24},{6... | collective-permute-start | bytes 786440 | tf_op jit(solution)/shard_map/ppermute | solution.py:41
  121.7 15.5 %collective-permute-start.19 = (bf16[256,1024]{0,1:T(8,128)(2,1)}, bf16[256,1024]{0,1:T(8,128)(2,1)S(1)}, u32[]{:S(2)}, u32[]{:S(2)}) collective-permute-start(bf16[256,1024]{0,1:T(8,128)(2,1)} %collective-permute-done.17), channel_id=1, source_target_pairs={{0,8},{8,16},{16,24},{24,0},{32,40},{40,48},{48,56},{56,32},{64,72... | collective-permute-start | bytes 1572872 | tf_op jit(solution)/shard_map/ppermute | solution.py:38
  128.9 7.6 %collective-permute-start.9 = (bf16[256,512]{0,1:T(8,128)(2,1)S(1)}, bf16[256,512]{0,1:T(8,128)(2,1)S(1)}, u32[]{:S(2)}, u32[]{:S(2)}) collective-permute-start(bf16[256,512]{0,1:T(8,128)(2,1)S(1)} %collective-permute-done.7), channel_id=1, source_target_pairs={{0,32},{8,40},{16,48},{24,56},{32,64},{40,72},{48,80},{56,88},{64,... | collective-permute-start | bytes 786440 | tf_op jit(solution)/shard_map/ppermute | solution.py:38
  137.3 1.3 copy-start.1
  140.4 2.5 %copy-start.5 = (bf16[256,4096]{1,0:T(8,128)(2,1)S(1)}, bf16[256,4096]{1,0:T(8,128)(2,1)}, u32[]{:S(2)}) copy-start(bf16[256,4096]{1,0:T(8,128)(2,1)} %all-gather.2.cloned.1.call-done) | copy-start | bytes 6291460
  146.4 22.2 %all-to-all-start.2 = ((bf16[32,16,512]{2,1,0:T(8,128)(2,1)}), bf16[32,16,512]{2,1,0:T(8,128)(2,1)S(1)}, u32[]{:S(2)}, u32[]{:S(2)}) async-start(bf16[32,16,512]{2,1,0:T(8,128)(2,1)} %bitcast.106), calls=%async_computation.3 | async-start | bytes 1048576 | tf_op jit(solution)/shard_map/all_to_all | solution.py:141
  153.6 59.7 %reduce-scatter.2.cloned.1.call-start = ((), (), s32[]{:S(2)}) async-start(), calls=%async_computation.5 | async-start | bytes 2359296 | tf_op jit(solution)/shard_map/reduce_scatter | solution.py:128
  159.7 9.4 %copy-start.2 = (bf16[32,4,8,128]{3,2,1,0:T(8,128)(2,1)S(1)}, bf16[32,4,8,128]{3,2,1,0:T(8,128)(2,1)}, u32[]{:S(2)}) copy-start(bf16[32,4,8,128]{3,2,1,0:T(8,128)(2,1)} %get-tuple-element.12) | copy-start | bytes 786436
  159.7 9.4 %copy-start.6 = (f32[4,256,256]{1,2,0:T(8,128)S(1)}, f32[4,256,256]{1,2,0:T(8,128)}, u32[]{:S(2)}) copy-start(f32[4,256,256]{1,2,0:T(8,128)} %get-tuple-element.23) | copy-start | bytes 3145732
Sparse Core Ops, SparseCore 0:
  32.0 26.8 all-gather.1
  159.9 32.7 reduce-scatter.1
